TPU v7x, 512 devices: a whole 4x4x16 slice. The times are simulated.
512 devices in a mesh: dp: 16 (over z), row: 4 (over y), col: 8 (over x, core).
Axes of the slice: x: 4, y: 4, z: 16, core: 2. Of those that a mesh axis runs over, the one named last changes fastest.
Arguments:
- layer_input: bfloat16 [3072, 4096], P(('dp', 'col'), 'row'), may hold values from -6 to 6
- hidden_grad: bfloat16 [3072, 14336], P(('dp', 'row'), 'col'), may hold values from -6 to 6
- gate_slots: bfloat16 [4, 8, 48, 128, 128], P('row', 'col', 'dp'), may hold values from -0.125 to 0.125
- up_slots: bfloat16 [4, 8, 48, 128, 128], P('row', 'col', 'dp'), may hold values from -0.125 to 0.125
- block_mask: int32 [32, 112], replicated, may hold values from 0 to 1, as said below
Outputs:
- input_grad: bfloat16 [3072, 4096], P(('dp', 'col'), 'row')
- gate_slot_grad: float32 [4, 8, 48, 128, 128], P('row', 'col', 'dp')
- up_slot_grad: float32 [4, 8, 48, 128, 128], P('row', 'col', 'dp')
Inputs may be any that keep to these rules, and one draw needn't show every extreme that they name: `block_mask`: every tile of 8 x 14 blocks keeps between 24 and 48 blocks; some tile keeps exactly 48, which tile depends on the draw.
All inputs are finite; a program needn't handle non-finite values.
Results may differ from a plain program's by a relative error of at most 0.022.
Values may be sent and summed in bfloat16 or wider, within the bound.
No kernel may reach another device: no remote copies, remote signals or barrier semaphores. Data moves between devices by JAX's collectives and lax.ppermute only.
A program may use at most 64 MiB of HBM per device.

v0:
```python
import jax
import jax.numpy as jnp
from jax import lax
from jax.sharding import PartitionSpec as P


def slot_maps(block_mask, tile_rows, tile_cols, capacity):
    row_first = lax.axis_index("row") * tile_rows
    col_first = lax.axis_index("col") * tile_cols
    tile_mask = lax.dynamic_slice(block_mask, (row_first, col_first), (tile_rows, tile_cols))
    flat_mask = tile_mask.reshape(tile_rows * tile_cols)
    position = jnp.cumsum(flat_mask) - 1
    slot_ids = jnp.arange(capacity, dtype=jnp.int32)
    chosen = ((flat_mask[:, None] > 0) & (position[:, None] == slot_ids[None, :])).astype(jnp.int32)
    block_ids = jnp.arange(tile_rows * tile_cols, dtype=jnp.int32)
    slot_block = jnp.sum(chosen * block_ids[:, None], axis=0)
    live_slots = jnp.sum(chosen, axis=0).astype(jnp.float32)
    slot_row = slot_block // tile_cols
    slot_col = slot_block % tile_cols
    col_table = (slot_col[:, None] == jnp.arange(tile_cols, dtype=jnp.int32)[None, :]).astype(
        jnp.float32
    ) * live_slots[:, None]
    row_table = (slot_row[:, None] == jnp.arange(tile_rows, dtype=jnp.int32)[None, :]).astype(
        jnp.float32
    ) * live_slots[:, None]
    return (slot_row, slot_col, live_slots, col_table, row_table)


def slot_products(picked, pair_weights, col_table):
    per_slot = jnp.einsum("tsk,skn->tsn", picked, pair_weights, preferred_element_type=jnp.float32)
    return jnp.einsum("tsn,sc->tcn", per_slot, col_table, precision=lax.Precision.HIGHEST)


def back_products(grad_picked, pair_weights, row_table):
    per_slot = jnp.einsum(
        "tsn,skn->tsk", grad_picked, pair_weights, preferred_element_type=jnp.float32
    )
    return jnp.einsum("tsk,sr->trk", per_slot, row_table, precision=lax.Precision.HIGHEST)


def on_device(layer_input, hidden_grad, gate_slots, up_slots, block_mask):
    gate_local = gate_slots[0, 0]
    up_local = up_slots[0, 0]
    block_size = gate_local.shape[-1]
    replicas = lax.axis_size("dp")
    capacity = gate_local.shape[0] * replicas
    token_panel = lax.all_gather(layer_input, "col", axis=0, tiled=True)
    grad_panel = lax.all_gather(hidden_grad, "row", axis=0, tiled=True)
    tok_rows = token_panel.shape[0]
    feat_cols = token_panel.shape[1]
    unit_cols = grad_panel.shape[1]
    tile_rows = feat_cols // block_size
    tile_cols = unit_cols // block_size
    slot_row, slot_col, live_slots, col_table, row_table = slot_maps(
        block_mask, tile_rows, tile_cols, capacity
    )
    token_blocks = token_panel.reshape(tok_rows, tile_rows, block_size)
    picked_tokens = jnp.take(token_blocks, slot_row, axis=1)
    gate_all, up_all = (
        lax.all_gather(gate_local, "dp", axis=0, tiled=True),
        lax.all_gather(up_local, "dp", axis=0, tiled=True),
    )
    pair_all = jnp.concatenate([gate_all, up_all], axis=2)
    pair_part = slot_products(picked_tokens, pair_all, col_table)
    gate_part = pair_part[:, :, :block_size].reshape(tok_rows, unit_cols)
    up_part = pair_part[:, :, block_size:].reshape(tok_rows, unit_cols)
    gate_sum, up_sum = (
        lax.psum(gate_part.astype(jnp.bfloat16), "row").astype(jnp.float32),
        lax.psum(up_part.astype(jnp.bfloat16), "row").astype(jnp.float32),
    )
    sigmoid_gate = jax.nn.sigmoid(gate_sum)
    upstream = grad_panel.astype(jnp.float32)
    gate_grad = (upstream * up_sum * sigmoid_gate * (1.0 + gate_sum * (1.0 - sigmoid_gate))).astype(
        jnp.bfloat16
    )
    up_grad = (upstream * gate_sum * sigmoid_gate).astype(jnp.bfloat16)
    grad_pair = jnp.concatenate(
        [
            gate_grad.reshape(tok_rows, tile_cols, block_size),
            up_grad.reshape(tok_rows, tile_cols, block_size),
        ],
        axis=2,
    )
    grad_picked = jnp.take(grad_pair, slot_col, axis=1)
    summed = back_products(grad_picked, pair_all, row_table)
    input_sum = lax.psum_scatter(
        summed.reshape(tok_rows // lax.axis_size("col") * lax.axis_size("col"), feat_cols).astype(
            jnp.bfloat16
        ),
        "col",
        scatter_dimension=0,
        tiled=True,
    )
    pair_term = (
        jnp.einsum("tsk,tsn->skn", picked_tokens, grad_picked, preferred_element_type=jnp.float32)
        * live_slots[:, None, None]
    )
    pair_total = lax.psum_scatter(
        pair_term.astype(jnp.bfloat16), "dp", scatter_dimension=0, tiled=True
    ).astype(jnp.float32)
    gate_out = (pair_total[:, :, :block_size] / replicas)[None, None]
    up_out = (pair_total[:, :, block_size:] / replicas)[None, None]
    return (input_sum, gate_out, up_out)


def solution(mesh):
    return jax.shard_map(
        on_device,
        mesh=mesh,
        in_specs=(
            P(("dp", "col"), "row"),
            P(("dp", "row"), "col"),
            P("row", "col", "dp", None, None),
            P("row", "col", "dp", None, None),
            P(),
        ),
        out_specs=(
            P(("dp", "col"), "row"),
            P("row", "col", "dp", None, None),
            P("row", "col", "dp", None, None),
        ),
        check_vma=False,
    )
```

profile of v0, /device:TPU:8, one launch (start us, length us, event | category | flops | bytes accessed | tf_op | source)
XLA Modules:
  0.0 370.0 jit_solution(6575437389521833175)
XLA Ops:
  7.2 0.7 all-gather.5.cloned.1.call-update
  7.9 0.7 all-gather.7.cloned.1.call-update
  8.7 0.8 broadcast_compare_fusion
  10.1 13.5 %all_gather.15 = bf16[192,1024]{1,0:T(8,128)(2,1)S(1)} all-gather(bf16[24,1024]{1,0:T(8,128)(2,1)} %param.5), channel_id=1, replica_groups=mesh['dp'=16,'row'=4,'col'=8] {'col'}, dimensions={0}, use_global_device_ids=true | all-gather | bytes 442368 | tf_op jit(solution)/shard_map/all_gather | solution.py:47
  23.7 1.0 gather_fusion
  24.7 61.7 %all-gather.5.cloned.1.call-done = bf16[1,1,48,128,128]{4,3,1,0,2:T(8,128)(2,1)} async-done(((bf16[1,1,3,128,128]{4,3,1,0,2:T(8,128)(2,1)}), bf16[1,1,48,128,128]{4,3,1,0,2:T(8,128)(2,1)}) %all-gather.5.cloned.1.call-update) | async-done | bytes 1572880 | tf_op jit(solution)/shard_map/all_gather | solution.py:60
  86.4 71.1 %all-gather.7.cloned.1.call-done = bf16[1,1,48,128,128]{4,3,1,0,2:T(8,128)(2,1)} async-done(((bf16[1,1,3,128,128]{4,3,1,0,2:T(8,128)(2,1)}), bf16[1,1,48,128,128]{4,3,1,0,2:T(8,128)(2,1)}) %all-gather.7.cloned.1.call-update) | async-done | bytes 1572880 | tf_op jit(solution)/shard_map/all_gather | solution.py:61
  157.5 3.3 convolution_bitcast_fusion
  160.8 9.9 %fusion.20 = bf16[192,14,256]{2,1,0:T(8,128)(2,1)S(1)} fusion(f32[192,48,256]{2,0,1:T(8,128)S(1)} %convolution_bitcast_fusion, f32[48]{0:T(128)S(1)} %convert_element_type.55, s32[48]{0:T(128)S(1)} %get-tuple-element.8), kind=kOutput, calls=%fused_computation.23 | convolution fusion | flops 397051200 | bytes 10813824 | tf_op jit(solution)/shard_map/tsn,sc->tcn/dot_general | solution.py:31
  171.0 1.0 copy.56
  172.1 1.1 copy.57
  173.2 13.2 %all_gather.14 = bf16[192,1792]{1,0:T(8,128)(2,1)S(1)} all-gather(bf16[48,1792]{1,0:T(8,128)(2,1)S(1)} %copy-done.3), channel_id=1, replica_groups=mesh['dp'=16,'row'=4,'col'=8] {'row'}, dimensions={0}, use_global_device_ids=true | all-gather | bytes 860160 | tf_op jit(solution)/shard_map/all_gather | solution.py:48
  186.4 46.7 %all-reduce.3.cloned.1.call-done = (bf16[192,1792]{1,0:T(8,128)(2,1)}, bf16[192,1792]{1,0:T(8,128)(2,1)}) async-done(((bf16[192,1792]{1,0:T(8,128)(2,1)}, bf16[192,1792]{1,0:T(8,128)(2,1)}), (bf16[192,1792]{1,0:T(8,128)(2,1)}, bf16[192,1792]{1,0:T(8,128)(2,1)})) %all-reduce.3.cloned.1.call-update) | async-done | bytes 1376272 | tf_op jit(solution)/shard_map/psum | solution.py:68
  233.1 2.1 fusion.36
  235.7 3.1 gather_fusion.1
  238.8 6.2 %multiply_convert_fusion = bf16[48,128,256]{2,1,0:T(8,128)(2,1)} fusion(f32[48]{0:T(128)S(1)} %convert_element_type.55, bf16[48,192,256]{2,1,0:T(8,128)(2,1)} %gather_fusion.1, pred[48]{0:T(512)(128)(4,1)S(1)} %get-tuple-element.7, bf16[48,192,128]{2,1,0:T(8,128)(2,1)} %copy-done, pred[48]{0:T(512)(128)(4,1)S(1)} %get-tuple-element.22), kind=kOutput, calls=%fused_computation.4 | convolution fusion | flops 610664448 | bytes 10223904 | tf_op jit(solution)/shard_map/tsk,tsn->skn/dot_general | solution.py:95
  245.1 1.3 copy-done.1
  246.9 3.3 fusion.10
  250.3 4.9 %fusion.32 = bf16[8,192,128]{2,0,1:T(8,128)(2,1)S(1)} fusion(f32[192,48,128]{2,0,1:T(8,128)S(1)} %fusion.10, f32[48]{0:T(128)S(1)} %convert_element_type.55, s32[48]{0:T(128)S(1)} %get-tuple-element.23), kind=kOutput, calls=%fused_computation.34 | convolution fusion | flops 113443584 | bytes 5112192 | tf_op jit(solution)/shard_map/tsk,sr->trk/dot_general | solution.py:38
  255.2 0.8 copy.60
  256.0 67.8 %reduce-scatter.5.cloned.1.call-done = bf16[3,128,256]{2,1,0:T(8,128)(2,1)} async-done(((bf16[48,128,256]{2,1,0:T(8,128)(2,1)}), bf16[3,128,256]{2,1,0:T(8,128)(2,1)}) %reduce-scatter.5.cloned.1.call-update) | async-done | bytes 196624 | tf_op jit(solution)/shard_map/reduce_scatter | solution.py:98
  323.8 1.0 convert_element_type.67
  324.8 0.8 fusion.37
  325.5 38.0 %reduce-scatter.3.cloned.1.call-done = bf16[24,1024]{1,0:T(8,128)(2,1)} async-done(((bf16[192,1024]{1,0:T(8,128)(2,1)}), bf16[24,1024]{1,0:T(8,128)(2,1)}) %reduce-scatter.3.cloned.1.call-update) | async-done | bytes 49168 | tf_op jit(solution)/shard_map/reduce_scatter | solution.py:86
  (29 shorter events, 2.2 us)
Async XLA Ops:
  7.2 79.3 %all-gather.5.cloned.1.call-start = ((), (), s32[]{:S(2)}) async-start(), calls=%async_computation.4 | async-start | bytes 1671168 | tf_op jit(solution)/shard_map/all_gather | solution.py:60
  7.9 149.6 %all-gather.7.cloned.1.call-start = ((), (), s32[]{:S(2)}) async-start(), calls=%async_computation.5 | async-start | bytes 1671168 | tf_op jit(solution)/shard_map/all_gather | solution.py:61
  8.6 224.4 %all-reduce.3.cloned.1.call-start = ((), (), s32[]{:S(2)}) async-start(), calls=%async_computation.6 | async-start | bytes 2752512 | tf_op jit(solution)/shard_map/psum | solution.py:68
  24.7 136.1 %copy-start = (bf16[48,192,128]{2,1,0:T(8,128)(2,1)}, bf16[48,192,128]{2,1,0:T(8,128)(2,1)S(1)}, u32[]{:S(2)}) copy-start(bf16[48,192,128]{2,1,0:T(8,128)(2,1)S(1)} %gather_fusion) | copy-start | bytes 7077892
  171.0 2.2 copy-start.3
  173.2 150.6 %reduce-scatter.5.cloned.1.call-start = ((), (), s32[]{:S(2)}) async-start(), calls=%async_computation.3 | async-start | bytes 3342336 | tf_op jit(solution)/shard_map/reduce_scatter | solution.py:98
  245.1 1.4 copy-start.1
  245.1 1.9 copy-start.2
  245.1 118.4 %reduce-scatter.3.cloned.1.call-start = ((), (), s32[]{:S(2)}) async-start(), calls=%async_computation.2 | async-start | bytes 442368 | tf_op jit(solution)/shard_map/reduce_scatter | solution.py:86
Sparse Core Ops, SparseCore 0:
  10.0 76.3 all-gather.4
  88.5 68.9 all-gather.6
  173.3 59.7 all-reduce.2
  245.2 78.5 reduce-scatter.4
  327.0 36.4 reduce-scatter.2
where the time goes:
time: 370 us
  waiting for transfers between devices  287 us (78%)
  matrix products  27.7 us (7%)
  blocking collectives  26.7 us (7%)
  between operations  13.9 us (4%)
  local copies, waits for them, and re-layouts  9.72 us (3%)
  other arithmetic  5.19 us (1%)
    all_gather x1, waiting for transfers between devices, on_device(): lax.all_gather(up_local, 'dp', axis=0, tiled=True)  71.1 us
    reduce_scatter x1, waiting for transfers between devices, on_device(): lax.psum_scatter(pair_term.astype(jnp.bfloat16), 'dp', scatter_dimension=...  67.8 us
    all_gather x1, waiting for transfers between devices, on_device(): lax.all_gather(gate_local, 'dp', axis=0, tiled=True)  61.7 us
    psum x1, waiting for transfers between devices, on_device(): lax.psum(gate_part.astype(jnp.bfloat16), 'row').astype(jnp.float32)  46.7 us
    reduce_scatter x1, waiting for transfers between devices, on_device(): lax.psum_scatter(summed.reshape(tok_rows // lax.axis_size('col') * lax.ax...  38 us
    all_gather x1, blocking collectives, on_device(): token_panel = lax.all_gather(layer_input, 'col', axis=0, tiled=True)  13.5 us
    all_gather x1, blocking collectives, on_device(): grad_panel = lax.all_gather(hidden_grad, 'row', axis=0, tiled=True)  13.2 us
    dot_general x1, matrix products, slot_products(): jnp.einsum('tsn,sc->tcn', per_slot, col_table, precision=lax.Precision.HI...  9.9 us
  transfers between devices with their start and end apart: 5, of which 5 were waited for; matrix products, arithmetic and copies ran while one was open for 4% of the time, Pallas kernels for 0%

commit v1 on v0

v1 whole, which is shorter than its diff:
```python
import jax
import jax.numpy as jnp
from jax import lax
from jax.sharding import PartitionSpec as P

F32 = jnp.float32
BF16 = jnp.bfloat16


def _shift(x, axis, n, step):
    return lax.ppermute(x, axis, perm=[(i, (i + step) % n) for i in range(n)])


def ring_gather(x, axis, n):
    ahead = n // 2
    behind = n - 1 - ahead
    out = [None] * n
    out[0] = x
    fwd = x
    bwd = x
    for s in range(1, ahead + 1):
        fwd = _shift(fwd, axis, n, 1)
        out[(n - s) % n] = fwd
        if s <= behind:
            bwd = _shift(bwd, axis, n, -1)
            out[s] = bwd
    return out


def ring_sum_scatter(parts, axis, n):
    ahead = n // 2
    behind = n - 1 - ahead
    fwd = parts[ahead]
    bwd = parts[(n - behind) % n] if behind > 0 else None
    for s in range(1, ahead + 1):
        fwd = _shift(fwd, axis, n, 1)
        total = fwd.astype(F32) + parts[ahead - s].astype(F32)
        fwd = total.astype(BF16) if s < ahead else total
        if s <= behind:
            bwd = _shift(bwd, axis, n, -1)
            if s < behind:
                bwd = (bwd.astype(F32) + parts[(s - behind) % n].astype(F32)).astype(BF16)
    if bwd is None:
        return fwd
    return fwd + bwd.astype(F32)


def on_device(layer_input, hidden_grad, gate_slots, up_slots, block_mask):
    n_dp = lax.axis_size("dp")
    n_row = lax.axis_size("row")
    n_col = lax.axis_size("col")
    k_dp = lax.axis_index("dp")
    k_row = lax.axis_index("row")
    k_col = lax.axis_index("col")
    bs = gate_slots.shape[-1]
    per_dev = gate_slots.shape[2]
    cap = per_dev * n_dp
    feat = layer_input.shape[1]
    units = hidden_grad.shape[1]
    tile_rows = feat // bs
    tile_cols = units // bs
    tok = layer_input.shape[0] * n_col
    rows_per = tok // n_row
    cols_per = tok // n_col

    pair_local = jnp.concatenate([gate_slots[0, 0], up_slots[0, 0]], axis=2)
    pair_rel = jnp.concatenate(ring_gather(pair_local, "dp", n_dp), axis=0)

    x_rel = jnp.stack(ring_gather(layer_input, "col", n_col))
    x_abs = jnp.roll(x_rel, k_col, axis=0).reshape(tok, tile_rows, bs)

    tile_mask = lax.dynamic_slice(
        block_mask, (k_row * tile_rows, k_col * tile_cols), (tile_rows, tile_cols)
    ).reshape(tile_rows * tile_cols)
    kept = tile_mask > 0
    position = jnp.cumsum(kept.astype(jnp.int32)) - 1
    q = jnp.arange(cap, dtype=jnp.int32)
    slot_of_q = ((k_dp + q // per_dev) % n_dp) * per_dev + q % per_dev
    onehot = (kept[None, :] & (position[None, :] == slot_of_q[:, None])).astype(BF16)

    dense = jnp.einsum("qb,qkn->bkn", onehot, pair_rel, preferred_element_type=F32).astype(BF16)
    dense4 = dense.reshape(tile_rows, tile_cols, bs, 2 * bs)

    pre = jnp.einsum("trk,rckn->tcn", x_abs, dense4, preferred_element_type=F32).astype(BF16)
    pre_roll = jnp.roll(pre.reshape(n_row, rows_per, tile_cols, 2 * bs), -k_row, axis=0)
    pre_sum = ring_sum_scatter([pre_roll[m] for m in range(n_row)], "row", n_row)
    gate = pre_sum[..., :bs]
    up = pre_sum[..., bs:]
    upstream = hidden_grad.astype(F32).reshape(rows_per, tile_cols, bs)
    sig = jax.nn.sigmoid(gate)
    gate_grad = (upstream * up * sig * (1.0 + gate * (1.0 - sig))).astype(BF16)
    up_grad = (upstream * gate * sig).astype(BF16)
    grad_local = jnp.concatenate([gate_grad, up_grad], axis=2)
    grad_rel = jnp.stack(ring_gather(grad_local, "row", n_row))
    grad_abs = jnp.roll(grad_rel, k_row, axis=0).reshape(tok, tile_cols, 2 * bs)

    dx = jnp.einsum("tcn,rckn->trk", grad_abs, dense4, preferred_element_type=F32).astype(BF16)
    dx_roll = jnp.roll(dx.reshape(n_col, cols_per, feat), -k_col, axis=0)
    input_grad = ring_sum_scatter([dx_roll[m] for m in range(n_col)], "col", n_col).astype(BF16)

    dw = jnp.einsum("trk,tcn->rckn", x_abs, grad_abs, preferred_element_type=F32).astype(BF16)
    slot_dw = jnp.einsum(
        "qb,bkn->qkn",
        onehot,
        dw.reshape(tile_rows * tile_cols, bs, 2 * bs),
        preferred_element_type=F32,
    ).astype(BF16)
    dw_sum = ring_sum_scatter(
        [slot_dw[m * per_dev:(m + 1) * per_dev] for m in range(n_dp)], "dp", n_dp
    ) / n_dp
    gate_out = dw_sum[..., :bs][None, None]
    up_out = dw_sum[..., bs:][None, None]
    return (input_grad, gate_out, up_out)


def solution(mesh):
    return jax.shard_map(
        on_device,
        mesh=mesh,
        in_specs=(
            P(("dp", "col"), "row"),
            P(("dp", "row"), "col"),
            P("row", "col", "dp", None, None),
            P("row", "col", "dp", None, None),
            P(),
        ),
        out_specs=(
            P(("dp", "col"), "row"),
            P("row", "col", "dp", None, None),
            P("row", "col", "dp", None, None),
        ),
        check_vma=False,
    )
```

time: 370 us -> 330 us (0.89)
  the two profiles are of different devices: /device:TPU:8 before, /device:TPU:2 now
where the time goes in v1:
time: 330 us; the launch traced here: 325 us
  starting transfers between devices  140 us (42%)
  waiting for transfers between devices  79.7 us (24%)
  local copies, waits for them, and re-layouts  65.5 us (20%)
  matrix products  26 us (8%)
  other arithmetic  12.3 us (4%)
    ppermute x50, starting transfers between devices, _shift(): return lax.ppermute(x, axis, perm=[(i, (i + step) % n) for i in range(n)])  140 us
    ppermute x50, waiting for transfers between devices, _shift(): return lax.ppermute(x, axis, perm=[(i, (i + step) % n) for i in range(n)])  79.7 us
    concatenate x1, local copies, waits for them, and re-layouts, on_device(): pair_rel = jnp.concatenate(ring_gather(pair_local, 'dp', n_dp), axis=0)  39.9 us
    convert_element_type x1, local copies, waits for them, and re-layouts, on_device(): jnp.einsum('trk,tcn->rckn', x_abs, grad_abs, preferred_element_type=F32)  9.92 us
    dot_general x1, matrix products, on_device(): jnp.einsum('qb,bkn->qkn', onehot, dw.reshape(tile_rows * tile_cols, bs, 2...  8.01 us
  transfers between devices with their start and end apart: 50, of which 28 were waited for; matrix products, arithmetic and copies ran while one was open for 5% of the time, Pallas kernels for 0%

profile of v1, /device:TPU:2, one launch (start us, length us, event | category | flops | bytes accessed | tf_op | source)
XLA Modules:
  0.0 324.9 jit_solution(7470256005762392757)
XLA Ops:
  1.9 11.4 %collective-permute-start.7 = (bf16[3,128,256]{2,0,1:T(4,128)(2,1)S(1)}, bf16[3,128,256]{2,0,1:T(4,128)(2,1)S(1)}, u32[]{:S(2)}, u32[]{:S(2)}) collective-permute-start(bf16[3,128,256]{2,0,1:T(4,128)(2,1)S(1)} %pad_maximum_fusion.1), channel_id=1, source_target_pairs={{0,480},{32,0},{64,32},{96,64},{128,96},{160,128},{192,160},{224,1... | collective-permute-start | bytes 589832 | tf_op jit(solution)/shard_map/ppermute | solution.py:11
  19.1 5.0 %collective-permute-done.14 = bf16[3,128,256]{2,0,1:T(4,128)(2,1)S(1)} collective-permute-done((bf16[3,128,256]{2,0,1:T(4,128)(2,1)S(1)}, bf16[3,128,256]{2,0,1:T(4,128)(2,1)S(1)}, u32[]{:S(2)}, u32[]{:S(2)}) %collective-permute-start.14) | collective-permute-done | bytes 196640 | tf_op jit(solution)/shard_map/ppermute | solution.py:11
  26.7 5.1 %collective-permute-start.8 = (bf16[3,128,256]{2,0,1:T(4,128)(2,1)S(1)}, bf16[3,128,256]{2,0,1:T(4,128)(2,1)S(1)}, u32[]{:S(2)}, u32[]{:S(2)}) collective-permute-start(bf16[3,128,256]{2,0,1:T(4,128)(2,1)S(1)} %collective-permute-done.7), channel_id=1, source_target_pairs={{0,480},{32,0},{64,32},{96,64},{128,96},{160,128},{192,160},{224,1... | collective-permute-start | bytes 589832 | tf_op jit(solution)/shard_map/ppermute | solution.py:11
  38.3 5.6 %collective-permute-start.9 = (bf16[3,128,256]{2,0,1:T(4,128)(2,1)S(1)}, bf16[3,128,256]{2,0,1:T(4,128)(2,1)S(1)}, u32[]{:S(2)}, u32[]{:S(2)}) collective-permute-start(bf16[3,128,256]{2,0,1:T(4,128)(2,1)S(1)} %collective-permute-done.8), channel_id=1, source_target_pairs={{0,480},{32,0},{64,32},{96,64},{128,96},{160,128},{192,160},{224,1... | collective-permute-start | bytes 589832 | tf_op jit(solution)/shard_map/ppermute | solution.py:11
  49.7 5.6 %collective-permute-start.10 = (bf16[3,128,256]{2,0,1:T(4,128)(2,1)S(1)}, bf16[3,128,256]{2,0,1:T(4,128)(2,1)S(1)}, u32[]{:S(2)}, u32[]{:S(2)}) collective-permute-start(bf16[3,128,256]{2,0,1:T(4,128)(2,1)S(1)} %collective-permute-done.9), channel_id=1, source_target_pairs={{0,480},{32,0},{64,32},{96,64},{128,96},{160,128},{192,160},{224,1... | collective-permute-start | bytes 589832 | tf_op jit(solution)/shard_map/ppermute | solution.py:11
  60.3 5.6 %collective-permute-start.11 = (bf16[3,128,256]{2,0,1:T(4,128)(2,1)S(1)}, bf16[3,128,256]{2,0,1:T(4,128)(2,1)S(1)}, u32[]{:S(2)}, u32[]{:S(2)}) collective-permute-start(bf16[3,128,256]{2,0,1:T(4,128)(2,1)S(1)} %collective-permute-done.10), channel_id=1, source_target_pairs={{0,480},{32,0},{64,32},{96,64},{128,96},{160,128},{192,160},{224,1... | collective-permute-start | bytes 589832 | tf_op jit(solution)/shard_map/ppermute | solution.py:11
  70.0 5.6 %collective-permute-start.12 = (bf16[3,128,256]{2,0,1:T(4,128)(2,1)S(1)}, bf16[3,128,256]{2,0,1:T(4,128)(2,1)S(1)}, u32[]{:S(2)}, u32[]{:S(2)}) collective-permute-start(bf16[3,128,256]{2,0,1:T(4,128)(2,1)S(1)} %collective-permute-done.11), channel_id=1, source_target_pairs={{0,480},{32,0},{64,32},{96,64},{128,96},{160,128},{192,160},{224,1... | collective-permute-start | bytes 589832 | tf_op jit(solution)/shard_map/ppermute | solution.py:11
  79.5 5.6 %collective-permute-start.13 = (bf16[3,128,256]{2,0,1:T(4,128)(2,1)S(1)}, bf16[3,128,256]{2,0,1:T(4,128)(2,1)S(1)}, u32[]{:S(2)}, u32[]{:S(2)}) collective-permute-start(bf16[3,128,256]{2,0,1:T(4,128)(2,1)S(1)} %collective-permute-done.12), channel_id=1, source_target_pairs={{0,480},{32,0},{64,32},{96,64},{128,96},{160,128},{192,160},{224,1... | collective-permute-start | bytes 589832 | tf_op jit(solution)/shard_map/ppermute | solution.py:11
  94.7 39.9 %concatenate.16 = bf16[48,128,256]{2,0,1:T(8,128)(2,1)S(1)} concatenate(bf16[3,128,256]{2,0,1:T(4,128)(2,1)} %copy-done.1, bf16[3,128,256]{2,0,1:T(4,128)(2,1)} %copy-done.2, bf16[3,128,256]{2,0,1:T(4,128)(2,1)} %copy-done.5, bf16[3,128,256]{2,0,1:T(4,128)(2,1)} %copy-done.7, bf16[3,128,256]{2,0,1:T(4,128)(2,1)} %copy-done.9, bf16[3,128,256]{2,0,1:T(4,128)(2,1)} %copy-done.11, ...), dimensions={0} | concatenate | bytes 6291456 | tf_op jit(solution)/shard_map/concatenate | solution.py:67
  136.7 5.6 %copy.24 = bf16[112,128,256]{2,1,0:T(8,128)(2,1)} copy(bf16[112,128,256]{2,0,1:T(8,128)(2,1)S(1)} %convolution_convert_fusion) | data formatting | bytes 14680064 | tf_op jit(solution)/shard_map/convert_element_type | solution.py:81
  164.6 6.2 %collective-permute-done.23 = bf16[48,14,256]{2,1,0:T(8,128)(2,1)S(1)} collective-permute-done((bf16[48,14,256]{2,1,0:T(8,128)(2,1)S(1)}, bf16[48,14,256]{2,1,0:T(8,128)(2,1)S(1)}, u32[]{:S(2)}, u32[]{:S(2)}) %collective-permute-start.23) | collective-permute-done | bytes 344096 | tf_op jit(solution)/shard_map/ppermute | solution.py:11
  179.3 6.5 %collective-permute-done.26 = bf16[48,14,256]{2,1,0:T(8,128)(2,1)S(1)} collective-permute-done((bf16[48,14,256]{2,1,0:T(8,128)(2,1)S(1)}, bf16[48,14,256]{2,1,0:T(8,128)(2,1)S(1)}, u32[]{:S(2)}, u32[]{:S(2)}) %collective-permute-start.26) | collective-permute-done | bytes 344096 | tf_op jit(solution)/shard_map/ppermute | solution.py:11
  189.6 7.2 %collective-permute-done.27 = bf16[48,14,256]{2,1,0:T(8,128)(2,1)S(1)} collective-permute-done((bf16[48,14,256]{2,1,0:T(8,128)(2,1)S(1)}, bf16[48,14,256]{2,1,0:T(8,128)(2,1)S(1)}, u32[]{:S(2)}, u32[]{:S(2)}) %collective-permute-start.27) | collective-permute-done | bytes 344096 | tf_op jit(solution)/shard_map/ppermute | solution.py:11
  200.5 5.1 %convert_bitcast_fusion = bf16[8,14,128,256]{2,3,0,1:T(8,128)(2,1)} fusion(bf16[192,14,256,1]{2,0,3,1:T(8,128)(2,1)S(1)} %bitcast.121, bf16[192,8,128]{2,1,0:T(8,128)(2,1)S(1)} %bitcast.124), kind=kOutput, calls=%fused_computation.2 | convolution fusion | flops 1412956160 | bytes 9109504 | tf_op jit(solution)/shard_map/trk,tcn->rckn/dot_general | solution.py:101
  205.6 9.9 %copy.32 = bf16[8,14,128,256]{3,2,1,0:T(8,128)(2,1)} copy(bf16[8,14,128,256]{2,3,0,1:T(8,128)(2,1)} %convert_bitcast_fusion) | data formatting | bytes 14680064 | tf_op jit(solution)/shard_map/convert_element_type | solution.py:101
  215.5 8.0 %fusion.2 = bf16[48,128,256]{2,0,1:T(8,128)(2,1)S(1)} fusion(bf16[112,128,256]{2,1,0:T(8,128)(2,1)} %bitcast.118, s32[112]{0:T(128)S(1)} %add_reduce_fusion, s32[48]{0:T(128)S(1)} %fusion.40, pred[112]{0:T(512)(128)(4,1)S(1)} %gt.25), kind=kOutput, calls=%fused_computation.15 | convolution fusion | flops 353905152 | bytes 10486512 | tf_op jit(solution)/shard_map/qb,bkn->qkn/dot_general | solution.py:102
  226.5 5.1 %collective-permute-start.43 = (bf16[3,128,256]{2,0,1:T(4,128)(2,1)}, bf16[3,128,256]{2,0,1:T(4,128)(2,1)}, u32[]{:S(2)}, u32[]{:S(2)}) collective-permute-start(bf16[3,128,256]{2,0,1:T(4,128)(2,1)} %get-tuple-element.26), channel_id=1, source_target_pairs={{0,480},{32,0},{64,32},{96,64},{128,96},{160,128},{192,160},{224,1... | collective-permute-start | bytes 589832 | tf_op jit(solution)/shard_map/ppermute | solution.py:11
  239.0 6.0 %fusion.13 = bf16[192,8,128]{2,0,1:T(8,128)(2,1)S(1)} fusion(bf16[192,14,256,1]{2,0,1,3:T(8,128)(2,1)} %bitcast.122, bf16[8,14,128,256]{3,2,1,0:T(8,128)(2,1)} %bitcast.120), kind=kOutput, calls=%fused_computation.25 | convolution fusion | flops 1409482752 | bytes 9109504 | tf_op jit(solution)/shard_map/tcn,rckn->trk/dot_general | solution.py:97
  251.3 5.1 %collective-permute-start.44 = (bf16[3,128,256]{2,0,1:T(4,128)(2,1)S(1)}, bf16[3,128,256]{2,0,1:T(4,128)(2,1)S(1)}, u32[]{:S(2)}, u32[]{:S(2)}) collective-permute-start(bf16[3,128,256]{2,0,1:T(4,128)(2,1)S(1)} %get-tuple-element.24), channel_id=1, source_target_pairs={{0,480},{32,0},{64,32},{96,64},{128,96},{160,128},{192,160},{224,1... | collective-permute-start | bytes 589832 | tf_op jit(solution)/shard_map/ppermute | solution.py:11
  262.7 5.6 %collective-permute-start.45 = (bf16[3,128,256]{2,0,1:T(4,128)(2,1)S(1)}, bf16[3,128,256]{2,0,1:T(4,128)(2,1)S(1)}, u32[]{:S(2)}, u32[]{:S(2)}) collective-permute-start(bf16[3,128,256]{2,0,1:T(4,128)(2,1)S(1)} %get-tuple-element.22), channel_id=1, source_target_pairs={{0,480},{32,0},{64,32},{96,64},{128,96},{160,128},{192,160},{224,1... | collective-permute-start | bytes 589832 | tf_op jit(solution)/shard_map/ppermute | solution.py:11
  274.5 5.6 %collective-permute-start.46 = (bf16[3,128,256]{2,0,1:T(4,128)(2,1)S(1)}, bf16[3,128,256]{2,0,1:T(4,128)(2,1)S(1)}, u32[]{:S(2)}, u32[]{:S(2)}) collective-permute-start(bf16[3,128,256]{2,0,1:T(4,128)(2,1)S(1)} %get-tuple-element.20), channel_id=1, source_target_pairs={{0,480},{32,0},{64,32},{96,64},{128,96},{160,128},{192,160},{224,1... | collective-permute-start | bytes 589832 | tf_op jit(solution)/shard_map/ppermute | solution.py:11
  286.4 5.6 %collective-permute-start.47 = (bf16[3,128,256]{2,0,1:T(4,128)(2,1)S(1)}, bf16[3,128,256]{2,0,1:T(4,128)(2,1)S(1)}, u32[]{:S(2)}, u32[]{:S(2)}) collective-permute-start(bf16[3,128,256]{2,0,1:T(4,128)(2,1)S(1)} %get-tuple-element.18), channel_id=1, source_target_pairs={{0,480},{32,0},{64,32},{96,64},{128,96},{160,128},{192,160},{224,1... | collective-permute-start | bytes 589832 | tf_op jit(solution)/shard_map/ppermute | solution.py:11
  308.1 5.6 %collective-permute-start.49 = (bf16[3,128,256]{2,0,1:T(4,128)(2,1)S(1)}, bf16[3,128,256]{2,0,1:T(4,128)(2,1)S(1)}, u32[]{:S(2)}, u32[]{:S(2)}) collective-permute-start(bf16[3,128,256]{2,0,1:T(4,128)(2,1)S(1)} %get-tuple-element.14), channel_id=1, source_target_pairs={{0,480},{32,0},{64,32},{96,64},{128,96},{160,128},{192,160},{224,1... | collective-permute-start | bytes 589832 | tf_op jit(solution)/shard_map/ppermute | solution.py:11
  317.6 5.6 %collective-permute-done.42 = bf16[3,128,256]{2,0,1:T(4,128)(2,1)S(1)} collective-permute-done((bf16[3,128,256]{2,0,1:T(4,128)(2,1)S(1)}, bf16[3,128,256]{2,0,1:T(4,128)(2,1)S(1)}, u32[]{:S(2)}, u32[]{:S(2)}) %collective-permute-start.42) | collective-permute-done | bytes 196640 | tf_op jit(solution)/shard_map/ppermute | solution.py:11
  (165 shorter events, 141.1 us)
Async XLA Ops:
  1.9 24.8 %collective-permute-start.7 = (bf16[3,128,256]{2,0,1:T(4,128)(2,1)S(1)}, bf16[3,128,256]{2,0,1:T(4,128)(2,1)S(1)}, u32[]{:S(2)}, u32[]{:S(2)}) collective-permute-start(bf16[3,128,256]{2,0,1:T(4,128)(2,1)S(1)} %pad_maximum_fusion.1), channel_id=1, source_target_pairs={{0,480},{32,0},{64,32},{96,64},{128,96},{160,128},{192,160},{224,1... | collective-permute-start | bytes 589832 | tf_op jit(solution)/shard_map/ppermute | solution.py:11
  13.3 10.9 %collective-permute-start.14 = (bf16[3,128,256]{2,0,1:T(4,128)(2,1)S(1)}, bf16[3,128,256]{2,0,1:T(4,128)(2,1)S(1)}, u32[]{:S(2)}, u32[]{:S(2)}) collective-permute-start(bf16[3,128,256]{2,0,1:T(4,128)(2,1)S(1)} %pad_maximum_fusion.1), channel_id=1, source_target_pairs={{0,32},{32,64},{64,96},{96,128},{128,160},{160,192},{192,224},{224... | collective-permute-start | bytes 589832 | tf_op jit(solution)/shard_map/ppermute | solution.py:11
  26.1 19.8 %collective-permute-start.2 = (bf16[24,1024]{1,0:T(8,128)(2,1)S(1)}, bf16[24,1024]{1,0:T(8,128)(2,1)S(1)}, u32[]{:S(2)}, u32[]{:S(2)}) collective-permute-start(bf16[24,1024]{1,0:T(8,128)(2,1)S(1)} %collective-permute-done.1), channel_id=1, source_target_pairs={{0,7},{1,0},{2,1},{3,2},{4,3},{5,4},{6,5},{7,6},{8,15},{9,8},{10,9... | collective-permute-start | bytes 147464 | tf_op jit(solution)/shard_map/ppermute | solution.py:11
  26.7 11.6 %collective-permute-start.8 = (bf16[3,128,256]{2,0,1:T(4,128)(2,1)S(1)}, bf16[3,128,256]{2,0,1:T(4,128)(2,1)S(1)}, u32[]{:S(2)}, u32[]{:S(2)}) collective-permute-start(bf16[3,128,256]{2,0,1:T(4,128)(2,1)S(1)} %collective-permute-done.7), channel_id=1, source_target_pairs={{0,480},{32,0},{64,32},{96,64},{128,96},{160,128},{192,160},{224,1... | collective-permute-start | bytes 589832 | tf_op jit(solution)/shard_map/ppermute | solution.py:11
  36.1 21.1 %collective-permute-start.6 = (bf16[24,1024]{1,0:T(8,128)(2,1)S(1)}, bf16[24,1024]{1,0:T(8,128)(2,1)S(1)}, u32[]{:S(2)}, u32[]{:S(2)}) collective-permute-start(bf16[24,1024]{1,0:T(8,128)(2,1)S(1)} %collective-permute-done.5), channel_id=1, source_target_pairs={{0,1},{1,2},{2,3},{3,4},{4,5},{5,6},{6,7},{7,0},{8,9},{9,10},{10,1... | collective-permute-start | bytes 147464 | tf_op jit(solution)/shard_map/ppermute | solution.py:11
  38.3 11.4 %collective-permute-start.9 = (bf16[3,128,256]{2,0,1:T(4,128)(2,1)S(1)}, bf16[3,128,256]{2,0,1:T(4,128)(2,1)S(1)}, u32[]{:S(2)}, u32[]{:S(2)}) collective-permute-start(bf16[3,128,256]{2,0,1:T(4,128)(2,1)S(1)} %collective-permute-done.8), channel_id=1, source_target_pairs={{0,480},{32,0},{64,32},{96,64},{128,96},{160,128},{192,160},{224,1... | collective-permute-start | bytes 589832 | tf_op jit(solution)/shard_map/ppermute | solution.py:11
  44.0 11.4 %collective-permute-start.17 = (bf16[3,128,256]{2,0,1:T(4,128)(2,1)S(1)}, bf16[3,128,256]{2,0,1:T(4,128)(2,1)S(1)}, u32[]{:S(2)}, u32[]{:S(2)}) collective-permute-start(bf16[3,128,256]{2,0,1:T(4,128)(2,1)S(1)} %collective-permute-done.16), channel_id=1, source_target_pairs={{0,32},{32,64},{64,96},{96,128},{128,160},{160,192},{192,224},{224... | collective-permute-start | bytes 589832 | tf_op jit(solution)/shard_map/ppermute | solution.py:11
  49.7 10.6 %collective-permute-start.10 = (bf16[3,128,256]{2,0,1:T(4,128)(2,1)S(1)}, bf16[3,128,256]{2,0,1:T(4,128)(2,1)S(1)}, u32[]{:S(2)}, u32[]{:S(2)}) collective-permute-start(bf16[3,128,256]{2,0,1:T(4,128)(2,1)S(1)} %collective-permute-done.9), channel_id=1, source_target_pairs={{0,480},{32,0},{64,32},{96,64},{128,96},{160,128},{192,160},{224,1... | collective-permute-start | bytes 589832 | tf_op jit(solution)/shard_map/ppermute | solution.py:11
  148.5 11.2 %collective-permute-start.22 = (bf16[48,14,256]{2,1,0:T(8,128)(2,1)S(1)}, bf16[48,14,256]{2,1,0:T(8,128)(2,1)S(1)}, u32[]{:S(2)}, u32[]{:S(2)}) collective-permute-start(bf16[48,14,256]{2,1,0:T(8,128)(2,1)S(1)} %get-tuple-element.27), channel_id=1, source_target_pairs={{0,8},{8,16},{16,24},{24,0},{1,9},{9,17},{17,25},{25,1},{2,10},{10... | collective-permute-start | bytes 1032200 | tf_op jit(solution)/shard_map/ppermute | solution.py:11
  152.0 12.6 %collective-permute-start.24 = (bf16[48,14,256]{2,1,0:T(8,128)(2,1)S(1)}, bf16[48,14,256]{2,1,0:T(8,128)(2,1)}, u32[]{:S(2)}, u32[]{:S(2)}) collective-permute-start(bf16[48,14,256]{2,1,0:T(8,128)(2,1)S(1)} %get-tuple-element.28), channel_id=1, source_target_pairs={{0,24},{8,0},{16,8},{24,16},{1,25},{9,1},{17,9},{25,17},{2,26},{10... | collective-permute-start | bytes 1032200 | tf_op jit(solution)/shard_map/ppermute | solution.py:11
  159.8 11.0 %collective-permute-start.23 = (bf16[48,14,256]{2,1,0:T(8,128)(2,1)S(1)}, bf16[48,14,256]{2,1,0:T(8,128)(2,1)S(1)}, u32[]{:S(2)}, u32[]{:S(2)}) collective-permute-start(bf16[48,14,256]{2,1,0:T(8,128)(2,1)S(1)} %fusion.15), channel_id=1, source_target_pairs={{0,8},{8,16},{16,24},{24,0},{1,9},{9,17},{17,25},{25,1},{2,10},{10... | collective-permute-start | bytes 1032200 | tf_op jit(solution)/shard_map/ppermute | solution.py:11
  172.2 13.6 %collective-permute-start.26 = (bf16[48,14,256]{2,1,0:T(8,128)(2,1)S(1)}, bf16[48,14,256]{2,1,0:T(8,128)(2,1)S(1)}, u32[]{:S(2)}, u32[]{:S(2)}) collective-permute-start(bf16[48,14,256]{2,1,0:T(8,128)(2,1)S(1)} %get-tuple-element.37), channel_id=1, source_target_pairs={{0,8},{8,16},{16,24},{24,0},{1,9},{9,17},{17,25},{25,1},{2,10},{10... | collective-permute-start | bytes 1032200 | tf_op jit(solution)/shard_map/ppermute | solution.py:11
  175.9 13.7 %collective-permute-start.25 = (bf16[48,14,256]{2,1,0:T(8,128)(2,1)S(1)}, bf16[48,14,256]{2,1,0:T(8,128)(2,1)S(1)}, u32[]{:S(2)}, u32[]{:S(2)}) collective-permute-start(bf16[48,14,256]{2,1,0:T(8,128)(2,1)S(1)} %get-tuple-element.37), channel_id=1, source_target_pairs={{0,24},{8,0},{16,8},{24,16},{1,25},{9,1},{17,9},{25,17},{2,26},{10... | collective-permute-start | bytes 1032200 | tf_op jit(solution)/shard_map/ppermute | solution.py:11
  185.8 10.9 %collective-permute-start.27 = (bf16[48,14,256]{2,1,0:T(8,128)(2,1)S(1)}, bf16[48,14,256]{2,1,0:T(8,128)(2,1)S(1)}, u32[]{:S(2)}, u32[]{:S(2)}) collective-permute-start(bf16[48,14,256]{2,1,0:T(8,128)(2,1)S(1)} %collective-permute-done.26), channel_id=1, source_target_pairs={{0,8},{8,16},{16,24},{24,0},{1,9},{9,17},{17,25},{25,1},{2,10},{10... | collective-permute-start | bytes 1032200 | tf_op jit(solution)/shard_map/ppermute | solution.py:11
  224.5 11.4 %collective-permute-start.35 = (bf16[3,128,256]{2,0,1:T(4,128)(2,1)}, bf16[3,128,256]{2,0,1:T(4,128)(2,1)S(1)}, u32[]{:S(2)}, u32[]{:S(2)}) collective-permute-start(bf16[3,128,256]{2,0,1:T(4,128)(2,1)} %get-tuple-element.25), channel_id=1, source_target_pairs={{0,32},{32,64},{64,96},{96,128},{128,160},{160,192},{192,224},{224... | collective-permute-start | bytes 589832 | tf_op jit(solution)/shard_map/ppermute | solution.py:11
  226.5 20.9 %collective-permute-start.43 = (bf16[3,128,256]{2,0,1:T(4,128)(2,1)}, bf16[3,128,256]{2,0,1:T(4,128)(2,1)}, u32[]{:S(2)}, u32[]{:S(2)}) collective-permute-start(bf16[3,128,256]{2,0,1:T(4,128)(2,1)} %get-tuple-element.26), channel_id=1, source_target_pairs={{0,480},{32,0},{64,32},{96,64},{128,96},{160,128},{192,160},{224,1... | collective-permute-start | bytes 589832 | tf_op jit(solution)/shard_map/ppermute | solution.py:11
  236.9 11.1 %collective-permute-start.36 = (bf16[3,128,256]{2,0,1:T(4,128)(2,1)}, bf16[3,128,256]{2,0,1:T(4,128)(2,1)}, u32[]{:S(2)}, u32[]{:S(2)}) collective-permute-start(bf16[3,128,256]{2,0,1:T(4,128)(2,1)} %add_convert_fusion.12), channel_id=1, source_target_pairs={{0,32},{32,64},{64,96},{96,128},{128,160},{160,192},{192,224},{224... | collective-permute-start | bytes 589832 | tf_op jit(solution)/shard_map/ppermute | solution.py:11
  256.5 11.8 %collective-permute-start.28 = (bf16[24,1024]{1,0:T(8,128)(2,1)S(1)}, bf16[24,1024]{1,0:T(8,128)(2,1)S(1)}, u32[]{:S(2)}, u32[]{:S(2)}) collective-permute-start(bf16[24,1024]{1,0:T(8,128)(2,1)S(1)} %get-tuple-element.35), channel_id=1, source_target_pairs={{0,1},{1,2},{2,3},{3,4},{4,5},{5,6},{6,7},{7,0},{8,9},{9,10},{10,1... | collective-permute-start | bytes 147464 | tf_op jit(solution)/shard_map/ppermute | solution.py:11
  256.5 35.5 %collective-permute-start.32 = (bf16[24,1024]{1,0:T(8,128)(2,1)S(1)}, bf16[24,1024]{1,0:T(8,128)(2,1)S(1)}, u32[]{:S(2)}, u32[]{:S(2)}) collective-permute-start(bf16[24,1024]{1,0:T(8,128)(2,1)S(1)} %get-tuple-element.36), channel_id=1, source_target_pairs={{0,7},{1,0},{2,1},{3,2},{4,3},{5,4},{6,5},{7,6},{8,15},{9,8},{10,9... | collective-permute-start | bytes 147464 | tf_op jit(solution)/shard_map/ppermute | solution.py:11
  268.3 11.8 %collective-permute-start.29 = (bf16[24,1024]{1,0:T(8,128)(2,1)S(1)}, bf16[24,1024]{1,0:T(8,128)(2,1)S(1)}, u32[]{:S(2)}, u32[]{:S(2)}) collective-permute-start(bf16[24,1024]{1,0:T(8,128)(2,1)S(1)} %fusion.31), channel_id=1, source_target_pairs={{0,1},{1,2},{2,3},{3,4},{4,5},{5,6},{6,7},{7,0},{8,9},{9,10},{10,1... | collective-permute-start | bytes 147464 | tf_op jit(solution)/shard_map/ppermute | solution.py:11
  280.2 11.8 %collective-permute-start.30 = (bf16[24,1024]{1,0:T(8,128)(2,1)S(1)}, bf16[24,1024]{1,0:T(8,128)(2,1)S(1)}, u32[]{:S(2)}, u32[]{:S(2)}) collective-permute-start(bf16[24,1024]{1,0:T(8,128)(2,1)S(1)} %fusion.30), channel_id=1, source_target_pairs={{0,1},{1,2},{2,3},{3,4},{4,5},{5,6},{6,7},{7,0},{8,9},{9,10},{10,1... | collective-permute-start | bytes 147464 | tf_op jit(solution)/shard_map/ppermute | solution.py:11
  292.0 11.8 %collective-permute-start.33 = (bf16[24,1024]{1,0:T(8,128)(2,1)S(1)}, bf16[24,1024]{1,0:T(8,128)(2,1)S(1)}, u32[]{:S(2)}, u32[]{:S(2)}) collective-permute-start(bf16[24,1024]{1,0:T(8,128)(2,1)S(1)} %get-tuple-element.34), channel_id=1, source_target_pairs={{0,7},{1,0},{2,1},{3,2},{4,3},{5,4},{6,5},{7,6},{8,15},{9,8},{10,9... | collective-permute-start | bytes 147464 | tf_op jit(solution)/shard_map/ppermute | solution.py:11
  292.1 23.6 %collective-permute-start.31 = (bf16[24,1024]{1,0:T(8,128)(2,1)S(1)}, bf16[24,1024]{1,0:T(8,128)(2,1)S(1)}, u32[]{:S(2)}, u32[]{:S(2)}) collective-permute-start(bf16[24,1024]{1,0:T(8,128)(2,1)S(1)} %get-tuple-element.33), channel_id=1, source_target_pairs={{0,1},{1,2},{2,3},{3,4},{4,5},{5,6},{6,7},{7,0},{8,9},{9,10},{10,1... | collective-permute-start | bytes 147464 | tf_op jit(solution)/shard_map/ppermute | solution.py:11
  303.9 11.8 %collective-permute-start.34 = (bf16[24,1024]{1,0:T(8,128)(2,1)S(1)}, bf16[24,1024]{1,0:T(8,128)(2,1)S(1)}, u32[]{:S(2)}, u32[]{:S(2)}) collective-permute-start(bf16[24,1024]{1,0:T(8,128)(2,1)S(1)} %fusion.25), channel_id=1, source_target_pairs={{0,7},{1,0},{2,1},{3,2},{4,3},{5,4},{6,5},{7,6},{8,15},{9,8},{10,9... | collective-permute-start | bytes 147464 | tf_op jit(solution)/shard_map/ppermute | solution.py:11
  (42 other events, 755.1 us)

commit v2 on v1

--- a/solution.py
+++ b/solution.py
@@ -64,10 +64,12 @@
     cols_per = tok // n_col
 
     pair_local = jnp.concatenate([gate_slots[0, 0], up_slots[0, 0]], axis=2)
+    pair_local = pair_local.reshape(per_dev * bs, 2 * bs)
     pair_rel = jnp.concatenate(ring_gather(pair_local, "dp", n_dp), axis=0)
+    pair_rel = pair_rel.reshape(cap, bs, 2 * bs)
 
     x_rel = jnp.stack(ring_gather(layer_input, "col", n_col))
-    x_abs = jnp.roll(x_rel, k_col, axis=0).reshape(tok, tile_rows, bs)
+    x_abs = jnp.roll(x_rel, k_col, axis=0).reshape(tok, feat)
 
     tile_mask = lax.dynamic_slice(
         block_mask, (k_row * tile_rows, k_col * tile_cols), (tile_rows, tile_cols)
@@ -75,39 +77,44 @@
     kept = tile_mask > 0
     position = jnp.cumsum(kept.astype(jnp.int32)) - 1
     q = jnp.arange(cap, dtype=jnp.int32)
-    slot_of_q = ((k_dp + q // per_dev) % n_dp) * per_dev + q % per_dev
-    onehot = (kept[None, :] & (position[None, :] == slot_of_q[:, None])).astype(BF16)
+    slot_rel = ((k_dp + q // per_dev) % n_dp) * per_dev + q % per_dev
+    onehot_rel = (kept[None, :] & (position[None, :] == slot_rel[:, None])).astype(BF16)
+    onehot_abs = (kept[None, :] & (position[None, :] == q[:, None])).astype(BF16)
 
-    dense = jnp.einsum("qb,qkn->bkn", onehot, pair_rel, preferred_element_type=F32).astype(BF16)
-    dense4 = dense.reshape(tile_rows, tile_cols, bs, 2 * bs)
+    dense = jnp.einsum("qb,qkn->bkn", onehot_rel, pair_rel, preferred_element_type=F32).astype(BF16)
+    wd = dense.reshape(tile_rows, tile_cols, bs, 2 * bs).transpose(0, 2, 1, 3)
+    wd = wd.reshape(feat, tile_cols * 2 * bs)
 
-    pre = jnp.einsum("trk,rckn->tcn", x_abs, dense4, preferred_element_type=F32).astype(BF16)
-    pre_roll = jnp.roll(pre.reshape(n_row, rows_per, tile_cols, 2 * bs), -k_row, axis=0)
+    pre = jnp.dot(x_abs, wd, preferred_element_type=F32).astype(BF16)
+    pre_roll = jnp.roll(pre.reshape(n_row, rows_per, tile_cols * 2 * bs), -k_row, axis=0)
     pre_sum = ring_sum_scatter([pre_roll[m] for m in range(n_row)], "row", n_row)
+    pre_sum = pre_sum.reshape(rows_per, tile_cols, 2 * bs)
     gate = pre_sum[..., :bs]
     up = pre_sum[..., bs:]
     upstream = hidden_grad.astype(F32).reshape(rows_per, tile_cols, bs)
     sig = jax.nn.sigmoid(gate)
     gate_grad = (upstream * up * sig * (1.0 + gate * (1.0 - sig))).astype(BF16)
     up_grad = (upstream * gate * sig).astype(BF16)
-    grad_local = jnp.concatenate([gate_grad, up_grad], axis=2)
+    grad_local = jnp.concatenate([gate_grad, up_grad], axis=2).reshape(rows_per, tile_cols * 2 * bs)
     grad_rel = jnp.stack(ring_gather(grad_local, "row", n_row))
-    grad_abs = jnp.roll(grad_rel, k_row, axis=0).reshape(tok, tile_cols, 2 * bs)
+    grad_abs = jnp.roll(grad_rel, k_row, axis=0).reshape(tok, tile_cols * 2 * bs)
 
-    dx = jnp.einsum("tcn,rckn->trk", grad_abs, dense4, preferred_element_type=F32).astype(BF16)
+    dx = lax.dot_general(
+        grad_abs, wd, (((1,), (1,)), ((), ())), preferred_element_type=F32
+    ).astype(BF16)
     dx_roll = jnp.roll(dx.reshape(n_col, cols_per, feat), -k_col, axis=0)
     input_grad = ring_sum_scatter([dx_roll[m] for m in range(n_col)], "col", n_col).astype(BF16)
 
-    dw = jnp.einsum("trk,tcn->rckn", x_abs, grad_abs, preferred_element_type=F32).astype(BF16)
-    slot_dw = jnp.einsum(
-        "qb,bkn->qkn",
-        onehot,
-        dw.reshape(tile_rows * tile_cols, bs, 2 * bs),
-        preferred_element_type=F32,
+    dw = lax.dot_general(
+        x_abs, grad_abs, (((0,), (0,)), ((), ())), preferred_element_type=F32
     ).astype(BF16)
-    dw_sum = ring_sum_scatter(
-        [slot_dw[m * per_dev:(m + 1) * per_dev] for m in range(n_dp)], "dp", n_dp
-    ) / n_dp
+    dw_blocks = dw.reshape(tile_rows, bs, tile_cols, 2 * bs).transpose(0, 2, 1, 3)
+    dw_blocks = dw_blocks.reshape(tile_rows * tile_cols, bs, 2 * bs)
+    slot_dw = jnp.einsum("qb,bkn->qkn", onehot_abs, dw_blocks, preferred_element_type=F32).astype(BF16)
+    dw_sum = lax.psum_scatter(
+        slot_dw.reshape(cap * bs, 2 * bs), "dp", scatter_dimension=0, tiled=True
+    ).astype(F32) / n_dp
+    dw_sum = dw_sum.reshape(per_dev, bs, 2 * bs)
     gate_out = dw_sum[..., :bs][None, None]
     up_out = dw_sum[..., bs:][None, None]
     return (input_grad, gate_out, up_out)

time: 330 us -> 300 us (0.909)
  the two profiles are of different devices: /device:TPU:2 before, /device:TPU:10 now
where the time goes in v2:
time: 300 us; the launch traced here: 299 us
  waiting for transfers between devices  108 us (36%)
  starting transfers between devices  93.4 us (31%)
  local copies, waits for them, and re-layouts  47.5 us (16%)
  matrix products  22.7 us (8%)
  between operations  14.7 us (5%)
  other arithmetic  12.5 us (4%)
    ppermute x35, starting transfers between devices, _shift(): return lax.ppermute(x, axis, perm=[(i, (i + step) % n) for i in range(n)])  93.4 us
    ppermute x35, waiting for transfers between devices, _shift(): return lax.ppermute(x, axis, perm=[(i, (i + step) % n) for i in range(n)])  60.9 us
    reduce_scatter x1, waiting for transfers between devices, on_device(): lax.psum_scatter(slot_dw.reshape(cap * bs, 2 * bs), 'dp', scatter_dimensi...  46.9 us
    reshape x1, local copies, waits for them, and re-layouts, on_device(): dw.reshape(tile_rows, bs, tile_cols, 2 * bs).transpose(0, 2, 1, 3)  13.4 us
    transpose x1, local copies, waits for them, and re-layouts, on_device(): wd = dense.reshape(tile_rows, tile_cols, bs, 2 * bs).transpose(0, 2, 1, 3)  10.9 us
    transpose x1, local copies, waits for them, and re-layouts, on_device(): dw.reshape(tile_rows, bs, tile_cols, 2 * bs).transpose(0, 2, 1, 3)  6.27 us
  transfers between devices with their start and end apart: 36, of which 24 were waited for; matrix products, arithmetic and copies ran while one was open for 6% of the time, Pallas kernels for 0%

profile of v2, /device:TPU:10, one launch (start us, length us, event | category | flops | bytes accessed | tf_op | source)
XLA Modules:
  0.0 298.6 jit_solution(3180545738975063860)
XLA Ops:
  10.6 11.4 %collective-permute-start.7 = (bf16[384,256]{1,0:T(8,128)(2,1)}, bf16[384,256]{1,0:T(8,128)(2,1)}, u32[]{:S(2)}, u32[]{:S(2)}) collective-permute-start(bf16[384,256]{1,0:T(8,128)(2,1)} %get-tuple-element.17), channel_id=1, source_target_pairs={{0,480},{32,0},{64,32},{96,64},{128,96},{160,128},{192,160},{224,1... | collective-permute-start | bytes 589832 | tf_op jit(solution)/shard_map/ppermute | solution.py:11
  36.1 5.1 %collective-permute-start.8 = (bf16[384,256]{1,0:T(8,128)(2,1)}, bf16[384,256]{1,0:T(8,128)(2,1)S(1)}, u32[]{:S(2)}, u32[]{:S(2)}) collective-permute-start(bf16[384,256]{1,0:T(8,128)(2,1)} %collective-permute-done.7), channel_id=1, source_target_pairs={{0,480},{32,0},{64,32},{96,64},{128,96},{160,128},{192,160},{224,1... | collective-permute-start | bytes 589832 | tf_op jit(solution)/shard_map/ppermute | solution.py:11
  46.2 5.5 %collective-permute-start.9 = (bf16[384,256]{1,0:T(8,128)(2,1)S(1)}, bf16[384,256]{1,0:T(8,128)(2,1)S(1)}, u32[]{:S(2)}, u32[]{:S(2)}) collective-permute-start(bf16[384,256]{1,0:T(8,128)(2,1)S(1)} %collective-permute-done.8), channel_id=1, source_target_pairs={{0,480},{32,0},{64,32},{96,64},{128,96},{160,128},{192,160},{224,1... | collective-permute-start | bytes 589832 | tf_op jit(solution)/shard_map/ppermute | solution.py:11
  56.5 5.6 %collective-permute-start.10 = (bf16[384,256]{1,0:T(8,128)(2,1)S(1)}, bf16[384,256]{1,0:T(8,128)(2,1)S(1)}, u32[]{:S(2)}, u32[]{:S(2)}) collective-permute-start(bf16[384,256]{1,0:T(8,128)(2,1)S(1)} %collective-permute-done.9), channel_id=1, source_target_pairs={{0,480},{32,0},{64,32},{96,64},{128,96},{160,128},{192,160},{224,1... | collective-permute-start | bytes 589832 | tf_op jit(solution)/shard_map/ppermute | solution.py:11
  64.8 6.5 %collective-permute-done.17 = bf16[384,256]{1,0:T(8,128)(2,1)S(1)} collective-permute-done((bf16[384,256]{1,0:T(8,128)(2,1)S(1)}, bf16[384,256]{1,0:T(8,128)(2,1)S(1)}, u32[]{:S(2)}, u32[]{:S(2)}) %collective-permute-start.17) | collective-permute-done | bytes 196640 | tf_op jit(solution)/shard_map/ppermute | solution.py:11
  74.4 5.1 %collective-permute-start.11 = (bf16[384,256]{1,0:T(8,128)(2,1)S(1)}, bf16[384,256]{1,0:T(8,128)(2,1)S(1)}, u32[]{:S(2)}, u32[]{:S(2)}) collective-permute-start(bf16[384,256]{1,0:T(8,128)(2,1)S(1)} %collective-permute-done.10), channel_id=1, source_target_pairs={{0,480},{32,0},{64,32},{96,64},{128,96},{160,128},{192,160},{224,1... | collective-permute-start | bytes 589832 | tf_op jit(solution)/shard_map/ppermute | solution.py:11
  82.7 5.6 %collective-permute-start.12 = (bf16[384,256]{1,0:T(8,128)(2,1)S(1)}, bf16[384,256]{1,0:T(8,128)(2,1)S(1)}, u32[]{:S(2)}, u32[]{:S(2)}) collective-permute-start(bf16[384,256]{1,0:T(8,128)(2,1)S(1)} %collective-permute-done.11), channel_id=1, source_target_pairs={{0,480},{32,0},{64,32},{96,64},{128,96},{160,128},{192,160},{224,1... | collective-permute-start | bytes 589832 | tf_op jit(solution)/shard_map/ppermute | solution.py:11
  91.5 5.6 %collective-permute-start.13 = (bf16[384,256]{1,0:T(8,128)(2,1)S(1)}, bf16[384,256]{1,0:T(8,128)(2,1)S(1)}, u32[]{:S(2)}, u32[]{:S(2)}) collective-permute-start(bf16[384,256]{1,0:T(8,128)(2,1)S(1)} %collective-permute-done.12), channel_id=1, source_target_pairs={{0,480},{32,0},{64,32},{96,64},{128,96},{160,128},{192,160},{224,1... | collective-permute-start | bytes 589832 | tf_op jit(solution)/shard_map/ppermute | solution.py:11
  100.3 6.5 %collective-permute-done.21 = bf16[384,256]{1,0:T(8,128)(2,1)S(1)} collective-permute-done((bf16[384,256]{1,0:T(8,128)(2,1)S(1)}, bf16[384,256]{1,0:T(8,128)(2,1)S(1)}, u32[]{:S(2)}, u32[]{:S(2)}) %collective-permute-start.21) | collective-permute-done | bytes 196640 | tf_op jit(solution)/shard_map/ppermute | solution.py:11
  110.3 5.6 %copy.12 = bf16[112,128,256]{2,1,0:T(8,128)(2,1)} copy(bf16[112,128,256]{2,0,1:T(8,128)(2,1)S(1)} %convolution_convert_fusion.1) | data formatting | bytes 14680064 | tf_op jit(solution)/shard_map/convert_element_type | solution.py:84
  115.9 10.9 %copy.13 = bf16[8,128,14,256]{1,0,3,2:T(8,128)(2,1)} copy(bf16[8,128,14,256]{3,1,2,0:T(8,128)(2,1)} %bitcast.112) | data formatting | bytes 14680064 | tf_op jit(solution)/shard_map/transpose | solution.py:85
  126.8 5.6 %fusion.8 = bf16[192,3584]{1,0:T(8,128)(2,1)S(1)} fusion(bf16[192,1024]{1,0:T(8,128)(2,1)S(1)} %bitcast.121, bf16[448,8,8,128]{3,2,1,0:T(8,128)(2,1)} %bitcast.115), kind=kOutput, calls=%fused_computation.10 | convolution fusion | flops 1409974272 | bytes 9109504 | tf_op jit(solution)/shard_map/dot_general | solution.py:88
  138.9 5.4 %collective-permute-done.22 = bf16[48,3584]{1,0:T(8,128)(2,1)S(1)} collective-permute-done((bf16[48,3584]{1,0:T(8,128)(2,1)S(1)}, bf16[48,3584]{1,0:T(8,128)(2,1)S(1)}, u32[]{:S(2)}, u32[]{:S(2)}) %collective-permute-start.22) | collective-permute-done | bytes 344096 | tf_op jit(solution)/shard_map/ppermute | solution.py:11
  148.9 6.2 %collective-permute-done.23 = bf16[48,3584]{1,0:T(8,128)(2,1)} collective-permute-done((bf16[48,3584]{1,0:T(8,128)(2,1)S(1)}, bf16[48,3584]{1,0:T(8,128)(2,1)}, u32[]{:S(2)}, u32[]{:S(2)}) %collective-permute-start.23) | collective-permute-done | bytes 344096 | tf_op jit(solution)/shard_map/ppermute | solution.py:11
  162.9 6.0 %collective-permute-done.26 = bf16[48,3584]{1,0:T(8,128)(2,1)S(1)} collective-permute-done((bf16[48,3584]{1,0:T(8,128)(2,1)S(1)}, bf16[48,3584]{1,0:T(8,128)(2,1)S(1)}, u32[]{:S(2)}, u32[]{:S(2)}) %collective-permute-start.26) | collective-permute-done | bytes 344096 | tf_op jit(solution)/shard_map/ppermute | solution.py:11
  172.7 5.3 %collective-permute-done.27 = bf16[48,3584]{1,0:T(8,128)(2,1)S(1)} collective-permute-done((bf16[48,3584]{1,0:T(8,128)(2,1)S(1)}, bf16[48,3584]{1,0:T(8,128)(2,1)S(1)}, u32[]{:S(2)}, u32[]{:S(2)}) %collective-permute-start.27) | collective-permute-done | bytes 344096 | tf_op jit(solution)/shard_map/ppermute | solution.py:11
  181.4 5.1 %convolution_convert_fusion = bf16[1024,3584]{1,0:T(8,128)(2,1)} fusion(bf16[192,1024]{1,0:T(8,128)(2,1)S(1)} %bitcast.122, bf16[192,3584]{1,0:T(8,128)(2,1)S(1)} %bitcast.117), kind=kOutput, calls=%fused_computation | convolution fusion | flops 1412956160 | bytes 9109504 | tf_op jit(solution)/shard_map/dot_general | solution.py:108
  186.4 13.4 %reshape.180 = bf16[8,128,14,256]{3,2,1,0:T(8,128)(2,1)} reshape(bf16[1024,3584]{1,0:T(8,128)(2,1)} %convolution_convert_fusion) | data formatting | bytes 14680064 | tf_op jit(solution)/shard_map/reshape | solution.py:111
  199.9 6.3 %copy.15 = bf16[8,14,128,256]{3,2,1,0:T(8,128)(2,1)S(1)} copy(bf16[8,14,128,256]{3,1,2,0:T(8,128)(2,1)} %bitcast.111) | data formatting | bytes 14680064 | tf_op jit(solution)/shard_map/transpose | solution.py:111
  206.1 4.9 %fusion.12 = bf16[48,128,256]{2,0,1:T(8,128)(2,1)S(1)} fusion(bf16[112,128,256]{2,1,0:T(8,128)(2,1)S(1)} %bitcast.113, s32[112]{0:T(128)S(1)} %add_reduce_fusion, pred[112]{0:T(512)(128)(4,1)S(1)} %gt.25), kind=kOutput, calls=%fused_computation.22 | convolution fusion | flops 353905152 | bytes 10486320 | tf_op jit(solution)/shard_map/qb,bkn->qkn/dot_general | solution.py:113
  213.8 4.7 %fusion.23 = bf16[192,1024]{1,0:T(8,128)(2,1)S(1)} fusion(bf16[192,3584]{1,0:T(8,128)(2,1)S(1)} %bitcast.118, bf16[448,8,8,128]{3,2,1,0:T(8,128)(2,1)} %bitcast.116), kind=kOutput, calls=%fused_computation.31 | convolution fusion | flops 1409482752 | bytes 9109504 | tf_op jit(solution)/shard_map/dot_general | solution.py:102
  222.3 4.1 %collective-permute-start.32 = (bf16[24,1024]{1,0:T(8,128)(2,1)S(1)}, bf16[24,1024]{1,0:T(8,128)(2,1)S(1)}, u32[]{:S(2)}, u32[]{:S(2)}) collective-permute-start(bf16[24,1024]{1,0:T(8,128)(2,1)S(1)} %get-tuple-element.16), channel_id=1, source_target_pairs={{0,7},{1,0},{2,1},{3,2},{4,3},{5,4},{6,5},{7,6},{8,15},{9,8},{10,9... | collective-permute-start | bytes 147464 | tf_op jit(solution)/shard_map/ppermute | solution.py:11
  228.1 4.7 %collective-permute-done.30 = bf16[24,1024]{1,0:T(8,128)(2,1)S(1)} collective-permute-done((bf16[24,1024]{1,0:T(8,128)(2,1)S(1)}, bf16[24,1024]{1,0:T(8,128)(2,1)S(1)}, u32[]{:S(2)}, u32[]{:S(2)}) %collective-permute-start.30) | collective-permute-done | bytes 49184 | tf_op jit(solution)/shard_map/ppermute | solution.py:11
  243.1 46.9 %reduce-scatter.2.cloned.1.call-done = bf16[384,256]{1,0:T(8,128)(2,1)} async-done(((bf16[6144,256]{1,0:T(8,128)(2,1)}), bf16[384,256]{1,0:T(8,128)(2,1)}) %reduce-scatter.2.cloned.1.call-update) | async-done | bytes 196624 | tf_op jit(solution)/shard_map/reduce_scatter | solution.py:114
  (114 shorter events, 91.9 us)
Async XLA Ops:
  7.2 282.9 %reduce-scatter.2.cloned.1.call-start = ((), (), s32[]{:S(2)}) async-start(), calls=%async_computation.1 | async-start | bytes 3342336 | tf_op jit(solution)/shard_map/reduce_scatter | solution.py:114
  7.2 21.7 %collective-permute-start.3 = (bf16[24,1024]{1,0:T(8,128)(2,1)}, bf16[24,1024]{1,0:T(8,128)(2,1)}, u32[]{:S(2)}, u32[]{:S(2)}) collective-permute-start(bf16[24,1024]{1,0:T(8,128)(2,1)} %param.9), channel_id=1, source_target_pairs={{0,1},{1,2},{2,3},{3,4},{4,5},{5,6},{6,7},{7,0},{8,9},{9,10},{10,1... | collective-permute-start | bytes 147464 | tf_op jit(solution)/shard_map/ppermute | solution.py:11
  7.2 21.7 %collective-permute-start = (bf16[24,1024]{1,0:T(8,128)(2,1)}, bf16[24,1024]{1,0:T(8,128)(2,1)}, u32[]{:S(2)}, u32[]{:S(2)}) collective-permute-start(bf16[24,1024]{1,0:T(8,128)(2,1)} %param.9), channel_id=1, source_target_pairs={{0,7},{1,0},{2,1},{3,2},{4,3},{5,4},{6,5},{7,6},{8,15},{9,8},{10,9... | collective-permute-start | bytes 147464 | tf_op jit(solution)/shard_map/ppermute | solution.py:11
  10.6 25.5 %collective-permute-start.7 = (bf16[384,256]{1,0:T(8,128)(2,1)}, bf16[384,256]{1,0:T(8,128)(2,1)}, u32[]{:S(2)}, u32[]{:S(2)}) collective-permute-start(bf16[384,256]{1,0:T(8,128)(2,1)} %get-tuple-element.17), channel_id=1, source_target_pairs={{0,480},{32,0},{64,32},{96,64},{128,96},{160,128},{192,160},{224,1... | collective-permute-start | bytes 589832 | tf_op jit(solution)/shard_map/ppermute | solution.py:11
  22.0 19.3 %collective-permute-start.14 = (bf16[384,256]{1,0:T(8,128)(2,1)}, bf16[384,256]{1,0:T(8,128)(2,1)}, u32[]{:S(2)}, u32[]{:S(2)}) collective-permute-start(bf16[384,256]{1,0:T(8,128)(2,1)} %get-tuple-element.17), channel_id=1, source_target_pairs={{0,32},{32,64},{64,96},{96,128},{128,160},{160,192},{192,224},{224... | collective-permute-start | bytes 589832 | tf_op jit(solution)/shard_map/ppermute | solution.py:11
  36.1 10.1 %collective-permute-start.8 = (bf16[384,256]{1,0:T(8,128)(2,1)}, bf16[384,256]{1,0:T(8,128)(2,1)S(1)}, u32[]{:S(2)}, u32[]{:S(2)}) collective-permute-start(bf16[384,256]{1,0:T(8,128)(2,1)} %collective-permute-done.7), channel_id=1, source_target_pairs={{0,480},{32,0},{64,32},{96,64},{128,96},{160,128},{192,160},{224,1... | collective-permute-start | bytes 589832 | tf_op jit(solution)/shard_map/ppermute | solution.py:11
  41.3 10.7 %collective-permute-start.15 = (bf16[384,256]{1,0:T(8,128)(2,1)}, bf16[384,256]{1,0:T(8,128)(2,1)S(1)}, u32[]{:S(2)}, u32[]{:S(2)}) collective-permute-start(bf16[384,256]{1,0:T(8,128)(2,1)} %collective-permute-done.14), channel_id=1, source_target_pairs={{0,32},{32,64},{64,96},{96,128},{128,160},{160,192},{192,224},{224... | collective-permute-start | bytes 589832 | tf_op jit(solution)/shard_map/ppermute | solution.py:11
  46.2 10.2 %collective-permute-start.9 = (bf16[384,256]{1,0:T(8,128)(2,1)S(1)}, bf16[384,256]{1,0:T(8,128)(2,1)S(1)}, u32[]{:S(2)}, u32[]{:S(2)}) collective-permute-start(bf16[384,256]{1,0:T(8,128)(2,1)S(1)} %collective-permute-done.8), channel_id=1, source_target_pairs={{0,480},{32,0},{64,32},{96,64},{128,96},{160,128},{192,160},{224,1... | collective-permute-start | bytes 589832 | tf_op jit(solution)/shard_map/ppermute | solution.py:11
  52.0 10.1 %collective-permute-start.16 = (bf16[384,256]{1,0:T(8,128)(2,1)S(1)}, bf16[384,256]{1,0:T(8,128)(2,1)S(1)}, u32[]{:S(2)}, u32[]{:S(2)}) collective-permute-start(bf16[384,256]{1,0:T(8,128)(2,1)S(1)} %collective-permute-done.15), channel_id=1, source_target_pairs={{0,32},{32,64},{64,96},{96,128},{128,160},{160,192},{192,224},{224... | collective-permute-start | bytes 589832 | tf_op jit(solution)/shard_map/ppermute | solution.py:11
  56.5 17.9 %collective-permute-start.10 = (bf16[384,256]{1,0:T(8,128)(2,1)S(1)}, bf16[384,256]{1,0:T(8,128)(2,1)S(1)}, u32[]{:S(2)}, u32[]{:S(2)}) collective-permute-start(bf16[384,256]{1,0:T(8,128)(2,1)S(1)} %collective-permute-done.9), channel_id=1, source_target_pairs={{0,480},{32,0},{64,32},{96,64},{128,96},{160,128},{192,160},{224,1... | collective-permute-start | bytes 589832 | tf_op jit(solution)/shard_map/ppermute | solution.py:11
  62.1 9.2 %collective-permute-start.17 = (bf16[384,256]{1,0:T(8,128)(2,1)S(1)}, bf16[384,256]{1,0:T(8,128)(2,1)S(1)}, u32[]{:S(2)}, u32[]{:S(2)}) collective-permute-start(bf16[384,256]{1,0:T(8,128)(2,1)S(1)} %collective-permute-done.16), channel_id=1, source_target_pairs={{0,32},{32,64},{64,96},{96,128},{128,160},{160,192},{192,224},{224... | collective-permute-start | bytes 589832 | tf_op jit(solution)/shard_map/ppermute | solution.py:11
  71.3 9.2 %collective-permute-start.18 = (bf16[384,256]{1,0:T(8,128)(2,1)S(1)}, bf16[384,256]{1,0:T(8,128)(2,1)S(1)}, u32[]{:S(2)}, u32[]{:S(2)}) collective-permute-start(bf16[384,256]{1,0:T(8,128)(2,1)S(1)} %collective-permute-done.17), channel_id=1, source_target_pairs={{0,32},{32,64},{64,96},{96,128},{128,160},{160,192},{192,224},{224... | collective-permute-start | bytes 589832 | tf_op jit(solution)/shard_map/ppermute | solution.py:11
  74.4 8.3 %collective-permute-start.11 = (bf16[384,256]{1,0:T(8,128)(2,1)S(1)}, bf16[384,256]{1,0:T(8,128)(2,1)S(1)}, u32[]{:S(2)}, u32[]{:S(2)}) collective-permute-start(bf16[384,256]{1,0:T(8,128)(2,1)S(1)} %collective-permute-done.10), channel_id=1, source_target_pairs={{0,480},{32,0},{64,32},{96,64},{128,96},{160,128},{192,160},{224,1... | collective-permute-start | bytes 589832 | tf_op jit(solution)/shard_map/ppermute | solution.py:11
  80.5 8.8 %collective-permute-start.19 = (bf16[384,256]{1,0:T(8,128)(2,1)S(1)}, bf16[384,256]{1,0:T(8,128)(2,1)S(1)}, u32[]{:S(2)}, u32[]{:S(2)}) collective-permute-start(bf16[384,256]{1,0:T(8,128)(2,1)S(1)} %collective-permute-done.18), channel_id=1, source_target_pairs={{0,32},{32,64},{64,96},{96,128},{128,160},{160,192},{192,224},{224... | collective-permute-start | bytes 589832 | tf_op jit(solution)/shard_map/ppermute | solution.py:11
  82.7 8.8 %collective-permute-start.12 = (bf16[384,256]{1,0:T(8,128)(2,1)S(1)}, bf16[384,256]{1,0:T(8,128)(2,1)S(1)}, u32[]{:S(2)}, u32[]{:S(2)}) collective-permute-start(bf16[384,256]{1,0:T(8,128)(2,1)S(1)} %collective-permute-done.11), channel_id=1, source_target_pairs={{0,480},{32,0},{64,32},{96,64},{128,96},{160,128},{192,160},{224,1... | collective-permute-start | bytes 589832 | tf_op jit(solution)/shard_map/ppermute | solution.py:11
  89.3 8.8 %collective-permute-start.20 = (bf16[384,256]{1,0:T(8,128)(2,1)S(1)}, bf16[384,256]{1,0:T(8,128)(2,1)S(1)}, u32[]{:S(2)}, u32[]{:S(2)}) collective-permute-start(bf16[384,256]{1,0:T(8,128)(2,1)S(1)} %collective-permute-done.19), channel_id=1, source_target_pairs={{0,32},{32,64},{64,96},{96,128},{128,160},{160,192},{192,224},{224... | collective-permute-start | bytes 589832 | tf_op jit(solution)/shard_map/ppermute | solution.py:11
  91.5 8.8 %collective-permute-start.13 = (bf16[384,256]{1,0:T(8,128)(2,1)S(1)}, bf16[384,256]{1,0:T(8,128)(2,1)S(1)}, u32[]{:S(2)}, u32[]{:S(2)}) collective-permute-start(bf16[384,256]{1,0:T(8,128)(2,1)S(1)} %collective-permute-done.12), channel_id=1, source_target_pairs={{0,480},{32,0},{64,32},{96,64},{128,96},{160,128},{192,160},{224,1... | collective-permute-start | bytes 589832 | tf_op jit(solution)/shard_map/ppermute | solution.py:11
  98.1 8.8 %collective-permute-start.21 = (bf16[384,256]{1,0:T(8,128)(2,1)S(1)}, bf16[384,256]{1,0:T(8,128)(2,1)S(1)}, u32[]{:S(2)}, u32[]{:S(2)}) collective-permute-start(bf16[384,256]{1,0:T(8,128)(2,1)S(1)} %collective-permute-done.20), channel_id=1, source_target_pairs={{0,32},{32,64},{64,96},{96,128},{128,160},{160,192},{192,224},{224... | collective-permute-start | bytes 589832 | tf_op jit(solution)/shard_map/ppermute | solution.py:11
  133.0 11.3 %collective-permute-start.22 = (bf16[48,3584]{1,0:T(8,128)(2,1)S(1)}, bf16[48,3584]{1,0:T(8,128)(2,1)S(1)}, u32[]{:S(2)}, u32[]{:S(2)}) collective-permute-start(bf16[48,3584]{1,0:T(8,128)(2,1)S(1)} %get-tuple-element.7), channel_id=1, source_target_pairs={{0,8},{8,16},{16,24},{24,0},{1,9},{9,17},{17,25},{25,1},{2,10},{10... | collective-permute-start | bytes 1032200 | tf_op jit(solution)/shard_map/ppermute | solution.py:11
  136.5 12.4 %collective-permute-start.24 = (bf16[48,3584]{1,0:T(8,128)(2,1)S(1)}, bf16[48,3584]{1,0:T(8,128)(2,1)S(1)}, u32[]{:S(2)}, u32[]{:S(2)}) collective-permute-start(bf16[48,3584]{1,0:T(8,128)(2,1)S(1)} %get-tuple-element.8), channel_id=1, source_target_pairs={{0,24},{8,0},{16,8},{24,16},{1,25},{9,1},{17,9},{25,17},{2,26},{10... | collective-permute-start | bytes 1032200 | tf_op jit(solution)/shard_map/ppermute | solution.py:11
  144.4 10.8 %collective-permute-start.23 = (bf16[48,3584]{1,0:T(8,128)(2,1)S(1)}, bf16[48,3584]{1,0:T(8,128)(2,1)}, u32[]{:S(2)}, u32[]{:S(2)}) collective-permute-start(bf16[48,3584]{1,0:T(8,128)(2,1)S(1)} %fusion.27), channel_id=1, source_target_pairs={{0,8},{8,16},{16,24},{24,0},{1,9},{9,17},{17,25},{25,1},{2,10},{10... | collective-permute-start | bytes 1032200 | tf_op jit(solution)/shard_map/ppermute | solution.py:11
  156.9 12.0 %collective-permute-start.26 = (bf16[48,3584]{1,0:T(8,128)(2,1)S(1)}, bf16[48,3584]{1,0:T(8,128)(2,1)S(1)}, u32[]{:S(2)}, u32[]{:S(2)}) collective-permute-start(bf16[48,3584]{1,0:T(8,128)(2,1)S(1)} %bitcast.129), channel_id=1, source_target_pairs={{0,8},{8,16},{16,24},{24,0},{1,9},{9,17},{17,25},{25,1},{2,10},{10... | collective-permute-start | bytes 1032200 | tf_op jit(solution)/shard_map/ppermute | solution.py:11
  160.5 12.1 %collective-permute-start.25 = (bf16[48,3584]{1,0:T(8,128)(2,1)S(1)}, bf16[48,3584]{1,0:T(8,128)(2,1)S(1)}, u32[]{:S(2)}, u32[]{:S(2)}) collective-permute-start(bf16[48,3584]{1,0:T(8,128)(2,1)S(1)} %bitcast.130), channel_id=1, source_target_pairs={{0,24},{8,0},{16,8},{24,16},{1,25},{9,1},{17,9},{25,17},{2,26},{10... | collective-permute-start | bytes 1032200 | tf_op jit(solution)/shard_map/ppermute | solution.py:11
  168.9 9.1 %collective-permute-start.27 = (bf16[48,3584]{1,0:T(8,128)(2,1)S(1)}, bf16[48,3584]{1,0:T(8,128)(2,1)S(1)}, u32[]{:S(2)}, u32[]{:S(2)}) collective-permute-start(bf16[48,3584]{1,0:T(8,128)(2,1)S(1)} %collective-permute-done.26), channel_id=1, source_target_pairs={{0,8},{8,16},{16,24},{24,0},{1,9},{9,17},{17,25},{25,1},{2,10},{10... | collective-permute-start | bytes 1032200 | tf_op jit(solution)/shard_map/ppermute | solution.py:11
  (14 other events, 64.1 us)
Sparse Core Ops, SparseCore 0:
  213.9 76.0 reduce-scatter.1

commit v3 on v2

--- a/solution.py
+++ b/solution.py
@@ -65,8 +65,7 @@
 
     pair_local = jnp.concatenate([gate_slots[0, 0], up_slots[0, 0]], axis=2)
     pair_local = pair_local.reshape(per_dev * bs, 2 * bs)
-    pair_rel = jnp.concatenate(ring_gather(pair_local, "dp", n_dp), axis=0)
-    pair_rel = pair_rel.reshape(cap, bs, 2 * bs)
+    pair_all = lax.all_gather(pair_local, "dp", axis=0, tiled=True).reshape(cap, bs, 2 * bs)
 
     x_rel = jnp.stack(ring_gather(layer_input, "col", n_col))
     x_abs = jnp.roll(x_rel, k_col, axis=0).reshape(tok, feat)
@@ -77,11 +76,13 @@
     kept = tile_mask > 0
     position = jnp.cumsum(kept.astype(jnp.int32)) - 1
     q = jnp.arange(cap, dtype=jnp.int32)
-    slot_rel = ((k_dp + q // per_dev) % n_dp) * per_dev + q % per_dev
-    onehot_rel = (kept[None, :] & (position[None, :] == slot_rel[:, None])).astype(BF16)
-    onehot_abs = (kept[None, :] & (position[None, :] == q[:, None])).astype(BF16)
+    picks = kept[None, :] & (position[None, :] == q[:, None])
+    onehot = picks.astype(BF16)
+    onehot3 = onehot.reshape(cap, tile_rows, tile_cols)
+    row_pick = jnp.sum(onehot3, axis=2)
+    col_pick = jnp.sum(onehot3, axis=1)
 
-    dense = jnp.einsum("qb,qkn->bkn", onehot_rel, pair_rel, preferred_element_type=F32).astype(BF16)
+    dense = jnp.einsum("qb,qkn->bkn", onehot, pair_all, preferred_element_type=F32).astype(BF16)
     wd = dense.reshape(tile_rows, tile_cols, bs, 2 * bs).transpose(0, 2, 1, 3)
     wd = wd.reshape(feat, tile_cols * 2 * bs)
 
@@ -105,12 +106,13 @@
     dx_roll = jnp.roll(dx.reshape(n_col, cols_per, feat), -k_col, axis=0)
     input_grad = ring_sum_scatter([dx_roll[m] for m in range(n_col)], "col", n_col).astype(BF16)
 
-    dw = lax.dot_general(
-        x_abs, grad_abs, (((0,), (0,)), ((), ())), preferred_element_type=F32
+    x_pick = jnp.einsum(
+        "qr,trk->qtk", row_pick, x_abs.reshape(tok, tile_rows, bs), preferred_element_type=F32
     ).astype(BF16)
-    dw_blocks = dw.reshape(tile_rows, bs, tile_cols, 2 * bs).transpose(0, 2, 1, 3)
-    dw_blocks = dw_blocks.reshape(tile_rows * tile_cols, bs, 2 * bs)
-    slot_dw = jnp.einsum("qb,bkn->qkn", onehot_abs, dw_blocks, preferred_element_type=F32).astype(BF16)
+    g_pick = jnp.einsum(
+        "qc,tcn->qtn", col_pick, grad_abs.reshape(tok, tile_cols, 2 * bs), preferred_element_type=F32
+    ).astype(BF16)
+    slot_dw = jnp.einsum("qtk,qtn->qkn", x_pick, g_pick, preferred_element_type=F32).astype(BF16)
     dw_sum = lax.psum_scatter(
         slot_dw.reshape(cap * bs, 2 * bs), "dp", scatter_dimension=0, tiled=True
     ).astype(F32) / n_dp

time: 300 us -> 263 us (0.88)
  the two profiles are of different devices: /device:TPU:10 before, /device:TPU:8 now
where the time goes in v3:
time: 263 us; the launch traced here: 262 us
  waiting for transfers between devices  155 us (59%)
  starting transfers between devices  33.7 us (13%)
  local copies, waits for them, and re-layouts  26.2 us (10%)
  matrix products  21.7 us (8%)
  between operations  14.4 us (5%)
  other arithmetic  10.6 us (4%)
    all_gather x1, waiting for transfers between devices, on_device(): lax.all_gather(pair_local, 'dp', axis=0, tiled=True)  59.9 us
    ppermute x20, waiting for transfers between devices, _shift(): return lax.ppermute(x, axis, perm=[(i, (i + step) % n) for i in range(n)])  49.6 us
    reduce_scatter x1, waiting for transfers between devices, on_device(): lax.psum_scatter(slot_dw.reshape(cap * bs, 2 * bs), 'dp', scatter_dimensi...  45.7 us
    ppermute x20, starting transfers between devices, _shift(): return lax.ppermute(x, axis, perm=[(i, (i + step) % n) for i in range(n)])  33.6 us
    transpose x1, local copies, waits for them, and re-layouts, on_device(): wd = dense.reshape(tile_rows, tile_cols, bs, 2 * bs).transpose(0, 2, 1, 3)  10.9 us
    convert_element_type x1, local copies, waits for them, and re-layouts, on_device(): jnp.einsum('qb,qkn->bkn', onehot, pair_all, preferred_element_type=F32)  5.68 us
    dot_general x1, matrix products, on_device(): pre = jnp.dot(x_abs, wd, preferred_element_type=F32).astype(BF16)  5.64 us
  transfers between devices with their start and end apart: 22, of which 14 were waited for; matrix products, arithmetic and copies ran while one was open for 4% of the time, Pallas kernels for 0%

profile of v3, /device:TPU:8, one launch (start us, length us, event | category | flops | bytes accessed | tf_op | source)
XLA Modules:
  0.0 261.8 jit_solution(11555577868764550067)
XLA Ops:
  17.9 3.0 %collective-permute-start.2 = (bf16[24,1024]{1,0:T(8,128)(2,1)S(1)}, bf16[24,1024]{1,0:T(8,128)(2,1)S(1)}, u32[]{:S(2)}, u32[]{:S(2)}) collective-permute-start(bf16[24,1024]{1,0:T(8,128)(2,1)S(1)} %collective-permute-done.1), channel_id=1, source_target_pairs={{0,7},{1,0},{2,1},{3,2},{4,3},{5,4},{6,5},{7,6},{8,15},{9,8},{10,9... | collective-permute-start | bytes 147464 | tf_op jit(solution)/shard_map/ppermute | solution.py:11
  20.9 4.7 %collective-permute-done.5 = bf16[24,1024]{1,0:T(8,128)(2,1)S(1)} collective-permute-done((bf16[24,1024]{1,0:T(8,128)(2,1)S(1)}, bf16[24,1024]{1,0:T(8,128)(2,1)S(1)}, u32[]{:S(2)}, u32[]{:S(2)}) %collective-permute-start.5) | collective-permute-done | bytes 49184 | tf_op jit(solution)/shard_map/ppermute | solution.py:11
  25.7 4.7 %collective-permute-done.6 = bf16[24,1024]{1,0:T(8,128)(2,1)S(1)} collective-permute-done((bf16[24,1024]{1,0:T(8,128)(2,1)S(1)}, bf16[24,1024]{1,0:T(8,128)(2,1)S(1)}, u32[]{:S(2)}, u32[]{:S(2)}) %collective-permute-start.6) | collective-permute-done | bytes 49184 | tf_op jit(solution)/shard_map/ppermute | solution.py:11
  30.6 59.9 %all-gather.2.cloned.1.call-done = bf16[6144,256]{1,0:T(8,128)(2,1)} async-done(((bf16[384,256]{1,0:T(8,128)(2,1)}), bf16[6144,256]{1,0:T(8,128)(2,1)}) %all-gather.2.cloned.1.call-update) | async-done | bytes 3145744 | tf_op jit(solution)/shard_map/all_gather | solution.py:68
  90.5 4.2 %convolution_convert_fusion = bf16[112,128,256]{2,0,1:T(8,128)(2,1)S(1)} fusion(bf16[48,128,256]{2,1,0:T(8,128)(2,1)} %bitcast.122, s32[112]{0:T(128)S(1)} %get-tuple-element.20, pred[112]{0:T(512)(128)(4,1)S(1)} %gt.25), kind=kOutput, calls=%fused_computation.4 | convolution fusion | flops 356002304 | bytes 10486320 | tf_op jit(solution)/shard_map/qb,qkn->bkn/dot_general | solution.py:85
  94.7 5.7 %copy.12 = bf16[112,128,256]{2,1,0:T(8,128)(2,1)} copy(bf16[112,128,256]{2,0,1:T(8,128)(2,1)S(1)} %convolution_convert_fusion) | data formatting | bytes 14680064 | tf_op jit(solution)/shard_map/convert_element_type | solution.py:85
  100.3 10.9 %copy.13 = bf16[8,128,14,256]{1,0,3,2:T(8,128)(2,1)} copy(bf16[8,128,14,256]{3,1,2,0:T(8,128)(2,1)} %bitcast.116) | data formatting | bytes 14680064 | tf_op jit(solution)/shard_map/transpose | solution.py:86
  111.3 5.6 %fusion.6 = bf16[192,3584]{1,0:T(8,128)(2,1)S(1)} fusion(bf16[192,1024]{1,0:T(8,128)(2,1)S(1)} %bitcast.125, bf16[448,8,8,128]{3,2,1,0:T(8,128)(2,1)} %bitcast.118), kind=kOutput, calls=%fused_computation.7 | convolution fusion | flops 1409974272 | bytes 9109504 | tf_op jit(solution)/shard_map/dot_general | solution.py:89
  117.5 3.4 %collective-permute-start.7 = (bf16[48,3584]{1,0:T(8,128)(2,1)S(1)}, bf16[48,3584]{1,0:T(8,128)(2,1)S(1)}, u32[]{:S(2)}, u32[]{:S(2)}) collective-permute-start(bf16[48,3584]{1,0:T(8,128)(2,1)S(1)} %get-tuple-element.9), channel_id=1, source_target_pairs={{0,8},{8,16},{16,24},{24,0},{1,9},{9,17},{17,25},{25,1},{2,10},{10... | collective-permute-start | bytes 1032200 | tf_op jit(solution)/shard_map/ppermute | solution.py:11
  123.4 5.1 %collective-permute-done.7 = bf16[48,3584]{1,0:T(8,128)(2,1)S(1)} collective-permute-done((bf16[48,3584]{1,0:T(8,128)(2,1)S(1)}, bf16[48,3584]{1,0:T(8,128)(2,1)S(1)}, u32[]{:S(2)}, u32[]{:S(2)}) %collective-permute-start.7) | collective-permute-done | bytes 344096 | tf_op jit(solution)/shard_map/ppermute | solution.py:11
  128.5 3.3 %collective-permute-start.8 = (bf16[48,3584]{1,0:T(8,128)(2,1)S(1)}, bf16[48,3584]{1,0:T(8,128)(2,1)}, u32[]{:S(2)}, u32[]{:S(2)}) collective-permute-start(bf16[48,3584]{1,0:T(8,128)(2,1)S(1)} %fusion.30), channel_id=1, source_target_pairs={{0,8},{8,16},{16,24},{24,0},{1,9},{9,17},{17,25},{25,1},{2,10},{10... | collective-permute-start | bytes 1032200 | tf_op jit(solution)/shard_map/ppermute | solution.py:11
  132.9 8.2 %collective-permute-done.8 = bf16[48,3584]{1,0:T(8,128)(2,1)} collective-permute-done((bf16[48,3584]{1,0:T(8,128)(2,1)S(1)}, bf16[48,3584]{1,0:T(8,128)(2,1)}, u32[]{:S(2)}, u32[]{:S(2)}) %collective-permute-start.8) | collective-permute-done | bytes 344096 | tf_op jit(solution)/shard_map/ppermute | solution.py:11
  143.6 3.3 %collective-permute-start.11 = (bf16[48,3584]{1,0:T(8,128)(2,1)}, bf16[48,3584]{1,0:T(8,128)(2,1)S(1)}, u32[]{:S(2)}, u32[]{:S(2)}) collective-permute-start(bf16[48,3584]{1,0:T(8,128)(2,1)} %bitcast.55), channel_id=1, source_target_pairs={{0,8},{8,16},{16,24},{24,0},{1,9},{9,17},{17,25},{25,1},{2,10},{10... | collective-permute-start | bytes 1032200 | tf_op jit(solution)/shard_map/ppermute | solution.py:11
  147.2 4.0 %collective-permute-start.10 = (bf16[48,3584]{1,0:T(8,128)(2,1)}, bf16[48,3584]{1,0:T(8,128)(2,1)}, u32[]{:S(2)}, u32[]{:S(2)}) collective-permute-start(bf16[48,3584]{1,0:T(8,128)(2,1)} %bitcast.55), channel_id=1, source_target_pairs={{0,24},{8,0},{16,8},{24,16},{1,25},{9,1},{17,9},{25,17},{2,26},{10... | collective-permute-start | bytes 1032200 | tf_op jit(solution)/shard_map/ppermute | solution.py:11
  151.2 4.3 %collective-permute-done.11 = bf16[48,3584]{1,0:T(8,128)(2,1)S(1)} collective-permute-done((bf16[48,3584]{1,0:T(8,128)(2,1)}, bf16[48,3584]{1,0:T(8,128)(2,1)S(1)}, u32[]{:S(2)}, u32[]{:S(2)}) %collective-permute-start.11) | collective-permute-done | bytes 344096 | tf_op jit(solution)/shard_map/ppermute | solution.py:11
  158.8 6.8 %collective-permute-done.12 = bf16[48,3584]{1,0:T(8,128)(2,1)} collective-permute-done((bf16[48,3584]{1,0:T(8,128)(2,1)S(1)}, bf16[48,3584]{1,0:T(8,128)(2,1)}, u32[]{:S(2)}, u32[]{:S(2)}) %collective-permute-start.12) | collective-permute-done | bytes 344096 | tf_op jit(solution)/shard_map/ppermute | solution.py:11
  165.6 3.8 %fusion.21 = bf16[4,48,3584]{2,1,0:T(8,128)(2,1)} fusion(s32[]{:T(128)S(6)} %select_n.34, bf16[1,48,3584]{2,1,0:T(8,128)(2,1)S(1)} %stack_reshape.3, bf16[1,48,3584]{2,1,0:T(8,128)(2,1)} %bitcast.21, bf16[1,48,3584]{2,1,0:T(8,128)(2,1)} %bitcast.22, bf16[1,48,3584]{2,1,0:T(8,128)(2,1)S(1)} %bitcast.129), kind=kLoop, calls=%fused_computation.28 | loop fusion | flops 4816896 | bytes 2752516 | tf_op jit(solution)/shard_map/jit(_roll_dynamic)/concatenate | solution.py:101
  169.4 3.7 %reshape_reshape.7 = bf16[192,14,256]{2,1,0:T(8,128)(2,1)} reshape(bf16[4,48,3584]{2,1,0:T(8,128)(2,1)} %fusion.21) | data formatting | bytes 2752512 | tf_op jit(solution)/shard_map/reshape;reshape | solution.py:113
  176.0 3.6 %fusion.13 = bf16[48,128,256]{2,1,0:T(8,128)(2,1)} fusion(bf16[48,192,256]{2,0,1:T(8,128)(2,1)S(1)} %convolution_convert_fusion.1, bf16[48,192,128]{2,0,1:T(8,128)(2,1)S(1)} %convolution_convert_fusion.2), kind=kOutput, calls=%fused_computation.23 | convolution fusion | flops 605552640 | bytes 10223616 | tf_op jit(solution)/shard_map/qtk,qtn->qkn/dot_general | solution.py:115
  180.9 4.7 %fusion.26 = bf16[192,1024]{1,0:T(8,128)(2,1)S(1)} fusion(bf16[192,3584]{1,0:T(8,128)(2,1)S(1)} %bitcast.120, bf16[448,8,8,128]{3,2,1,0:T(8,128)(2,1)} %bitcast.119), kind=kOutput, calls=%fused_computation.33 | convolution fusion | flops 1409482752 | bytes 9109504 | tf_op jit(solution)/shard_map/dot_general | solution.py:103
  185.8 4.7 %collective-permute-done.13 = bf16[24,1024]{1,0:T(8,128)(2,1)S(1)} collective-permute-done((bf16[24,1024]{1,0:T(8,128)(2,1)S(1)}, bf16[24,1024]{1,0:T(8,128)(2,1)S(1)}, u32[]{:S(2)}, u32[]{:S(2)}) %collective-permute-start.13) | collective-permute-done | bytes 49184 | tf_op jit(solution)/shard_map/ppermute | solution.py:11
  195.3 4.7 %collective-permute-done.15 = bf16[24,1024]{1,0:T(8,128)(2,1)S(1)} collective-permute-done((bf16[24,1024]{1,0:T(8,128)(2,1)S(1)}, bf16[24,1024]{1,0:T(8,128)(2,1)S(1)}, u32[]{:S(2)}, u32[]{:S(2)}) %collective-permute-start.15) | collective-permute-done | bytes 49184 | tf_op jit(solution)/shard_map/ppermute | solution.py:11
  201.8 3.4 %collective-permute-start.19 = (bf16[24,1024]{1,0:T(8,128)(2,1)S(1)}, bf16[24,1024]{1,0:T(8,128)(2,1)S(1)}, u32[]{:S(2)}, u32[]{:S(2)}) collective-permute-start(bf16[24,1024]{1,0:T(8,128)(2,1)S(1)} %fusion.36), channel_id=1, source_target_pairs={{0,7},{1,0},{2,1},{3,2},{4,3},{5,4},{6,5},{7,6},{8,15},{9,8},{10,9... | collective-permute-start | bytes 147464 | tf_op jit(solution)/shard_map/ppermute | solution.py:11
  207.6 45.7 %reduce-scatter.2.cloned.1.call-done = bf16[384,256]{1,0:T(8,128)(2,1)} async-done(((bf16[6144,256]{1,0:T(8,128)(2,1)}), bf16[384,256]{1,0:T(8,128)(2,1)}) %reduce-scatter.2.cloned.1.call-update) | async-done | bytes 196624 | tf_op jit(solution)/shard_map/reduce_scatter | solution.py:116
  (73 shorter events, 36.1 us)
Async XLA Ops:
  7.2 83.3 %all-gather.2.cloned.1.call-start = ((), (), s32[]{:S(2)}) async-start(), calls=%async_computation.1 | async-start | bytes 3342336 | tf_op jit(solution)/shard_map/all_gather | solution.py:68
  8.9 244.4 %reduce-scatter.2.cloned.1.call-start = ((), (), s32[]{:S(2)}) async-start(), calls=%async_computation.2 | async-start | bytes 3342336 | tf_op jit(solution)/shard_map/reduce_scatter | solution.py:116
  8.9 4.3 %collective-permute-start = (bf16[24,1024]{1,0:T(8,128)(2,1)}, bf16[24,1024]{1,0:T(8,128)(2,1)S(1)}, u32[]{:S(2)}, u32[]{:S(2)}) collective-permute-start(bf16[24,1024]{1,0:T(8,128)(2,1)} %param.9), channel_id=1, source_target_pairs={{0,7},{1,0},{2,1},{3,2},{4,3},{5,4},{6,5},{7,6},{8,15},{9,8},{10,9... | collective-permute-start | bytes 147464 | tf_op jit(solution)/shard_map/ppermute | solution.py:11
  11.1 5.0 %collective-permute-start.3 = (bf16[24,1024]{1,0:T(8,128)(2,1)}, bf16[24,1024]{1,0:T(8,128)(2,1)S(1)}, u32[]{:S(2)}, u32[]{:S(2)}) collective-permute-start(bf16[24,1024]{1,0:T(8,128)(2,1)} %param.9), channel_id=1, source_target_pairs={{0,1},{1,2},{2,3},{3,4},{4,5},{5,6},{6,7},{7,0},{8,9},{9,10},{10,1... | collective-permute-start | bytes 147464 | tf_op jit(solution)/shard_map/ppermute | solution.py:11
  13.2 4.7 %collective-permute-start.1 = (bf16[24,1024]{1,0:T(8,128)(2,1)S(1)}, bf16[24,1024]{1,0:T(8,128)(2,1)S(1)}, u32[]{:S(2)}, u32[]{:S(2)}) collective-permute-start(bf16[24,1024]{1,0:T(8,128)(2,1)S(1)} %collective-permute-done), channel_id=1, source_target_pairs={{0,7},{1,0},{2,1},{3,2},{4,3},{5,4},{6,5},{7,6},{8,15},{9,8},{10,9... | collective-permute-start | bytes 147464 | tf_op jit(solution)/shard_map/ppermute | solution.py:11
  16.2 4.7 %collective-permute-start.4 = (bf16[24,1024]{1,0:T(8,128)(2,1)S(1)}, bf16[24,1024]{1,0:T(8,128)(2,1)S(1)}, u32[]{:S(2)}, u32[]{:S(2)}) collective-permute-start(bf16[24,1024]{1,0:T(8,128)(2,1)S(1)} %collective-permute-done.3), channel_id=1, source_target_pairs={{0,1},{1,2},{2,3},{3,4},{4,5},{5,6},{6,7},{7,0},{8,9},{9,10},{10,1... | collective-permute-start | bytes 147464 | tf_op jit(solution)/shard_map/ppermute | solution.py:11
  17.9 7.7 %collective-permute-start.2 = (bf16[24,1024]{1,0:T(8,128)(2,1)S(1)}, bf16[24,1024]{1,0:T(8,128)(2,1)S(1)}, u32[]{:S(2)}, u32[]{:S(2)}) collective-permute-start(bf16[24,1024]{1,0:T(8,128)(2,1)S(1)} %collective-permute-done.1), channel_id=1, source_target_pairs={{0,7},{1,0},{2,1},{3,2},{4,3},{5,4},{6,5},{7,6},{8,15},{9,8},{10,9... | collective-permute-start | bytes 147464 | tf_op jit(solution)/shard_map/ppermute | solution.py:11
  20.9 4.7 %collective-permute-start.5 = (bf16[24,1024]{1,0:T(8,128)(2,1)S(1)}, bf16[24,1024]{1,0:T(8,128)(2,1)S(1)}, u32[]{:S(2)}, u32[]{:S(2)}) collective-permute-start(bf16[24,1024]{1,0:T(8,128)(2,1)S(1)} %collective-permute-done.4), channel_id=1, source_target_pairs={{0,1},{1,2},{2,3},{3,4},{4,5},{5,6},{6,7},{7,0},{8,9},{9,10},{10,1... | collective-permute-start | bytes 147464 | tf_op jit(solution)/shard_map/ppermute | solution.py:11
  25.6 4.7 %collective-permute-start.6 = (bf16[24,1024]{1,0:T(8,128)(2,1)S(1)}, bf16[24,1024]{1,0:T(8,128)(2,1)S(1)}, u32[]{:S(2)}, u32[]{:S(2)}) collective-permute-start(bf16[24,1024]{1,0:T(8,128)(2,1)S(1)} %collective-permute-done.5), channel_id=1, source_target_pairs={{0,1},{1,2},{2,3},{3,4},{4,5},{5,6},{6,7},{7,0},{8,9},{9,10},{10,1... | collective-permute-start | bytes 147464 | tf_op jit(solution)/shard_map/ppermute | solution.py:11
  117.5 10.9 %collective-permute-start.7 = (bf16[48,3584]{1,0:T(8,128)(2,1)S(1)}, bf16[48,3584]{1,0:T(8,128)(2,1)S(1)}, u32[]{:S(2)}, u32[]{:S(2)}) collective-permute-start(bf16[48,3584]{1,0:T(8,128)(2,1)S(1)} %get-tuple-element.9), channel_id=1, source_target_pairs={{0,8},{8,16},{16,24},{24,0},{1,9},{9,17},{17,25},{25,1},{2,10},{10... | collective-permute-start | bytes 1032200 | tf_op jit(solution)/shard_map/ppermute | solution.py:11
  120.9 11.9 %collective-permute-start.9 = (bf16[48,3584]{1,0:T(8,128)(2,1)S(1)}, bf16[48,3584]{1,0:T(8,128)(2,1)S(1)}, u32[]{:S(2)}, u32[]{:S(2)}) collective-permute-start(bf16[48,3584]{1,0:T(8,128)(2,1)S(1)} %get-tuple-element.10), channel_id=1, source_target_pairs={{0,24},{8,0},{16,8},{24,16},{1,25},{9,1},{17,9},{25,17},{2,26},{10... | collective-permute-start | bytes 1032200 | tf_op jit(solution)/shard_map/ppermute | solution.py:11
  128.5 12.6 %collective-permute-start.8 = (bf16[48,3584]{1,0:T(8,128)(2,1)S(1)}, bf16[48,3584]{1,0:T(8,128)(2,1)}, u32[]{:S(2)}, u32[]{:S(2)}) collective-permute-start(bf16[48,3584]{1,0:T(8,128)(2,1)S(1)} %fusion.30), channel_id=1, source_target_pairs={{0,8},{8,16},{16,24},{24,0},{1,9},{9,17},{17,25},{25,1},{2,10},{10... | collective-permute-start | bytes 1032200 | tf_op jit(solution)/shard_map/ppermute | solution.py:11
  143.6 11.9 %collective-permute-start.11 = (bf16[48,3584]{1,0:T(8,128)(2,1)}, bf16[48,3584]{1,0:T(8,128)(2,1)S(1)}, u32[]{:S(2)}, u32[]{:S(2)}) collective-permute-start(bf16[48,3584]{1,0:T(8,128)(2,1)} %bitcast.55), channel_id=1, source_target_pairs={{0,8},{8,16},{16,24},{24,0},{1,9},{9,17},{17,25},{25,1},{2,10},{10... | collective-permute-start | bytes 1032200 | tf_op jit(solution)/shard_map/ppermute | solution.py:11
  147.2 11.6 %collective-permute-start.10 = (bf16[48,3584]{1,0:T(8,128)(2,1)}, bf16[48,3584]{1,0:T(8,128)(2,1)}, u32[]{:S(2)}, u32[]{:S(2)}) collective-permute-start(bf16[48,3584]{1,0:T(8,128)(2,1)} %bitcast.55), channel_id=1, source_target_pairs={{0,24},{8,0},{16,8},{24,16},{1,25},{9,1},{17,9},{25,17},{2,26},{10... | collective-permute-start | bytes 1032200 | tf_op jit(solution)/shard_map/ppermute | solution.py:11
  155.4 10.2 %collective-permute-start.12 = (bf16[48,3584]{1,0:T(8,128)(2,1)S(1)}, bf16[48,3584]{1,0:T(8,128)(2,1)}, u32[]{:S(2)}, u32[]{:S(2)}) collective-permute-start(bf16[48,3584]{1,0:T(8,128)(2,1)S(1)} %collective-permute-done.11), channel_id=1, source_target_pairs={{0,8},{8,16},{16,24},{24,0},{1,9},{9,17},{17,25},{25,1},{2,10},{10... | collective-permute-start | bytes 1032200 | tf_op jit(solution)/shard_map/ppermute | solution.py:11
  179.6 1.3 copy-start
  185.8 4.7 %collective-permute-start.13 = (bf16[24,1024]{1,0:T(8,128)(2,1)S(1)}, bf16[24,1024]{1,0:T(8,128)(2,1)S(1)}, u32[]{:S(2)}, u32[]{:S(2)}) collective-permute-start(bf16[24,1024]{1,0:T(8,128)(2,1)S(1)} %get-tuple-element.17), channel_id=1, source_target_pairs={{0,1},{1,2},{2,3},{3,4},{4,5},{5,6},{6,7},{7,0},{8,9},{9,10},{10,1... | collective-permute-start | bytes 147464 | tf_op jit(solution)/shard_map/ppermute | solution.py:11
  190.5 4.7 %collective-permute-start.14 = (bf16[24,1024]{1,0:T(8,128)(2,1)S(1)}, bf16[24,1024]{1,0:T(8,128)(2,1)S(1)}, u32[]{:S(2)}, u32[]{:S(2)}) collective-permute-start(bf16[24,1024]{1,0:T(8,128)(2,1)S(1)} %fusion.42), channel_id=1, source_target_pairs={{0,1},{1,2},{2,3},{3,4},{4,5},{5,6},{6,7},{7,0},{8,9},{9,10},{10,1... | collective-permute-start | bytes 147464 | tf_op jit(solution)/shard_map/ppermute | solution.py:11
  190.6 4.8 %collective-permute-start.17 = (bf16[24,1024]{1,0:T(8,128)(2,1)S(1)}, bf16[24,1024]{1,0:T(8,128)(2,1)S(1)}, u32[]{:S(2)}, u32[]{:S(2)}) collective-permute-start(bf16[24,1024]{1,0:T(8,128)(2,1)S(1)} %get-tuple-element.18), channel_id=1, source_target_pairs={{0,7},{1,0},{2,1},{3,2},{4,3},{5,4},{6,5},{7,6},{8,15},{9,8},{10,9... | collective-permute-start | bytes 147464 | tf_op jit(solution)/shard_map/ppermute | solution.py:11
  195.3 4.7 %collective-permute-start.15 = (bf16[24,1024]{1,0:T(8,128)(2,1)S(1)}, bf16[24,1024]{1,0:T(8,128)(2,1)S(1)}, u32[]{:S(2)}, u32[]{:S(2)}) collective-permute-start(bf16[24,1024]{1,0:T(8,128)(2,1)S(1)} %fusion.41), channel_id=1, source_target_pairs={{0,1},{1,2},{2,3},{3,4},{4,5},{5,6},{6,7},{7,0},{8,9},{9,10},{10,1... | collective-permute-start | bytes 147464 | tf_op jit(solution)/shard_map/ppermute | solution.py:11
  200.0 1.8 collective-permute-start.18
  200.1 5.2 %collective-permute-start.16 = (bf16[24,1024]{1,0:T(8,128)(2,1)S(1)}, bf16[24,1024]{1,0:T(8,128)(2,1)S(1)}, u32[]{:S(2)}, u32[]{:S(2)}) collective-permute-start(bf16[24,1024]{1,0:T(8,128)(2,1)S(1)} %get-tuple-element.15), channel_id=1, source_target_pairs={{0,1},{1,2},{2,3},{3,4},{4,5},{5,6},{6,7},{7,0},{8,9},{9,10},{10,1... | collective-permute-start | bytes 147464 | tf_op jit(solution)/shard_map/ppermute | solution.py:11
  201.8 5.1 %collective-permute-start.19 = (bf16[24,1024]{1,0:T(8,128)(2,1)S(1)}, bf16[24,1024]{1,0:T(8,128)(2,1)S(1)}, u32[]{:S(2)}, u32[]{:S(2)}) collective-permute-start(bf16[24,1024]{1,0:T(8,128)(2,1)S(1)} %fusion.36), channel_id=1, source_target_pairs={{0,7},{1,0},{2,1},{3,2},{4,3},{5,4},{6,5},{7,6},{8,15},{9,8},{10,9... | collective-permute-start | bytes 147464 | tf_op jit(solution)/shard_map/ppermute | solution.py:11
Sparse Core Ops, SparseCore 0:
  10.6 79.7 all-gather.1
  179.7 73.5 reduce-scatter.1

commit v4 on v3

--- a/solution.py
+++ b/solution.py
@@ -68,7 +68,7 @@
     pair_all = lax.all_gather(pair_local, "dp", axis=0, tiled=True).reshape(cap, bs, 2 * bs)
 
     x_rel = jnp.stack(ring_gather(layer_input, "col", n_col))
-    x_abs = jnp.roll(x_rel, k_col, axis=0).reshape(tok, feat)
+    x_abs = jnp.roll(x_rel, k_col, axis=0).reshape(tok, tile_rows, bs)
 
     tile_mask = lax.dynamic_slice(
         block_mask, (k_row * tile_rows, k_col * tile_cols), (tile_rows, tile_cols)
@@ -77,42 +77,39 @@
     position = jnp.cumsum(kept.astype(jnp.int32)) - 1
     q = jnp.arange(cap, dtype=jnp.int32)
     picks = kept[None, :] & (position[None, :] == q[:, None])
-    onehot = picks.astype(BF16)
-    onehot3 = onehot.reshape(cap, tile_rows, tile_cols)
+    onehot3 = picks.astype(BF16).reshape(cap, tile_rows, tile_cols)
     row_pick = jnp.sum(onehot3, axis=2)
     col_pick = jnp.sum(onehot3, axis=1)
+    highest = lax.Precision.HIGHEST
 
-    dense = jnp.einsum("qb,qkn->bkn", onehot, pair_all, preferred_element_type=F32).astype(BF16)
-    wd = dense.reshape(tile_rows, tile_cols, bs, 2 * bs).transpose(0, 2, 1, 3)
-    wd = wd.reshape(feat, tile_cols * 2 * bs)
-
-    pre = jnp.dot(x_abs, wd, preferred_element_type=F32).astype(BF16)
-    pre_roll = jnp.roll(pre.reshape(n_row, rows_per, tile_cols * 2 * bs), -k_row, axis=0)
-    pre_sum = ring_sum_scatter([pre_roll[m] for m in range(n_row)], "row", n_row)
-    pre_sum = pre_sum.reshape(rows_per, tile_cols, 2 * bs)
+    x_pick = jnp.einsum("qr,trk->qtk", row_pick, x_abs, preferred_element_type=F32).astype(BF16)
+    per_slot = jnp.einsum("qtk,qkn->qtn", x_pick, pair_all, preferred_element_type=F32)
+    pre = jnp.einsum(
+        "qc,qtn->ctn", col_pick.astype(F32), per_slot, precision=highest, preferred_element_type=F32
+    ).astype(BF16)
+    pre_roll = jnp.roll(pre.reshape(tile_cols, n_row, rows_per, 2 * bs), -k_row, axis=1)
+    pre_sum = ring_sum_scatter([pre_roll[:, m] for m in range(n_row)], "row", n_row)
     gate = pre_sum[..., :bs]
     up = pre_sum[..., bs:]
-    upstream = hidden_grad.astype(F32).reshape(rows_per, tile_cols, bs)
+    upstream = hidden_grad.astype(F32).reshape(rows_per, tile_cols, bs).transpose(1, 0, 2)
     sig = jax.nn.sigmoid(gate)
     gate_grad = (upstream * up * sig * (1.0 + gate * (1.0 - sig))).astype(BF16)
     up_grad = (upstream * gate * sig).astype(BF16)
-    grad_local = jnp.concatenate([gate_grad, up_grad], axis=2).reshape(rows_per, tile_cols * 2 * bs)
-    grad_rel = jnp.stack(ring_gather(grad_local, "row", n_row))
-    grad_abs = jnp.roll(grad_rel, k_row, axis=0).reshape(tok, tile_cols * 2 * bs)
+    grad_local = jnp.concatenate([gate_grad, up_grad], axis=2)
+    grad_rel = jnp.stack(ring_gather(grad_local, "row", n_row), axis=1)
+    grad_abs = jnp.roll(grad_rel, k_row, axis=1).reshape(tile_cols, tok, 2 * bs)
 
-    dx = lax.dot_general(
-        grad_abs, wd, (((1,), (1,)), ((), ())), preferred_element_type=F32
+    g_pick = jnp.einsum("qc,ctn->qtn", col_pick, grad_abs, preferred_element_type=F32).astype(BF16)
+    slot_dw = jnp.einsum("qtk,qtn->qkn", x_pick, g_pick, preferred_element_type=F32).astype(BF16)
+
+    dx_slot = jnp.einsum("qtn,qkn->qtk", g_pick, pair_all, preferred_element_type=F32)
+    dx = jnp.einsum(
+        "qr,qtk->rtk", row_pick.astype(F32), dx_slot, precision=highest, preferred_element_type=F32
     ).astype(BF16)
-    dx_roll = jnp.roll(dx.reshape(n_col, cols_per, feat), -k_col, axis=0)
-    input_grad = ring_sum_scatter([dx_roll[m] for m in range(n_col)], "col", n_col).astype(BF16)
+    dx_roll = jnp.roll(dx.reshape(tile_rows, n_col, cols_per, bs), -k_col, axis=1)
+    dx_sum = ring_sum_scatter([dx_roll[:, m] for m in range(n_col)], "col", n_col)
+    input_grad = dx_sum.transpose(1, 0, 2).reshape(cols_per, feat).astype(BF16)
 
-    x_pick = jnp.einsum(
-        "qr,trk->qtk", row_pick, x_abs.reshape(tok, tile_rows, bs), preferred_element_type=F32
-    ).astype(BF16)
-    g_pick = jnp.einsum(
-        "qc,tcn->qtn", col_pick, grad_abs.reshape(tok, tile_cols, 2 * bs), preferred_element_type=F32
-    ).astype(BF16)
-    slot_dw = jnp.einsum("qtk,qtn->qkn", x_pick, g_pick, preferred_element_type=F32).astype(BF16)
     dw_sum = lax.psum_scatter(
         slot_dw.reshape(cap * bs, 2 * bs), "dp", scatter_dimension=0, tiled=True
     ).astype(F32) / n_dp

time: 263 us -> 247 us (0.939)
  the two profiles are of different devices: /device:TPU:8 before, /device:TPU:2 now
where the time goes in v4:
time: 247 us; the launch traced here: 246 us
  waiting for transfers between devices  157 us (64%)
  starting transfers between devices  31.2 us (13%)
  matrix products  26.2 us (11%)
  between operations  14.5 us (6%)
  other arithmetic  10.1 us (4%)
  local copies, waits for them, and re-layouts  6.49 us (3%)
    all_gather x1, waiting for transfers between devices, on_device(): lax.all_gather(pair_local, 'dp', axis=0, tiled=True)  60.8 us
    ppermute x20, waiting for transfers between devices, _shift(): return lax.ppermute(x, axis, perm=[(i, (i + step) % n) for i in range(n)])  55 us
    reduce_scatter x1, waiting for transfers between devices, on_device(): lax.psum_scatter(slot_dw.reshape(cap * bs, 2 * bs), 'dp', scatter_dimensi...  41.7 us
    ppermute x20, starting transfers between devices, _shift(): return lax.ppermute(x, axis, perm=[(i, (i + step) % n) for i in range(n)])  31.2 us
    dot_general x1, matrix products, on_device(): jnp.einsum('qc,qtn->ctn', col_pick.astype(F32), per_slot, precision=highe...  8.66 us
  transfers between devices with their start and end apart: 22, of which 15 were waited for; matrix products, arithmetic and copies ran while one was open for 6% of the time, Pallas kernels for 0%

profile of v4, /device:TPU:2, one launch (start us, length us, event | category | flops | bytes accessed | tf_op | source)
XLA Modules:
  0.0 245.9 jit_solution(7775233816213421277)
XLA Ops:
  11.8 5.5 %collective-permute-start.1 = (bf16[24,1024]{1,0:T(8,128)(2,1)S(1)}, bf16[24,1024]{1,0:T(8,128)(2,1)S(1)}, u32[]{:S(2)}, u32[]{:S(2)}) collective-permute-start(bf16[24,1024]{1,0:T(8,128)(2,1)S(1)} %collective-permute-done), channel_id=1, source_target_pairs={{0,7},{1,0},{2,1},{3,2},{4,3},{5,4},{6,5},{7,6},{8,15},{9,8},{10,9... | collective-permute-start | bytes 147464 | tf_op jit(solution)/shard_map/ppermute | solution.py:11
  20.9 3.5 %collective-permute-done.5 = bf16[24,1024]{1,0:T(8,128)(2,1)S(1)} collective-permute-done((bf16[24,1024]{1,0:T(8,128)(2,1)S(1)}, bf16[24,1024]{1,0:T(8,128)(2,1)S(1)}, u32[]{:S(2)}, u32[]{:S(2)}) %collective-permute-start.5) | collective-permute-done | bytes 49184 | tf_op jit(solution)/shard_map/ppermute | solution.py:11
  24.4 3.5 %collective-permute-done.6 = bf16[24,1024]{1,0:T(8,128)(2,1)S(1)} collective-permute-done((bf16[24,1024]{1,0:T(8,128)(2,1)S(1)}, bf16[24,1024]{1,0:T(8,128)(2,1)S(1)}, u32[]{:S(2)}, u32[]{:S(2)}) %collective-permute-start.6) | collective-permute-done | bytes 49184 | tf_op jit(solution)/shard_map/ppermute | solution.py:11
  29.8 60.8 %all-gather.2.cloned.1.call-done = bf16[6144,256]{1,0:T(8,128)(2,1)} async-done(((bf16[384,256]{1,0:T(8,128)(2,1)}), bf16[6144,256]{1,0:T(8,128)(2,1)}) %all-gather.2.cloned.1.call-update) | async-done | bytes 3145744 | tf_op jit(solution)/shard_map/all_gather | solution.py:68
  90.5 3.3 %fusion.12 = f32[48,192,256]{2,1,0:T(8,128)S(1)} fusion(bf16[48,128,256]{2,1,0:T(8,128)(2,1)} %bitcast.118, bf16[48,192,128]{2,0,1:T(8,128)(2,1)S(1)} %convolution_convert_fusion.1), kind=kOutput, calls=%fused_computation.21 | convolution fusion | flops 603979776 | bytes 14942208 | tf_op jit(solution)/shard_map/qtk,qkn->qtn/dot_general | solution.py:86
  93.8 8.7 %fusion.14 = bf16[14,192,256]{2,0,1:T(8,128)(2,1)S(1)} fusion(f32[48,192,256]{2,1,0:T(8,128)S(1)} %fusion.12, bf16[48,14]{0,1:T(8,128)(2,1)S(1)} %get-tuple-element.4), kind=kOutput, calls=%fused_computation.24 | convolution fusion | flops 397049856 | bytes 10814784 | tf_op jit(solution)/shard_map/qc,qtn->ctn/dot_general | solution.py:87
  103.4 3.4 %collective-permute-start.7 = (bf16[14,48,256]{2,0,1:T(8,128)(2,1)S(1)}, bf16[14,48,256]{2,0,1:T(8,128)(2,1)S(1)}, u32[]{:S(2)}, u32[]{:S(2)}) collective-permute-start(bf16[14,48,256]{2,0,1:T(8,128)(2,1)S(1)} %get-tuple-element.8), channel_id=1, source_target_pairs={{0,8},{8,16},{16,24},{24,0},{1,9},{9,17},{17,25},{25,1},{2,10},{10... | collective-permute-start | bytes 1032200 | tf_op jit(solution)/shard_map/ppermute | solution.py:11
  106.8 3.7 %collective-permute-start.9 = (bf16[14,48,256]{2,0,1:T(8,128)(2,1)S(1)}, bf16[14,48,256]{2,0,1:T(8,128)(2,1)}, u32[]{:S(2)}, u32[]{:S(2)}) collective-permute-start(bf16[14,48,256]{2,0,1:T(8,128)(2,1)S(1)} %get-tuple-element.9), channel_id=1, source_target_pairs={{0,24},{8,0},{16,8},{24,16},{1,25},{9,1},{17,9},{25,17},{2,26},{10... | collective-permute-start | bytes 1032200 | tf_op jit(solution)/shard_map/ppermute | solution.py:11
  110.5 7.7 %collective-permute-done.7 = bf16[14,48,256]{2,0,1:T(8,128)(2,1)S(1)} collective-permute-done((bf16[14,48,256]{2,0,1:T(8,128)(2,1)S(1)}, bf16[14,48,256]{2,0,1:T(8,128)(2,1)S(1)}, u32[]{:S(2)}, u32[]{:S(2)}) %collective-permute-start.7) | collective-permute-done | bytes 344096 | tf_op jit(solution)/shard_map/ppermute | solution.py:11
  118.3 1.9 collective-permute-start.8
  121.3 11.8 %collective-permute-done.8 = bf16[14,48,256]{2,0,1:T(8,128)(2,1)} collective-permute-done((bf16[14,48,256]{2,0,1:T(8,128)(2,1)S(1)}, bf16[14,48,256]{2,0,1:T(8,128)(2,1)}, u32[]{:S(2)}, u32[]{:S(2)}) %collective-permute-start.8) | collective-permute-done | bytes 344096 | tf_op jit(solution)/shard_map/ppermute | solution.py:11
  134.8 1.9 collective-permute-start.11
  136.7 5.1 %collective-permute-start.10 = (bf16[14,48,256]{2,0,1:T(8,128)(2,1)S(1)}, bf16[14,48,256]{2,0,1:T(8,128)(2,1)}, u32[]{:S(2)}, u32[]{:S(2)}) collective-permute-start(bf16[14,48,256]{2,0,1:T(8,128)(2,1)S(1)} %get-tuple-element.18), channel_id=1, source_target_pairs={{0,24},{8,0},{16,8},{24,16},{1,25},{9,1},{17,9},{25,17},{2,26},{10... | collective-permute-start | bytes 1032200 | tf_op jit(solution)/shard_map/ppermute | solution.py:11
  141.9 5.5 %collective-permute-done.11 = bf16[14,48,256]{2,0,1:T(8,128)(2,1)S(1)} collective-permute-done((bf16[14,48,256]{2,0,1:T(8,128)(2,1)S(1)}, bf16[14,48,256]{2,0,1:T(8,128)(2,1)S(1)}, u32[]{:S(2)}, u32[]{:S(2)}) %collective-permute-start.11) | collective-permute-done | bytes 344096 | tf_op jit(solution)/shard_map/ppermute | solution.py:11
  147.4 1.9 collective-permute-start.12
  149.3 9.0 %collective-permute-done.12 = bf16[14,48,256]{2,0,1:T(8,128)(2,1)} collective-permute-done((bf16[14,48,256]{2,0,1:T(8,128)(2,1)S(1)}, bf16[14,48,256]{2,0,1:T(8,128)(2,1)}, u32[]{:S(2)}, u32[]{:S(2)}) %collective-permute-start.12) | collective-permute-done | bytes 344096 | tf_op jit(solution)/shard_map/ppermute | solution.py:11
  158.3 3.4 %fusion.20 = bf16[14,4,48,256]{3,0,2,1:T(8,128)(2,1)S(1)} fusion(s32[]{:T(128)S(6)} %select_n.47, bf16[14,1,48,256]{3,0,2,1:T(8,128)(2,1)S(1)} %get-tuple-element.19, bf16[14,1,48,256]{3,0,2,1:T(8,128)(2,1)} %bitcast.20, bf16[14,1,48,256]{3,0,2,1:T(8,128)(2,1)} %bitcast.21, bf16[14,1,48,256]{3,0,2,1:T(8,128)(2,1)S(1)} %bitcast.127), kind=kLoop, calls=%fused_computation.28 | loop fusion | flops 4816896 | bytes 2752516 | tf_op jit(solution)/shard_map/jit(_roll_dynamic)/concatenate | solution.py:100
  163.2 3.6 %fusion.8 = bf16[48,128,256]{2,1,0:T(8,128)(2,1)} fusion(bf16[48,192,256]{2,0,1:T(8,128)(2,1)S(1)} %convolution_convert_fusion, bf16[48,192,128]{2,0,1:T(8,128)(2,1)S(1)} %convolution_convert_fusion.1), kind=kOutput, calls=%fused_computation.19 | convolution fusion | flops 605552640 | bytes 10223616 | tf_op jit(solution)/shard_map/qtk,qtn->qkn/dot_general | solution.py:103
  168.7 4.1 %fusion.6 = f32[48,192,128]{2,1,0:T(8,128)S(1)} fusion(bf16[48,128,256]{2,1,0:T(8,128)(2,1)S(1)} %bitcast.119, bf16[48,192,256]{2,0,1:T(8,128)(2,1)} %copy-done), kind=kOutput, calls=%fused_computation.6 | convolution fusion | flops 603979776 | bytes 12582912 | tf_op jit(solution)/shard_map/qtn,qkn->qtk/dot_general | solution.py:105
  172.8 4.3 %fusion.25 = bf16[8,192,128]{2,0,1:T(8,128)(2,1)S(1)} fusion(f32[48,192,128]{2,1,0:T(8,128)S(1)} %fusion.6, bf16[48,8]{0,1:T(8,128)(2,1)S(1)} %get-tuple-element.5), kind=kOutput, calls=%fused_computation.33 | convolution fusion | flops 113442816 | bytes 5112576 | tf_op jit(solution)/shard_map/qr,qtk->rtk/dot_general | solution.py:106
  177.3 3.5 %collective-permute-done.13 = bf16[8,24,128]{2,0,1:T(8,128)(2,1)S(1)} collective-permute-done((bf16[8,24,128]{2,0,1:T(8,128)(2,1)S(1)}, bf16[8,24,128]{2,0,1:T(8,128)(2,1)S(1)}, u32[]{:S(2)}, u32[]{:S(2)}) %collective-permute-start.13) | collective-permute-done | bytes 49184 | tf_op jit(solution)/shard_map/ppermute | solution.py:11
  184.4 3.5 %collective-permute-done.15 = bf16[8,24,128]{2,0,1:T(8,128)(2,1)S(1)} collective-permute-done((bf16[8,24,128]{2,0,1:T(8,128)(2,1)S(1)}, bf16[8,24,128]{2,0,1:T(8,128)(2,1)S(1)}, u32[]{:S(2)}, u32[]{:S(2)}) %collective-permute-start.15) | collective-permute-done | bytes 49184 | tf_op jit(solution)/shard_map/ppermute | solution.py:11
  190.1 3.1 %collective-permute-start.19 = (bf16[8,24,128]{2,0,1:T(8,128)(2,1)S(1)}, bf16[8,24,128]{2,0,1:T(8,128)(2,1)S(1)}, u32[]{:S(2)}, u32[]{:S(2)}) collective-permute-start(bf16[8,24,128]{2,0,1:T(8,128)(2,1)S(1)} %fusion.36), channel_id=1, source_target_pairs={{0,7},{1,0},{2,1},{3,2},{4,3},{5,4},{6,5},{7,6},{8,15},{9,8},{10,9... | collective-permute-start | bytes 147464 | tf_op jit(solution)/shard_map/ppermute | solution.py:11
  195.7 41.7 %reduce-scatter.2.cloned.1.call-done = bf16[384,256]{1,0:T(8,128)(2,1)} async-done(((bf16[6144,256]{1,0:T(8,128)(2,1)}), bf16[384,256]{1,0:T(8,128)(2,1)}) %reduce-scatter.2.cloned.1.call-update) | async-done | bytes 196624 | tf_op jit(solution)/shard_map/reduce_scatter | solution.py:113
  (80 shorter events, 27.0 us)
Async XLA Ops:
  7.2 83.4 %all-gather.2.cloned.1.call-start = ((), (), s32[]{:S(2)}) async-start(), calls=%async_computation.1 | async-start | bytes 3342336 | tf_op jit(solution)/shard_map/all_gather | solution.py:68
  8.9 228.5 %reduce-scatter.2.cloned.1.call-start = ((), (), s32[]{:S(2)}) async-start(), calls=%async_computation.2 | async-start | bytes 3342336 | tf_op jit(solution)/shard_map/reduce_scatter | solution.py:113
  8.9 2.9 %collective-permute-start = (bf16[24,1024]{1,0:T(8,128)(2,1)}, bf16[24,1024]{1,0:T(8,128)(2,1)S(1)}, u32[]{:S(2)}, u32[]{:S(2)}) collective-permute-start(bf16[24,1024]{1,0:T(8,128)(2,1)} %param.7), channel_id=1, source_target_pairs={{0,7},{1,0},{2,1},{3,2},{4,3},{5,4},{6,5},{7,6},{8,15},{9,8},{10,9... | collective-permute-start | bytes 147464 | tf_op jit(solution)/shard_map/ppermute | solution.py:11
  9.0 8.4 %collective-permute-start.3 = (bf16[24,1024]{1,0:T(8,128)(2,1)}, bf16[24,1024]{1,0:T(8,128)(2,1)S(1)}, u32[]{:S(2)}, u32[]{:S(2)}) collective-permute-start(bf16[24,1024]{1,0:T(8,128)(2,1)} %param.7), channel_id=1, source_target_pairs={{0,1},{1,2},{2,3},{3,4},{4,5},{5,6},{6,7},{7,0},{8,9},{9,10},{10,1... | collective-permute-start | bytes 147464 | tf_op jit(solution)/shard_map/ppermute | solution.py:11
  11.8 7.3 %collective-permute-start.1 = (bf16[24,1024]{1,0:T(8,128)(2,1)S(1)}, bf16[24,1024]{1,0:T(8,128)(2,1)S(1)}, u32[]{:S(2)}, u32[]{:S(2)}) collective-permute-start(bf16[24,1024]{1,0:T(8,128)(2,1)S(1)} %collective-permute-done), channel_id=1, source_target_pairs={{0,7},{1,0},{2,1},{3,2},{4,3},{5,4},{6,5},{7,6},{8,15},{9,8},{10,9... | collective-permute-start | bytes 147464 | tf_op jit(solution)/shard_map/ppermute | solution.py:11
  17.3 3.5 %collective-permute-start.4 = (bf16[24,1024]{1,0:T(8,128)(2,1)S(1)}, bf16[24,1024]{1,0:T(8,128)(2,1)S(1)}, u32[]{:S(2)}, u32[]{:S(2)}) collective-permute-start(bf16[24,1024]{1,0:T(8,128)(2,1)S(1)} %collective-permute-done.3), channel_id=1, source_target_pairs={{0,1},{1,2},{2,3},{3,4},{4,5},{5,6},{6,7},{7,0},{8,9},{9,10},{10,1... | collective-permute-start | bytes 147464 | tf_op jit(solution)/shard_map/ppermute | solution.py:11
  19.1 5.3 %collective-permute-start.2 = (bf16[24,1024]{1,0:T(8,128)(2,1)S(1)}, bf16[24,1024]{1,0:T(8,128)(2,1)S(1)}, u32[]{:S(2)}, u32[]{:S(2)}) collective-permute-start(bf16[24,1024]{1,0:T(8,128)(2,1)S(1)} %collective-permute-done.1), channel_id=1, source_target_pairs={{0,7},{1,0},{2,1},{3,2},{4,3},{5,4},{6,5},{7,6},{8,15},{9,8},{10,9... | collective-permute-start | bytes 147464 | tf_op jit(solution)/shard_map/ppermute | solution.py:11
  20.9 3.5 %collective-permute-start.5 = (bf16[24,1024]{1,0:T(8,128)(2,1)S(1)}, bf16[24,1024]{1,0:T(8,128)(2,1)S(1)}, u32[]{:S(2)}, u32[]{:S(2)}) collective-permute-start(bf16[24,1024]{1,0:T(8,128)(2,1)S(1)} %collective-permute-done.4), channel_id=1, source_target_pairs={{0,1},{1,2},{2,3},{3,4},{4,5},{5,6},{6,7},{7,0},{8,9},{9,10},{10,1... | collective-permute-start | bytes 147464 | tf_op jit(solution)/shard_map/ppermute | solution.py:11
  24.4 3.5 %collective-permute-start.6 = (bf16[24,1024]{1,0:T(8,128)(2,1)S(1)}, bf16[24,1024]{1,0:T(8,128)(2,1)S(1)}, u32[]{:S(2)}, u32[]{:S(2)}) collective-permute-start(bf16[24,1024]{1,0:T(8,128)(2,1)S(1)} %collective-permute-done.5), channel_id=1, source_target_pairs={{0,1},{1,2},{2,3},{3,4},{4,5},{5,6},{6,7},{7,0},{8,9},{9,10},{10,1... | collective-permute-start | bytes 147464 | tf_op jit(solution)/shard_map/ppermute | solution.py:11
  103.3 14.9 %copy-start.2 = (bf16[14,4,48,256]{3,0,2,1:T(8,128)(2,1)}, bf16[14,4,48,256]{3,0,2,1:T(8,128)(2,1)S(1)}, u32[]{:S(2)}) copy-start(bf16[14,4,48,256]{3,0,2,1:T(8,128)(2,1)S(1)} %fusion.24) | copy-start | bytes 4128772
  103.4 14.8 %collective-permute-start.7 = (bf16[14,48,256]{2,0,1:T(8,128)(2,1)S(1)}, bf16[14,48,256]{2,0,1:T(8,128)(2,1)S(1)}, u32[]{:S(2)}, u32[]{:S(2)}) collective-permute-start(bf16[14,48,256]{2,0,1:T(8,128)(2,1)S(1)} %get-tuple-element.8), channel_id=1, source_target_pairs={{0,8},{8,16},{16,24},{24,0},{1,9},{9,17},{17,25},{25,1},{2,10},{10... | collective-permute-start | bytes 1032200 | tf_op jit(solution)/shard_map/ppermute | solution.py:11
  106.8 14.5 %collective-permute-start.9 = (bf16[14,48,256]{2,0,1:T(8,128)(2,1)S(1)}, bf16[14,48,256]{2,0,1:T(8,128)(2,1)}, u32[]{:S(2)}, u32[]{:S(2)}) collective-permute-start(bf16[14,48,256]{2,0,1:T(8,128)(2,1)S(1)} %get-tuple-element.9), channel_id=1, source_target_pairs={{0,24},{8,0},{16,8},{24,16},{1,25},{9,1},{17,9},{25,17},{2,26},{10... | collective-permute-start | bytes 1032200 | tf_op jit(solution)/shard_map/ppermute | solution.py:11
  118.3 14.8 %collective-permute-start.8 = (bf16[14,48,256]{2,0,1:T(8,128)(2,1)S(1)}, bf16[14,48,256]{2,0,1:T(8,128)(2,1)}, u32[]{:S(2)}, u32[]{:S(2)}) collective-permute-start(bf16[14,48,256]{2,0,1:T(8,128)(2,1)S(1)} %fusion.29), channel_id=1, source_target_pairs={{0,8},{8,16},{16,24},{24,0},{1,9},{9,17},{17,25},{25,1},{2,10},{10... | collective-permute-start | bytes 1032200 | tf_op jit(solution)/shard_map/ppermute | solution.py:11
  134.8 12.6 %collective-permute-start.11 = (bf16[14,48,256]{2,0,1:T(8,128)(2,1)S(1)}, bf16[14,48,256]{2,0,1:T(8,128)(2,1)S(1)}, u32[]{:S(2)}, u32[]{:S(2)}) collective-permute-start(bf16[14,48,256]{2,0,1:T(8,128)(2,1)S(1)} %get-tuple-element.18), channel_id=1, source_target_pairs={{0,8},{8,16},{16,24},{24,0},{1,9},{9,17},{17,25},{25,1},{2,10},{10... | collective-permute-start | bytes 1032200 | tf_op jit(solution)/shard_map/ppermute | solution.py:11
  136.7 12.6 %collective-permute-start.10 = (bf16[14,48,256]{2,0,1:T(8,128)(2,1)S(1)}, bf16[14,48,256]{2,0,1:T(8,128)(2,1)}, u32[]{:S(2)}, u32[]{:S(2)}) collective-permute-start(bf16[14,48,256]{2,0,1:T(8,128)(2,1)S(1)} %get-tuple-element.18), channel_id=1, source_target_pairs={{0,24},{8,0},{16,8},{24,16},{1,25},{9,1},{17,9},{25,17},{2,26},{10... | collective-permute-start | bytes 1032200 | tf_op jit(solution)/shard_map/ppermute | solution.py:11
  147.4 11.0 %collective-permute-start.12 = (bf16[14,48,256]{2,0,1:T(8,128)(2,1)S(1)}, bf16[14,48,256]{2,0,1:T(8,128)(2,1)}, u32[]{:S(2)}, u32[]{:S(2)}) collective-permute-start(bf16[14,48,256]{2,0,1:T(8,128)(2,1)S(1)} %collective-permute-done.11), channel_id=1, source_target_pairs={{0,8},{8,16},{16,24},{24,0},{1,9},{9,17},{17,25},{25,1},{2,10},{10... | collective-permute-start | bytes 1032200 | tf_op jit(solution)/shard_map/ppermute | solution.py:11
  163.2 3.6 %copy-start = (bf16[48,192,256]{2,0,1:T(8,128)(2,1)}, bf16[48,192,256]{2,0,1:T(8,128)(2,1)S(1)}, u32[]{:S(2)}) copy-start(bf16[48,192,256]{2,0,1:T(8,128)(2,1)S(1)} %convolution_convert_fusion) | copy-start | bytes 14155780
  177.3 3.5 %collective-permute-start.13 = (bf16[8,24,128]{2,0,1:T(8,128)(2,1)S(1)}, bf16[8,24,128]{2,0,1:T(8,128)(2,1)S(1)}, u32[]{:S(2)}, u32[]{:S(2)}) collective-permute-start(bf16[8,24,128]{2,0,1:T(8,128)(2,1)S(1)} %get-tuple-element.16), channel_id=1, source_target_pairs={{0,1},{1,2},{2,3},{3,4},{4,5},{5,6},{6,7},{7,0},{8,9},{9,10},{10,1... | collective-permute-start | bytes 147464 | tf_op jit(solution)/shard_map/ppermute | solution.py:11
  180.8 3.5 %collective-permute-start.14 = (bf16[8,24,128]{2,0,1:T(8,128)(2,1)S(1)}, bf16[8,24,128]{2,0,1:T(8,128)(2,1)S(1)}, u32[]{:S(2)}, u32[]{:S(2)}) collective-permute-start(bf16[8,24,128]{2,0,1:T(8,128)(2,1)S(1)} %fusion.42), channel_id=1, source_target_pairs={{0,1},{1,2},{2,3},{3,4},{4,5},{5,6},{6,7},{7,0},{8,9},{9,10},{10,1... | collective-permute-start | bytes 147464 | tf_op jit(solution)/shard_map/ppermute | solution.py:11
  180.9 3.5 %collective-permute-start.17 = (bf16[8,24,128]{2,0,1:T(8,128)(2,1)S(1)}, bf16[8,24,128]{2,0,1:T(8,128)(2,1)S(1)}, u32[]{:S(2)}, u32[]{:S(2)}) collective-permute-start(bf16[8,24,128]{2,0,1:T(8,128)(2,1)S(1)} %get-tuple-element.17), channel_id=1, source_target_pairs={{0,7},{1,0},{2,1},{3,2},{4,3},{5,4},{6,5},{7,6},{8,15},{9,8},{10,9... | collective-permute-start | bytes 147464 | tf_op jit(solution)/shard_map/ppermute | solution.py:11
  184.4 3.5 %collective-permute-start.15 = (bf16[8,24,128]{2,0,1:T(8,128)(2,1)S(1)}, bf16[8,24,128]{2,0,1:T(8,128)(2,1)S(1)}, u32[]{:S(2)}, u32[]{:S(2)}) collective-permute-start(bf16[8,24,128]{2,0,1:T(8,128)(2,1)S(1)} %fusion.41), channel_id=1, source_target_pairs={{0,1},{1,2},{2,3},{3,4},{4,5},{5,6},{6,7},{7,0},{8,9},{9,10},{10,1... | collective-permute-start | bytes 147464 | tf_op jit(solution)/shard_map/ppermute | solution.py:11
  187.9 2.2 collective-permute-start.18
  188.4 5.8 %collective-permute-start.16 = (bf16[8,24,128]{2,0,1:T(8,128)(2,1)S(1)}, bf16[8,24,128]{2,0,1:T(8,128)(2,1)S(1)}, u32[]{:S(2)}, u32[]{:S(2)}) collective-permute-start(bf16[8,24,128]{2,0,1:T(8,128)(2,1)S(1)} %get-tuple-element.14), channel_id=1, source_target_pairs={{0,1},{1,2},{2,3},{3,4},{4,5},{5,6},{6,7},{7,0},{8,9},{9,10},{10,1... | collective-permute-start | bytes 147464 | tf_op jit(solution)/shard_map/ppermute | solution.py:11
  190.1 4.9 %collective-permute-start.19 = (bf16[8,24,128]{2,0,1:T(8,128)(2,1)S(1)}, bf16[8,24,128]{2,0,1:T(8,128)(2,1)S(1)}, u32[]{:S(2)}, u32[]{:S(2)}) collective-permute-start(bf16[8,24,128]{2,0,1:T(8,128)(2,1)S(1)} %fusion.36), channel_id=1, source_target_pairs={{0,7},{1,0},{2,1},{3,2},{4,3},{5,4},{6,5},{7,6},{8,15},{9,8},{10,9... | collective-permute-start | bytes 147464 | tf_op jit(solution)/shard_map/ppermute | solution.py:11
  (1 other events, 1.9 us)
Sparse Core Ops, SparseCore 0:
  10.6 79.8 all-gather.1
  167.0 70.3 reduce-scatter.1

commit v5 on v4

--- a/solution.py
+++ b/solution.py
@@ -63,9 +63,12 @@
     rows_per = tok // n_row
     cols_per = tok // n_col
 
-    pair_local = jnp.concatenate([gate_slots[0, 0], up_slots[0, 0]], axis=2)
-    pair_local = pair_local.reshape(per_dev * bs, 2 * bs)
-    pair_all = lax.all_gather(pair_local, "dp", axis=0, tiled=True).reshape(cap, bs, 2 * bs)
+    gate_all = lax.all_gather(
+        gate_slots[0, 0].reshape(per_dev * bs, bs), "dp", axis=0, tiled=True
+    ).reshape(cap, bs, bs)
+    up_all = lax.all_gather(
+        up_slots[0, 0].reshape(per_dev * bs, bs), "dp", axis=0, tiled=True
+    ).reshape(cap, bs, bs)
 
     x_rel = jnp.stack(ring_gather(layer_input, "col", n_col))
     x_abs = jnp.roll(x_rel, k_col, axis=0).reshape(tok, tile_rows, bs)
@@ -80,42 +83,48 @@
     onehot3 = picks.astype(BF16).reshape(cap, tile_rows, tile_cols)
     row_pick = jnp.sum(onehot3, axis=2)
     col_pick = jnp.sum(onehot3, axis=1)
-    highest = lax.Precision.HIGHEST
+    high = lax.Precision.HIGH
 
     x_pick = jnp.einsum("qr,trk->qtk", row_pick, x_abs, preferred_element_type=F32).astype(BF16)
-    per_slot = jnp.einsum("qtk,qkn->qtn", x_pick, pair_all, preferred_element_type=F32)
-    pre = jnp.einsum(
-        "qc,qtn->ctn", col_pick.astype(F32), per_slot, precision=highest, preferred_element_type=F32
-    ).astype(BF16)
-    pre_roll = jnp.roll(pre.reshape(tile_cols, n_row, rows_per, 2 * bs), -k_row, axis=1)
-    pre_sum = ring_sum_scatter([pre_roll[:, m] for m in range(n_row)], "row", n_row)
-    gate = pre_sum[..., :bs]
-    up = pre_sum[..., bs:]
+
+    def pre_rows(weights):
+        per_slot = jnp.einsum("qtk,qkn->qtn", x_pick, weights, preferred_element_type=F32)
+        pre = jnp.einsum(
+            "qc,qtn->ctn", col_pick.astype(F32), per_slot, precision=high, preferred_element_type=F32
+        ).astype(BF16)
+        pre_roll = jnp.roll(pre.reshape(tile_cols, n_row, rows_per, bs), -k_row, axis=1)
+        return ring_sum_scatter([pre_roll[:, m] for m in range(n_row)], "row", n_row)
+
+    gate = pre_rows(gate_all)
+    up = pre_rows(up_all)
     upstream = hidden_grad.astype(F32).reshape(rows_per, tile_cols, bs).transpose(1, 0, 2)
     sig = jax.nn.sigmoid(gate)
     gate_grad = (upstream * up * sig * (1.0 + gate * (1.0 - sig))).astype(BF16)
     up_grad = (upstream * gate * sig).astype(BF16)
-    grad_local = jnp.concatenate([gate_grad, up_grad], axis=2)
-    grad_rel = jnp.stack(ring_gather(grad_local, "row", n_row), axis=1)
-    grad_abs = jnp.roll(grad_rel, k_row, axis=1).reshape(tile_cols, tok, 2 * bs)
 
-    g_pick = jnp.einsum("qc,ctn->qtn", col_pick, grad_abs, preferred_element_type=F32).astype(BF16)
-    slot_dw = jnp.einsum("qtk,qtn->qkn", x_pick, g_pick, preferred_element_type=F32).astype(BF16)
+    def grad_slots(grad_part):
+        grad_rel = jnp.stack(ring_gather(grad_part, "row", n_row), axis=1)
+        grad_abs = jnp.roll(grad_rel, k_row, axis=1).reshape(tile_cols, tok, bs)
+        return jnp.einsum("qc,ctn->qtn", col_pick, grad_abs, preferred_element_type=F32).astype(BF16)
 
-    dx_slot = jnp.einsum("qtn,qkn->qtk", g_pick, pair_all, preferred_element_type=F32)
+    def slot_grad(picked):
+        slot_dw = jnp.einsum("qtk,qtn->qkn", x_pick, picked, preferred_element_type=F32).astype(BF16)
+        total = lax.psum_scatter(slot_dw.reshape(cap * bs, bs), "dp", scatter_dimension=0, tiled=True)
+        return (total.astype(F32) / n_dp).reshape(per_dev, bs, bs)[None, None]
+
+    gate_pick = grad_slots(gate_grad)
+    gate_out = slot_grad(gate_pick)
+    up_pick = grad_slots(up_grad)
+    up_out = slot_grad(up_pick)
+
+    dx_slot = jnp.einsum("qtn,qkn->qtk", gate_pick, gate_all, preferred_element_type=F32)
+    dx_slot = dx_slot + jnp.einsum("qtn,qkn->qtk", up_pick, up_all, preferred_element_type=F32)
     dx = jnp.einsum(
-        "qr,qtk->rtk", row_pick.astype(F32), dx_slot, precision=highest, preferred_element_type=F32
+        "qr,qtk->rtk", row_pick.astype(F32), dx_slot, precision=high, preferred_element_type=F32
     ).astype(BF16)
     dx_roll = jnp.roll(dx.reshape(tile_rows, n_col, cols_per, bs), -k_col, axis=1)
     dx_sum = ring_sum_scatter([dx_roll[:, m] for m in range(n_col)], "col", n_col)
     input_grad = dx_sum.transpose(1, 0, 2).reshape(cols_per, feat).astype(BF16)
-
-    dw_sum = lax.psum_scatter(
-        slot_dw.reshape(cap * bs, 2 * bs), "dp", scatter_dimension=0, tiled=True
-    ).astype(F32) / n_dp
-    dw_sum = dw_sum.reshape(per_dev, bs, 2 * bs)
-    gate_out = dw_sum[..., :bs][None, None]
-    up_out = dw_sum[..., bs:][None, None]
     return (input_grad, gate_out, up_out)
 
 

time: 247 us -> 375 us (1.52)
  waiting for transfers between devices: 157 us -> 265 us
  starting transfers between devices: 31.2 us -> 48.7 us
    reduce_scatter x1 -> x2, waiting for transfers between devices: 41.7 us -> 110 us  [slot_grad(): lax.psum_scatter(slot_dw.reshape(cap * bs, bs), 'dp', scatter_dimension=0...]
    all_gather x1 -> x2, waiting for transfers between devices: 60.8 us -> 118 us  [the longest x1 60.8 us: on_device(): lax.all_gather(gate_slots[0, 0].reshape(per_dev * bs, bs), 'dp', axis=0,...]
    ppermute x20 -> x26, waiting for transfers between devices: 55 us -> 35.6 us  [_shift(): return lax.ppermute(x, axis, perm=[(i, (i + step) % n) for i in range(n)])]
    ppermute x20 -> x26, starting transfers between devices: 31.2 us -> 48.5 us  [_shift(): return lax.ppermute(x, axis, perm=[(i, (i + step) % n) for i in range(n)])]
    dot_general x6 -> x11, matrix products: 25.3 us -> 25.3 us  [the longest x2 7.03 us: pre_rows(): jnp.einsum('qc,qtn->ctn', col_pick.astype(F32), per_slot, precision=high,...]
  transfers between devices with their start and end apart: 22 -> 30, of which waited for: 15 -> 17; matrix products, arithmetic and copies ran while one was open for 6% -> 9% of each run, Pallas kernels for 0% -> 0%
where the time goes in v5:
time: 375 us; the launch traced here: 374 us
  waiting for transfers between devices  265 us (71%)
  starting transfers between devices  48.7 us (13%)
  matrix products  26.1 us (7%)
  between operations  14.3 us (4%)
  other arithmetic  12.8 us (3%)
  local copies, waits for them, and re-layouts  7.4 us (2%)
    reduce_scatter x2, waiting for transfers between devices, slot_grad(): lax.psum_scatter(slot_dw.reshape(cap * bs, bs), 'dp', scatter_dimension=0...  110 us
    all_gather x1, waiting for transfers between devices, on_device(): lax.all_gather(gate_slots[0, 0].reshape(per_dev * bs, bs), 'dp', axis=0,...  60.8 us
    all_gather x1, waiting for transfers between devices, on_device(): lax.all_gather(up_slots[0, 0].reshape(per_dev * bs, bs), 'dp', axis=0, ti...  57.6 us
    ppermute x26, starting transfers between devices, _shift(): return lax.ppermute(x, axis, perm=[(i, (i + step) % n) for i in range(n)])  48.5 us
    ppermute x26, waiting for transfers between devices, _shift(): return lax.ppermute(x, axis, perm=[(i, (i + step) % n) for i in range(n)])  35.6 us
  transfers between devices with their start and end apart: 30, of which 17 were waited for; matrix products, arithmetic and copies ran while one was open for 9% of the time, Pallas kernels for 0%

profile of v5, /device:TPU:2, one launch (start us, length us, event | category | flops | bytes accessed | tf_op | source)
XLA Modules:
  0.0 373.9 jit_solution(405065625400467713)
XLA Ops:
  11.1 5.3 %collective-permute-start.1 = (bf16[24,1024]{1,0:T(8,128)(2,1)S(1)}, bf16[24,1024]{1,0:T(8,128)(2,1)S(1)}, u32[]{:S(2)}, u32[]{:S(2)}) collective-permute-start(bf16[24,1024]{1,0:T(8,128)(2,1)S(1)} %collective-permute-done), channel_id=1, source_target_pairs={{0,7},{1,0},{2,1},{3,2},{4,3},{5,4},{6,5},{7,6},{8,15},{9,8},{10,9... | collective-permute-start | bytes 147464 | tf_op jit(solution)/shard_map/ppermute | solution.py:11
  20.0 3.5 collective-permute-done.5
  23.5 3.5 collective-permute-done.6
  28.9 57.6 %all-gather.3.cloned.1.call-done = bf16[6144,128]{1,0:T(8,128)(2,1)} async-done(((bf16[384,128]{1,0:T(8,128)(2,1)}), bf16[6144,128]{1,0:T(8,128)(2,1)}) %all-gather.3.cloned.1.call-update) | async-done | bytes 1572880 | tf_op jit(solution)/shard_map/all_gather | solution.py:69
  88.7 3.5 fusion.25
  93.3 3.4 collective-permute-start.7
  96.7 60.8 %all-gather.5.cloned.1.call-done = bf16[6144,128]{1,0:T(8,128)(2,1)} async-done(((bf16[384,128]{1,0:T(8,128)(2,1)}), bf16[6144,128]{1,0:T(8,128)(2,1)}) %all-gather.5.cloned.1.call-update) | async-done | bytes 1572880 | tf_op jit(solution)/shard_map/all_gather | solution.py:66
  159.7 3.5 fusion.28
  164.4 3.5 collective-permute-start.10
  167.8 3.6 collective-permute-start.9
  171.4 3.6 collective-permute-start.12
  182.3 2.6 collective-permute-done.8
  184.9 5.3 %collective-permute-done.11 = bf16[14,48,128]{2,0,1:T(8,128)(2,1)} collective-permute-done((bf16[14,48,128]{2,0,1:T(8,128)(2,1)}, bf16[14,48,128]{2,0,1:T(8,128)(2,1)}, u32[]{:S(2)}, u32[]{:S(2)}) %collective-permute-start.11) | collective-permute-done | bytes 172064 | tf_op jit(solution)/shard_map/ppermute | solution.py:11
  196.3 5.1 %collective-permute-start.13 = (bf16[14,48,128]{2,0,1:T(8,128)(2,1)}, bf16[14,48,128]{2,0,1:T(8,128)(2,1)S(1)}, u32[]{:S(2)}, u32[]{:S(2)}) collective-permute-start(bf16[14,48,128]{2,0,1:T(8,128)(2,1)} %get-tuple-element.9), channel_id=1, source_target_pairs={{0,24},{8,0},{16,8},{24,16},{1,25},{9,1},{17,9},{25,17},{2,26},{10... | collective-permute-start | bytes 516104 | tf_op jit(solution)/shard_map/ppermute | solution.py:11
  201.5 3.9 %collective-permute-start.16 = (bf16[14,48,128]{2,0,1:T(8,128)(2,1)}, bf16[14,48,128]{2,0,1:T(8,128)(2,1)S(1)}, u32[]{:S(2)}, u32[]{:S(2)}) collective-permute-start(bf16[14,48,128]{2,0,1:T(8,128)(2,1)} %get-tuple-element.8), channel_id=1, source_target_pairs={{0,24},{8,0},{16,8},{24,16},{1,25},{9,1},{17,9},{25,17},{2,26},{10... | collective-permute-start | bytes 516104 | tf_op jit(solution)/shard_map/ppermute | solution.py:11
  209.3 4.8 %collective-permute-done.15 = bf16[14,48,128]{2,0,1:T(8,128)(2,1)S(1)} collective-permute-done((bf16[14,48,128]{2,0,1:T(8,128)(2,1)S(1)}, bf16[14,48,128]{2,0,1:T(8,128)(2,1)S(1)}, u32[]{:S(2)}, u32[]{:S(2)}) %collective-permute-start.15) | collective-permute-done | bytes 172064 | tf_op jit(solution)/shard_map/ppermute | solution.py:11
  217.0 3.6 fusion.37
  228.6 2.9 fusion.11
  232.7 3.4 fusion.31
  236.3 3.5 collective-permute-done.19
  243.4 3.5 collective-permute-done.21
  249.1 3.1 collective-permute-start.25
  254.6 38.0 %reduce-scatter.5.cloned.1.call-done = bf16[384,128]{1,0:T(8,128)(2,1)} async-done(((bf16[6144,128]{1,0:T(8,128)(2,1)}), bf16[384,128]{1,0:T(8,128)(2,1)}) %reduce-scatter.5.cloned.1.call-update) | async-done | bytes 98320 | tf_op jit(solution)/shard_map/reduce_scatter | solution.py:112
  294.2 71.6 %reduce-scatter.3.cloned.1.call-done = bf16[384,128]{1,0:T(8,128)(2,1)} async-done(((bf16[6144,128]{1,0:T(8,128)(2,1)}), bf16[384,128]{1,0:T(8,128)(2,1)}) %reduce-scatter.3.cloned.1.call-update) | async-done | bytes 98320 | tf_op jit(solution)/shard_map/reduce_scatter | solution.py:112
  (117 shorter events, 56.1 us)
Async XLA Ops:
  7.2 79.3 %all-gather.3.cloned.1.call-start = ((), (), s32[]{:S(2)}) async-start(), calls=%async_computation.2 | async-start | bytes 1671168 | tf_op jit(solution)/shard_map/all_gather | solution.py:69
  7.9 149.6 %all-gather.5.cloned.1.call-start = ((), (), s32[]{:S(2)}) async-start(), calls=%async_computation.3 | async-start | bytes 1671168 | tf_op jit(solution)/shard_map/all_gather | solution.py:66
  8.0 8.5 %collective-permute-start.3 = (bf16[24,1024]{1,0:T(8,128)(2,1)}, bf16[24,1024]{1,0:T(8,128)(2,1)S(1)}, u32[]{:S(2)}, u32[]{:S(2)}) collective-permute-start(bf16[24,1024]{1,0:T(8,128)(2,1)} %param.7), channel_id=1, source_target_pairs={{0,1},{1,2},{2,3},{3,4},{4,5},{5,6},{6,7},{7,0},{8,9},{9,10},{10,1... | collective-permute-start | bytes 147464 | tf_op jit(solution)/shard_map/ppermute | solution.py:11
  8.6 284.0 %reduce-scatter.5.cloned.1.call-start = ((), (), s32[]{:S(2)}) async-start(), calls=%async_computation.5 | async-start | bytes 1671168 | tf_op jit(solution)/shard_map/reduce_scatter | solution.py:112
  11.1 7.1 %collective-permute-start.1 = (bf16[24,1024]{1,0:T(8,128)(2,1)S(1)}, bf16[24,1024]{1,0:T(8,128)(2,1)S(1)}, u32[]{:S(2)}, u32[]{:S(2)}) collective-permute-start(bf16[24,1024]{1,0:T(8,128)(2,1)S(1)} %collective-permute-done), channel_id=1, source_target_pairs={{0,7},{1,0},{2,1},{3,2},{4,3},{5,4},{6,5},{7,6},{8,15},{9,8},{10,9... | collective-permute-start | bytes 147464 | tf_op jit(solution)/shard_map/ppermute | solution.py:11
  18.2 5.3 %collective-permute-start.2 = (bf16[24,1024]{1,0:T(8,128)(2,1)S(1)}, bf16[24,1024]{1,0:T(8,128)(2,1)S(1)}, u32[]{:S(2)}, u32[]{:S(2)}) collective-permute-start(bf16[24,1024]{1,0:T(8,128)(2,1)S(1)} %collective-permute-done.1), channel_id=1, source_target_pairs={{0,7},{1,0},{2,1},{3,2},{4,3},{5,4},{6,5},{7,6},{8,15},{9,8},{10,9... | collective-permute-start | bytes 147464 | tf_op jit(solution)/shard_map/ppermute | solution.py:11
  93.3 81.8 %collective-permute-start.7 = (bf16[14,48,128]{2,0,1:T(8,128)(2,1)S(1)}, bf16[14,48,128]{2,0,1:T(8,128)(2,1)S(1)}, u32[]{:S(2)}, u32[]{:S(2)}) collective-permute-start(bf16[14,48,128]{2,0,1:T(8,128)(2,1)S(1)} %get-tuple-element.12), channel_id=1, source_target_pairs={{0,8},{8,16},{16,24},{24,0},{1,9},{9,17},{17,25},{25,1},{2,10},{10... | collective-permute-start | bytes 516104 | tf_op jit(solution)/shard_map/ppermute | solution.py:11
  164.4 13.8 %collective-permute-start.10 = (bf16[14,48,128]{2,0,1:T(8,128)(2,1)S(1)}, bf16[14,48,128]{2,0,1:T(8,128)(2,1)S(1)}, u32[]{:S(2)}, u32[]{:S(2)}) collective-permute-start(bf16[14,48,128]{2,0,1:T(8,128)(2,1)S(1)} %get-tuple-element.10), channel_id=1, source_target_pairs={{0,8},{8,16},{16,24},{24,0},{1,9},{9,17},{17,25},{25,1},{2,10},{10... | collective-permute-start | bytes 516104 | tf_op jit(solution)/shard_map/ppermute | solution.py:11
  167.8 14.4 %collective-permute-start.9 = (bf16[14,48,128]{2,0,1:T(8,128)(2,1)}, bf16[14,48,128]{2,0,1:T(8,128)(2,1)}, u32[]{:S(2)}, u32[]{:S(2)}) collective-permute-start(bf16[14,48,128]{2,0,1:T(8,128)(2,1)} %get-tuple-element.13), channel_id=1, source_target_pairs={{0,24},{8,0},{16,8},{24,16},{1,25},{9,1},{17,9},{25,17},{2,26},{10... | collective-permute-start | bytes 516104 | tf_op jit(solution)/shard_map/ppermute | solution.py:11
  171.4 10.9 %collective-permute-start.12 = (bf16[14,48,128]{2,0,1:T(8,128)(2,1)}, bf16[14,48,128]{2,0,1:T(8,128)(2,1)}, u32[]{:S(2)}, u32[]{:S(2)}) collective-permute-start(bf16[14,48,128]{2,0,1:T(8,128)(2,1)} %get-tuple-element.11), channel_id=1, source_target_pairs={{0,24},{8,0},{16,8},{24,16},{1,25},{9,1},{17,9},{25,17},{2,26},{10... | collective-permute-start | bytes 516104 | tf_op jit(solution)/shard_map/ppermute | solution.py:11
  175.8 9.1 %collective-permute-start.8 = (bf16[14,48,128]{2,0,1:T(8,128)(2,1)}, bf16[14,48,128]{2,0,1:T(8,128)(2,1)}, u32[]{:S(2)}, u32[]{:S(2)}) collective-permute-start(bf16[14,48,128]{2,0,1:T(8,128)(2,1)} %fusion.58), channel_id=1, source_target_pairs={{0,8},{8,16},{16,24},{24,0},{1,9},{9,17},{17,25},{25,1},{2,10},{10... | collective-permute-start | bytes 516104 | tf_op jit(solution)/shard_map/ppermute | solution.py:11
  179.0 11.2 %collective-permute-start.11 = (bf16[14,48,128]{2,0,1:T(8,128)(2,1)}, bf16[14,48,128]{2,0,1:T(8,128)(2,1)}, u32[]{:S(2)}, u32[]{:S(2)}) collective-permute-start(bf16[14,48,128]{2,0,1:T(8,128)(2,1)} %fusion.52), channel_id=1, source_target_pairs={{0,8},{8,16},{16,24},{24,0},{1,9},{9,17},{17,25},{25,1},{2,10},{10... | collective-permute-start | bytes 516104 | tf_op jit(solution)/shard_map/ppermute | solution.py:11
  192.5 12.9 %collective-permute-start.14 = (bf16[14,48,128]{2,0,1:T(8,128)(2,1)}, bf16[14,48,128]{2,0,1:T(8,128)(2,1)S(1)}, u32[]{:S(2)}, u32[]{:S(2)}) collective-permute-start(bf16[14,48,128]{2,0,1:T(8,128)(2,1)} %get-tuple-element.9), channel_id=1, source_target_pairs={{0,8},{8,16},{16,24},{24,0},{1,9},{9,17},{17,25},{25,1},{2,10},{10... | collective-permute-start | bytes 516104 | tf_op jit(solution)/shard_map/ppermute | solution.py:11
  194.4 12.9 %collective-permute-start.17 = (bf16[14,48,128]{2,0,1:T(8,128)(2,1)}, bf16[14,48,128]{2,0,1:T(8,128)(2,1)S(1)}, u32[]{:S(2)}, u32[]{:S(2)}) collective-permute-start(bf16[14,48,128]{2,0,1:T(8,128)(2,1)} %get-tuple-element.8), channel_id=1, source_target_pairs={{0,8},{8,16},{16,24},{24,0},{1,9},{9,17},{17,25},{25,1},{2,10},{10... | collective-permute-start | bytes 516104 | tf_op jit(solution)/shard_map/ppermute | solution.py:11
  196.3 13.0 %collective-permute-start.13 = (bf16[14,48,128]{2,0,1:T(8,128)(2,1)}, bf16[14,48,128]{2,0,1:T(8,128)(2,1)S(1)}, u32[]{:S(2)}, u32[]{:S(2)}) collective-permute-start(bf16[14,48,128]{2,0,1:T(8,128)(2,1)} %get-tuple-element.9), channel_id=1, source_target_pairs={{0,24},{8,0},{16,8},{24,16},{1,25},{9,1},{17,9},{25,17},{2,26},{10... | collective-permute-start | bytes 516104 | tf_op jit(solution)/shard_map/ppermute | solution.py:11
  201.5 7.8 %collective-permute-start.16 = (bf16[14,48,128]{2,0,1:T(8,128)(2,1)}, bf16[14,48,128]{2,0,1:T(8,128)(2,1)S(1)}, u32[]{:S(2)}, u32[]{:S(2)}) collective-permute-start(bf16[14,48,128]{2,0,1:T(8,128)(2,1)} %get-tuple-element.8), channel_id=1, source_target_pairs={{0,24},{8,0},{16,8},{24,16},{1,25},{9,1},{17,9},{25,17},{2,26},{10... | collective-permute-start | bytes 516104 | tf_op jit(solution)/shard_map/ppermute | solution.py:11
  205.4 8.8 %collective-permute-start.15 = (bf16[14,48,128]{2,0,1:T(8,128)(2,1)S(1)}, bf16[14,48,128]{2,0,1:T(8,128)(2,1)S(1)}, u32[]{:S(2)}, u32[]{:S(2)}) collective-permute-start(bf16[14,48,128]{2,0,1:T(8,128)(2,1)S(1)} %collective-permute-done.14), channel_id=1, source_target_pairs={{0,8},{8,16},{16,24},{24,0},{1,9},{9,17},{17,25},{25,1},{2,10},{10... | collective-permute-start | bytes 516104 | tf_op jit(solution)/shard_map/ppermute | solution.py:11
  207.4 8.9 %collective-permute-start.18 = (bf16[14,48,128]{2,0,1:T(8,128)(2,1)S(1)}, bf16[14,48,128]{2,0,1:T(8,128)(2,1)S(1)}, u32[]{:S(2)}, u32[]{:S(2)}) collective-permute-start(bf16[14,48,128]{2,0,1:T(8,128)(2,1)S(1)} %collective-permute-done.17), channel_id=1, source_target_pairs={{0,8},{8,16},{16,24},{24,0},{1,9},{9,17},{17,25},{25,1},{2,10},{10... | collective-permute-start | bytes 516104 | tf_op jit(solution)/shard_map/ppermute | solution.py:11
  223.9 141.8 %reduce-scatter.3.cloned.1.call-start = ((), (), s32[]{:S(2)}) async-start(), calls=%async_computation.4 | async-start | bytes 1671168 | tf_op jit(solution)/shard_map/reduce_scatter | solution.py:112
  236.3 3.5 collective-permute-start.19
  239.9 3.5 collective-permute-start.20
  239.9 3.5 collective-permute-start.23
  247.3 5.8 %collective-permute-start.22 = (bf16[8,24,128]{2,0,1:T(8,128)(2,1)S(1)}, bf16[8,24,128]{2,0,1:T(8,128)(2,1)S(1)}, u32[]{:S(2)}, u32[]{:S(2)}) collective-permute-start(bf16[8,24,128]{2,0,1:T(8,128)(2,1)S(1)} %get-tuple-element.14), channel_id=1, source_target_pairs={{0,1},{1,2},{2,3},{3,4},{4,5},{5,6},{6,7},{7,0},{8,9},{9,10},{10,1... | collective-permute-start | bytes 147464 | tf_op jit(solution)/shard_map/ppermute | solution.py:11
  249.1 4.9 %collective-permute-start.25 = (bf16[8,24,128]{2,0,1:T(8,128)(2,1)S(1)}, bf16[8,24,128]{2,0,1:T(8,128)(2,1)S(1)}, u32[]{:S(2)}, u32[]{:S(2)}) collective-permute-start(bf16[8,24,128]{2,0,1:T(8,128)(2,1)S(1)} %fusion.61), channel_id=1, source_target_pairs={{0,7},{1,0},{2,1},{3,2},{4,3},{5,4},{6,5},{7,6},{8,15},{9,8},{10,9... | collective-permute-start | bytes 147464 | tf_op jit(solution)/shard_map/ppermute | solution.py:11
  (16 other events, 62.9 us)
Sparse Core Ops, SparseCore 0:
  10.0 76.3 all-gather.2
  88.6 68.9 all-gather.4
  224.1 68.5 reduce-scatter.4
  295.3 70.4 reduce-scatter.2

commit v6 on v4

--- a/solution.py
+++ b/solution.py
@@ -45,6 +45,38 @@
     return fwd + bwd.astype(F32)
 
 
+def _halves(x, half):
+    return x[..., :half], x[..., half:]
+
+
+def ring4_gather(x, axis, half):
+    n = 4
+    from_left = _shift(x, axis, n, 1)
+    from_right = _shift(x, axis, n, -1)
+    far_a = _shift(_halves(from_left, half)[0], axis, n, 1)
+    far_b = _shift(_halves(from_right, half)[1], axis, n, -1)
+    return [x, from_right, jnp.concatenate([far_a, far_b], axis=-1), from_left]
+
+
+def ring4_sum_scatter(parts, axis, half):
+    n = 4
+    own_a, own_b = _halves(parts[0], half)
+    next_a, next_b = _halves(parts[1], half)
+    far_a, far_b = _halves(parts[2], half)
+    prev_a, prev_b = _halves(parts[3], half)
+    got_left = _shift(jnp.concatenate([far_a, next_b], axis=-1), axis, n, 1)
+    got_right = _shift(jnp.concatenate([prev_a, far_b], axis=-1), axis, n, -1)
+    left_a, left_b = _halves(got_left, half)
+    right_a, right_b = _halves(got_right, half)
+    send_a = (left_a.astype(F32) + next_a.astype(F32)).astype(BF16)
+    send_b = (right_b.astype(F32) + prev_b.astype(F32)).astype(BF16)
+    two_left = _shift(send_a, axis, n, 1)
+    two_right = _shift(send_b, axis, n, -1)
+    total_a = own_a.astype(F32) + two_left.astype(F32) + right_a.astype(F32)
+    total_b = own_b.astype(F32) + two_right.astype(F32) + left_b.astype(F32)
+    return jnp.concatenate([total_a, total_b], axis=-1)
+
+
 def on_device(layer_input, hidden_grad, gate_slots, up_slots, block_mask):
     n_dp = lax.axis_size("dp")
     n_row = lax.axis_size("row")
@@ -80,7 +112,7 @@
     onehot3 = picks.astype(BF16).reshape(cap, tile_rows, tile_cols)
     row_pick = jnp.sum(onehot3, axis=2)
     col_pick = jnp.sum(onehot3, axis=1)
-    highest = lax.Precision.HIGHEST
+    highest = lax.Precision.HIGH
 
     x_pick = jnp.einsum("qr,trk->qtk", row_pick, x_abs, preferred_element_type=F32).astype(BF16)
     per_slot = jnp.einsum("qtk,qkn->qtn", x_pick, pair_all, preferred_element_type=F32)
@@ -88,7 +120,10 @@
         "qc,qtn->ctn", col_pick.astype(F32), per_slot, precision=highest, preferred_element_type=F32
     ).astype(BF16)
     pre_roll = jnp.roll(pre.reshape(tile_cols, n_row, rows_per, 2 * bs), -k_row, axis=1)
-    pre_sum = ring_sum_scatter([pre_roll[:, m] for m in range(n_row)], "row", n_row)
+    if n_row == 4:
+        pre_sum = ring4_sum_scatter([pre_roll[:, m] for m in range(n_row)], "row", bs)
+    else:
+        pre_sum = ring_sum_scatter([pre_roll[:, m] for m in range(n_row)], "row", n_row)
     gate = pre_sum[..., :bs]
     up = pre_sum[..., bs:]
     upstream = hidden_grad.astype(F32).reshape(rows_per, tile_cols, bs).transpose(1, 0, 2)
@@ -96,7 +131,10 @@
     gate_grad = (upstream * up * sig * (1.0 + gate * (1.0 - sig))).astype(BF16)
     up_grad = (upstream * gate * sig).astype(BF16)
     grad_local = jnp.concatenate([gate_grad, up_grad], axis=2)
-    grad_rel = jnp.stack(ring_gather(grad_local, "row", n_row), axis=1)
+    if n_row == 4:
+        grad_rel = jnp.stack(ring4_gather(grad_local, "row", bs), axis=1)
+    else:
+        grad_rel = jnp.stack(ring_gather(grad_local, "row", n_row), axis=1)
     grad_abs = jnp.roll(grad_rel, k_row, axis=1).reshape(tile_cols, tok, 2 * bs)
 
     g_pick = jnp.einsum("qc,ctn->qtn", col_pick, grad_abs, preferred_element_type=F32).astype(BF16)

time: 247 us -> 246 us (level)
  waiting for transfers between devices: 157 us -> 146 us
  starting transfers between devices: 31.2 us -> 42.1 us
  matrix products: 26.2 us -> 23.5 us
    ppermute x20 -> x22, waiting for transfers between devices: 55 us -> 38.5 us  [_shift(): return lax.ppermute(x, axis, perm=[(i, (i + step) % n) for i in range(n)])]
    ppermute x20 -> x22, starting transfers between devices: 31.2 us -> 42 us  [_shift(): return lax.ppermute(x, axis, perm=[(i, (i + step) % n) for i in range(n)])]
    reduce_scatter x1, waiting for transfers between devices: 41.7 us -> 46.3 us  [on_device(): lax.psum_scatter(slot_dw.reshape(cap * bs, 2 * bs), 'dp', scatter_dimensi...]
  transfers between devices with their start and end apart: 22 -> 24, of which waited for: 15 -> 17; matrix products, arithmetic and copies ran while one was open for 6% -> 7% of each run, Pallas kernels for 0% -> 0%
where the time goes in v6:
time: 246 us; the launch traced here: 245 us
  waiting for transfers between devices  146 us (59%)
  starting transfers between devices  42.1 us (17%)
  matrix products  23.5 us (10%)
  between operations  14.5 us (6%)
  other arithmetic  11.2 us (5%)
  local copies, waits for them, and re-layouts  8.11 us (3%)
    all_gather x1, waiting for transfers between devices, on_device(): lax.all_gather(pair_local, 'dp', axis=0, tiled=True)  60.8 us
    reduce_scatter x1, waiting for transfers between devices, on_device(): lax.psum_scatter(slot_dw.reshape(cap * bs, 2 * bs), 'dp', scatter_dimensi...  46.3 us
    ppermute x22, starting transfers between devices, _shift(): return lax.ppermute(x, axis, perm=[(i, (i + step) % n) for i in range(n)])  42 us
    ppermute x22, waiting for transfers between devices, _shift(): return lax.ppermute(x, axis, perm=[(i, (i + step) % n) for i in range(n)])  38.5 us
    dot_general x1, matrix products, on_device(): jnp.einsum('qc,qtn->ctn', col_pick.astype(F32), per_slot, precision=highe...  6.91 us
  transfers between devices with their start and end apart: 24, of which 17 were waited for; matrix products, arithmetic and copies ran while one was open for 7% of the time, Pallas kernels for 0%

profile of v6, /device:TPU:2, one launch (start us, length us, event | category | flops | bytes accessed | tf_op | source)
XLA Modules:
  0.0 245.0 jit_solution(12492038843388178673)
XLA Ops:
  11.8 5.5 %collective-permute-start.1 = (bf16[24,1024]{1,0:T(8,128)(2,1)S(1)}, bf16[24,1024]{1,0:T(8,128)(2,1)S(1)}, u32[]{:S(2)}, u32[]{:S(2)}) collective-permute-start(bf16[24,1024]{1,0:T(8,128)(2,1)S(1)} %collective-permute-done), channel_id=1, source_target_pairs={{0,7},{1,0},{2,1},{3,2},{4,3},{5,4},{6,5},{7,6},{8,15},{9,8},{10,9... | collective-permute-start | bytes 147464 | tf_op jit(solution)/shard_map/ppermute | solution.py:11
  20.9 3.5 %collective-permute-done.5 = bf16[24,1024]{1,0:T(8,128)(2,1)S(1)} collective-permute-done((bf16[24,1024]{1,0:T(8,128)(2,1)S(1)}, bf16[24,1024]{1,0:T(8,128)(2,1)S(1)}, u32[]{:S(2)}, u32[]{:S(2)}) %collective-permute-start.5) | collective-permute-done | bytes 49184 | tf_op jit(solution)/shard_map/ppermute | solution.py:11
  24.4 3.5 %collective-permute-done.6 = bf16[24,1024]{1,0:T(8,128)(2,1)S(1)} collective-permute-done((bf16[24,1024]{1,0:T(8,128)(2,1)S(1)}, bf16[24,1024]{1,0:T(8,128)(2,1)S(1)}, u32[]{:S(2)}, u32[]{:S(2)}) %collective-permute-start.6) | collective-permute-done | bytes 49184 | tf_op jit(solution)/shard_map/ppermute | solution.py:11
  29.8 60.8 %all-gather.2.cloned.1.call-done = bf16[6144,256]{1,0:T(8,128)(2,1)} async-done(((bf16[384,256]{1,0:T(8,128)(2,1)}), bf16[6144,256]{1,0:T(8,128)(2,1)}) %all-gather.2.cloned.1.call-update) | async-done | bytes 3145744 | tf_op jit(solution)/shard_map/all_gather | solution.py:100
  90.5 3.3 %fusion.12 = f32[48,192,256]{2,1,0:T(8,128)S(1)} fusion(bf16[48,128,256]{2,1,0:T(8,128)(2,1)} %bitcast.119, bf16[48,192,128]{2,0,1:T(8,128)(2,1)S(1)} %convolution_convert_fusion.1), kind=kOutput, calls=%fused_computation.21 | convolution fusion | flops 603979776 | bytes 14942208 | tf_op jit(solution)/shard_map/qtk,qkn->qtn/dot_general | solution.py:118
  93.8 6.9 %fusion.14 = bf16[14,192,256]{2,0,1:T(8,128)(2,1)S(1)} fusion(f32[48,192,256]{2,1,0:T(8,128)S(1)} %fusion.12, bf16[48,14]{0,1:T(8,128)(2,1)S(1)} %get-tuple-element.4), kind=kOutput, calls=%fused_computation.24 | convolution fusion | flops 198868992 | bytes 10814784 | tf_op jit(solution)/shard_map/qc,qtn->ctn/dot_general | solution.py:119
  101.7 3.4 %collective-permute-start.9 = (bf16[14,48,256]{2,0,1:T(8,128)(2,1)S(1)}, bf16[14,48,256]{2,0,1:T(8,128)(2,1)S(1)}, u32[]{:S(2)}, u32[]{:S(2)}) collective-permute-start(bf16[14,48,256]{2,0,1:T(8,128)(2,1)S(1)} %pad_maximum_fusion.1), channel_id=1, source_target_pairs={{0,8},{8,16},{16,24},{24,0},{1,9},{9,17},{17,25},{25,1},{2,10},{10... | collective-permute-start | bytes 1032200 | tf_op jit(solution)/shard_map/ppermute | solution.py:11
  105.2 3.7 %collective-permute-start.7 = (bf16[14,48,256]{2,0,1:T(8,128)(2,1)S(1)}, bf16[14,48,256]{2,0,1:T(8,128)(2,1)S(1)}, u32[]{:S(2)}, u32[]{:S(2)}) collective-permute-start(bf16[14,48,256]{2,0,1:T(8,128)(2,1)S(1)} %pad_maximum_fusion), channel_id=1, source_target_pairs={{0,24},{8,0},{16,8},{24,16},{1,25},{9,1},{17,9},{25,17},{2,26},{10... | collective-permute-start | bytes 1032200 | tf_op jit(solution)/shard_map/ppermute | solution.py:11
  108.9 5.8 %collective-permute-done.9 = bf16[14,48,256]{2,0,1:T(8,128)(2,1)S(1)} collective-permute-done((bf16[14,48,256]{2,0,1:T(8,128)(2,1)S(1)}, bf16[14,48,256]{2,0,1:T(8,128)(2,1)S(1)}, u32[]{:S(2)}, u32[]{:S(2)}) %collective-permute-start.9) | collective-permute-done | bytes 344096 | tf_op jit(solution)/shard_map/ppermute | solution.py:11
  115.4 2.1 collective-permute-start.10
  118.3 5.1 %collective-permute-start.8 = (bf16[14,48,128]{2,0,1:T(8,128)(2,1)}, bf16[14,48,128]{2,0,1:T(8,128)(2,1)}, u32[]{:S(2)}, u32[]{:S(2)}) collective-permute-start(bf16[14,48,128]{2,0,1:T(8,128)(2,1)} %add_convert_fusion.1), channel_id=1, source_target_pairs={{0,24},{8,0},{16,8},{24,16},{1,25},{9,1},{17,9},{25,17},{2,26},{10... | collective-permute-start | bytes 516104 | tf_op jit(solution)/shard_map/ppermute | solution.py:11
  125.6 3.5 %collective-permute-done.8 = bf16[14,48,128]{2,0,1:T(8,128)(2,1)} collective-permute-done((bf16[14,48,128]{2,0,1:T(8,128)(2,1)}, bf16[14,48,128]{2,0,1:T(8,128)(2,1)}, u32[]{:S(2)}, u32[]{:S(2)}) %collective-permute-start.8) | collective-permute-done | bytes 172064 | tf_op jit(solution)/shard_map/ppermute | solution.py:11
  132.5 5.6 %collective-permute-start.11 = (bf16[14,48,256]{2,0,1:T(8,128)(2,1)S(1)}, bf16[14,48,256]{2,0,1:T(8,128)(2,1)S(1)}, u32[]{:S(2)}, u32[]{:S(2)}) collective-permute-start(bf16[14,48,256]{2,0,1:T(8,128)(2,1)S(1)} %get-tuple-element.20), channel_id=1, source_target_pairs={{0,24},{8,0},{16,8},{24,16},{1,25},{9,1},{17,9},{25,17},{2,26},{10... | collective-permute-start | bytes 1032200 | tf_op jit(solution)/shard_map/ppermute | solution.py:11
  138.1 3.8 %collective-permute-done.12 = bf16[14,48,256]{2,0,1:T(8,128)(2,1)S(1)} collective-permute-done((bf16[14,48,256]{2,0,1:T(8,128)(2,1)S(1)}, bf16[14,48,256]{2,0,1:T(8,128)(2,1)S(1)}, u32[]{:S(2)}, u32[]{:S(2)}) %collective-permute-start.12) | collective-permute-done | bytes 344096 | tf_op jit(solution)/shard_map/ppermute | solution.py:11
  145.3 5.1 %collective-permute-start.14 = (bf16[14,48,128]{2,0,1:T(8,128)(2,1)}, bf16[14,48,128]{2,0,1:T(8,128)(2,1)}, u32[]{:S(2)}, u32[]{:S(2)}) collective-permute-start(bf16[14,48,128]{2,0,1:T(8,128)(2,1)} %slice.129), channel_id=1, source_target_pairs={{0,24},{8,0},{16,8},{24,16},{1,25},{9,1},{17,9},{25,17},{2,26},{10... | collective-permute-start | bytes 516104 | tf_op jit(solution)/shard_map/ppermute | solution.py:11
  151.7 2.2 collective-permute-done.14
  155.0 2.2 fusion.20
  158.6 3.6 %fusion.8 = bf16[48,128,256]{2,1,0:T(8,128)(2,1)} fusion(bf16[48,192,256]{2,0,1:T(8,128)(2,1)S(1)} %convolution_convert_fusion, bf16[48,192,128]{2,0,1:T(8,128)(2,1)S(1)} %convolution_convert_fusion.1), kind=kOutput, calls=%fused_computation.19 | convolution fusion | flops 605552640 | bytes 10223616 | tf_op jit(solution)/shard_map/qtk,qtn->qkn/dot_general | solution.py:141
  164.1 4.1 %fusion.6 = f32[48,192,128]{2,1,0:T(8,128)S(1)} fusion(bf16[48,128,256]{2,1,0:T(8,128)(2,1)S(1)} %bitcast.120, bf16[48,192,256]{2,0,1:T(8,128)(2,1)} %copy-done), kind=kOutput, calls=%fused_computation.6 | convolution fusion | flops 603979776 | bytes 12582912 | tf_op jit(solution)/shard_map/qtn,qkn->qtk/dot_general | solution.py:143
  168.2 3.4 %fusion.25 = bf16[8,192,128]{2,0,1:T(8,128)(2,1)S(1)} fusion(f32[48,192,128]{2,1,0:T(8,128)S(1)} %fusion.6, bf16[48,8]{0,1:T(8,128)(2,1)S(1)} %get-tuple-element.5), kind=kOutput, calls=%fused_computation.33 | convolution fusion | flops 56819712 | bytes 5112576 | tf_op jit(solution)/shard_map/qr,qtk->rtk/dot_general | solution.py:144
  171.9 3.5 %collective-permute-done.15 = bf16[8,24,128]{2,0,1:T(8,128)(2,1)S(1)} collective-permute-done((bf16[8,24,128]{2,0,1:T(8,128)(2,1)S(1)}, bf16[8,24,128]{2,0,1:T(8,128)(2,1)S(1)}, u32[]{:S(2)}, u32[]{:S(2)}) %collective-permute-start.15) | collective-permute-done | bytes 49184 | tf_op jit(solution)/shard_map/ppermute | solution.py:11
  179.0 3.5 %collective-permute-done.17 = bf16[8,24,128]{2,0,1:T(8,128)(2,1)S(1)} collective-permute-done((bf16[8,24,128]{2,0,1:T(8,128)(2,1)S(1)}, bf16[8,24,128]{2,0,1:T(8,128)(2,1)S(1)}, u32[]{:S(2)}, u32[]{:S(2)}) %collective-permute-start.17) | collective-permute-done | bytes 49184 | tf_op jit(solution)/shard_map/ppermute | solution.py:11
  184.6 3.1 %collective-permute-start.21 = (bf16[8,24,128]{2,0,1:T(8,128)(2,1)S(1)}, bf16[8,24,128]{2,0,1:T(8,128)(2,1)S(1)}, u32[]{:S(2)}, u32[]{:S(2)}) collective-permute-start(bf16[8,24,128]{2,0,1:T(8,128)(2,1)S(1)} %fusion.34), channel_id=1, source_target_pairs={{0,7},{1,0},{2,1},{3,2},{4,3},{5,4},{6,5},{7,6},{8,15},{9,8},{10,9... | collective-permute-start | bytes 147464 | tf_op jit(solution)/shard_map/ppermute | solution.py:11
  190.2 46.3 %reduce-scatter.2.cloned.1.call-done = bf16[384,256]{1,0:T(8,128)(2,1)} async-done(((bf16[6144,256]{1,0:T(8,128)(2,1)}), bf16[384,256]{1,0:T(8,128)(2,1)}) %reduce-scatter.2.cloned.1.call-update) | async-done | bytes 196624 | tf_op jit(solution)/shard_map/reduce_scatter | solution.py:151
  (92 shorter events, 37.0 us)
Async XLA Ops:
  7.2 83.4 %all-gather.2.cloned.1.call-start = ((), (), s32[]{:S(2)}) async-start(), calls=%async_computation.1 | async-start | bytes 3342336 | tf_op jit(solution)/shard_map/all_gather | solution.py:100
  8.9 227.6 %reduce-scatter.2.cloned.1.call-start = ((), (), s32[]{:S(2)}) async-start(), calls=%async_computation.2 | async-start | bytes 3342336 | tf_op jit(solution)/shard_map/reduce_scatter | solution.py:151
  8.9 2.9 %collective-permute-start = (bf16[24,1024]{1,0:T(8,128)(2,1)}, bf16[24,1024]{1,0:T(8,128)(2,1)S(1)}, u32[]{:S(2)}, u32[]{:S(2)}) collective-permute-start(bf16[24,1024]{1,0:T(8,128)(2,1)} %param.7), channel_id=1, source_target_pairs={{0,7},{1,0},{2,1},{3,2},{4,3},{5,4},{6,5},{7,6},{8,15},{9,8},{10,9... | collective-permute-start | bytes 147464 | tf_op jit(solution)/shard_map/ppermute | solution.py:11
  9.0 8.4 %collective-permute-start.3 = (bf16[24,1024]{1,0:T(8,128)(2,1)}, bf16[24,1024]{1,0:T(8,128)(2,1)S(1)}, u32[]{:S(2)}, u32[]{:S(2)}) collective-permute-start(bf16[24,1024]{1,0:T(8,128)(2,1)} %param.7), channel_id=1, source_target_pairs={{0,1},{1,2},{2,3},{3,4},{4,5},{5,6},{6,7},{7,0},{8,9},{9,10},{10,1... | collective-permute-start | bytes 147464 | tf_op jit(solution)/shard_map/ppermute | solution.py:11
  11.8 7.3 %collective-permute-start.1 = (bf16[24,1024]{1,0:T(8,128)(2,1)S(1)}, bf16[24,1024]{1,0:T(8,128)(2,1)S(1)}, u32[]{:S(2)}, u32[]{:S(2)}) collective-permute-start(bf16[24,1024]{1,0:T(8,128)(2,1)S(1)} %collective-permute-done), channel_id=1, source_target_pairs={{0,7},{1,0},{2,1},{3,2},{4,3},{5,4},{6,5},{7,6},{8,15},{9,8},{10,9... | collective-permute-start | bytes 147464 | tf_op jit(solution)/shard_map/ppermute | solution.py:11
  17.3 3.5 %collective-permute-start.4 = (bf16[24,1024]{1,0:T(8,128)(2,1)S(1)}, bf16[24,1024]{1,0:T(8,128)(2,1)S(1)}, u32[]{:S(2)}, u32[]{:S(2)}) collective-permute-start(bf16[24,1024]{1,0:T(8,128)(2,1)S(1)} %collective-permute-done.3), channel_id=1, source_target_pairs={{0,1},{1,2},{2,3},{3,4},{4,5},{5,6},{6,7},{7,0},{8,9},{9,10},{10,1... | collective-permute-start | bytes 147464 | tf_op jit(solution)/shard_map/ppermute | solution.py:11
  19.1 5.3 %collective-permute-start.2 = (bf16[24,1024]{1,0:T(8,128)(2,1)S(1)}, bf16[24,1024]{1,0:T(8,128)(2,1)S(1)}, u32[]{:S(2)}, u32[]{:S(2)}) collective-permute-start(bf16[24,1024]{1,0:T(8,128)(2,1)S(1)} %collective-permute-done.1), channel_id=1, source_target_pairs={{0,7},{1,0},{2,1},{3,2},{4,3},{5,4},{6,5},{7,6},{8,15},{9,8},{10,9... | collective-permute-start | bytes 147464 | tf_op jit(solution)/shard_map/ppermute | solution.py:11
  20.9 3.5 %collective-permute-start.5 = (bf16[24,1024]{1,0:T(8,128)(2,1)S(1)}, bf16[24,1024]{1,0:T(8,128)(2,1)S(1)}, u32[]{:S(2)}, u32[]{:S(2)}) collective-permute-start(bf16[24,1024]{1,0:T(8,128)(2,1)S(1)} %collective-permute-done.4), channel_id=1, source_target_pairs={{0,1},{1,2},{2,3},{3,4},{4,5},{5,6},{6,7},{7,0},{8,9},{9,10},{10,1... | collective-permute-start | bytes 147464 | tf_op jit(solution)/shard_map/ppermute | solution.py:11
  24.4 3.5 %collective-permute-start.6 = (bf16[24,1024]{1,0:T(8,128)(2,1)S(1)}, bf16[24,1024]{1,0:T(8,128)(2,1)S(1)}, u32[]{:S(2)}, u32[]{:S(2)}) collective-permute-start(bf16[24,1024]{1,0:T(8,128)(2,1)S(1)} %collective-permute-done.5), channel_id=1, source_target_pairs={{0,1},{1,2},{2,3},{3,4},{4,5},{5,6},{6,7},{7,0},{8,9},{9,10},{10,1... | collective-permute-start | bytes 147464 | tf_op jit(solution)/shard_map/ppermute | solution.py:11
  101.7 13.0 %collective-permute-start.9 = (bf16[14,48,256]{2,0,1:T(8,128)(2,1)S(1)}, bf16[14,48,256]{2,0,1:T(8,128)(2,1)S(1)}, u32[]{:S(2)}, u32[]{:S(2)}) collective-permute-start(bf16[14,48,256]{2,0,1:T(8,128)(2,1)S(1)} %pad_maximum_fusion.1), channel_id=1, source_target_pairs={{0,8},{8,16},{16,24},{24,0},{1,9},{9,17},{17,25},{25,1},{2,10},{10... | collective-permute-start | bytes 1032200 | tf_op jit(solution)/shard_map/ppermute | solution.py:11
  105.2 12.3 %collective-permute-start.7 = (bf16[14,48,256]{2,0,1:T(8,128)(2,1)S(1)}, bf16[14,48,256]{2,0,1:T(8,128)(2,1)S(1)}, u32[]{:S(2)}, u32[]{:S(2)}) collective-permute-start(bf16[14,48,256]{2,0,1:T(8,128)(2,1)S(1)} %pad_maximum_fusion), channel_id=1, source_target_pairs={{0,24},{8,0},{16,8},{24,16},{1,25},{9,1},{17,9},{25,17},{2,26},{10... | collective-permute-start | bytes 1032200 | tf_op jit(solution)/shard_map/ppermute | solution.py:11
  115.4 10.1 %collective-permute-start.10 = (bf16[14,48,128]{2,0,1:T(8,128)(2,1)}, bf16[14,48,128]{2,0,1:T(8,128)(2,1)}, u32[]{:S(2)}, u32[]{:S(2)}) collective-permute-start(bf16[14,48,128]{2,0,1:T(8,128)(2,1)} %add_convert_fusion), channel_id=1, source_target_pairs={{0,8},{8,16},{16,24},{24,0},{1,9},{9,17},{17,25},{25,1},{2,10},{10... | collective-permute-start | bytes 516104 | tf_op jit(solution)/shard_map/ppermute | solution.py:11
  118.3 10.7 %collective-permute-start.8 = (bf16[14,48,128]{2,0,1:T(8,128)(2,1)}, bf16[14,48,128]{2,0,1:T(8,128)(2,1)}, u32[]{:S(2)}, u32[]{:S(2)}) collective-permute-start(bf16[14,48,128]{2,0,1:T(8,128)(2,1)} %add_convert_fusion.1), channel_id=1, source_target_pairs={{0,24},{8,0},{16,8},{24,16},{1,25},{9,1},{17,9},{25,17},{2,26},{10... | collective-permute-start | bytes 516104 | tf_op jit(solution)/shard_map/ppermute | solution.py:11
  130.6 11.3 %collective-permute-start.12 = (bf16[14,48,256]{2,0,1:T(8,128)(2,1)S(1)}, bf16[14,48,256]{2,0,1:T(8,128)(2,1)S(1)}, u32[]{:S(2)}, u32[]{:S(2)}) collective-permute-start(bf16[14,48,256]{2,0,1:T(8,128)(2,1)S(1)} %get-tuple-element.20), channel_id=1, source_target_pairs={{0,8},{8,16},{16,24},{24,0},{1,9},{9,17},{17,25},{25,1},{2,10},{10... | collective-permute-start | bytes 1032200 | tf_op jit(solution)/shard_map/ppermute | solution.py:11
  132.5 12.1 %collective-permute-start.11 = (bf16[14,48,256]{2,0,1:T(8,128)(2,1)S(1)}, bf16[14,48,256]{2,0,1:T(8,128)(2,1)S(1)}, u32[]{:S(2)}, u32[]{:S(2)}) collective-permute-start(bf16[14,48,256]{2,0,1:T(8,128)(2,1)S(1)} %get-tuple-element.20), channel_id=1, source_target_pairs={{0,24},{8,0},{16,8},{24,16},{1,25},{9,1},{17,9},{25,17},{2,26},{10... | collective-permute-start | bytes 1032200 | tf_op jit(solution)/shard_map/ppermute | solution.py:11
  142.6 9.1 %collective-permute-start.13 = (bf16[14,48,128]{2,0,1:T(8,128)(2,1)}, bf16[14,48,128]{2,0,1:T(8,128)(2,1)}, u32[]{:S(2)}, u32[]{:S(2)}) collective-permute-start(bf16[14,48,128]{2,0,1:T(8,128)(2,1)} %slice.128), channel_id=1, source_target_pairs={{0,8},{8,16},{16,24},{24,0},{1,9},{9,17},{17,25},{25,1},{2,10},{10... | collective-permute-start | bytes 516104 | tf_op jit(solution)/shard_map/ppermute | solution.py:11
  145.3 8.6 %collective-permute-start.14 = (bf16[14,48,128]{2,0,1:T(8,128)(2,1)}, bf16[14,48,128]{2,0,1:T(8,128)(2,1)}, u32[]{:S(2)}, u32[]{:S(2)}) collective-permute-start(bf16[14,48,128]{2,0,1:T(8,128)(2,1)} %slice.129), channel_id=1, source_target_pairs={{0,24},{8,0},{16,8},{24,16},{1,25},{9,1},{17,9},{25,17},{2,26},{10... | collective-permute-start | bytes 516104 | tf_op jit(solution)/shard_map/ppermute | solution.py:11
  171.8 3.5 %collective-permute-start.15 = (bf16[8,24,128]{2,0,1:T(8,128)(2,1)S(1)}, bf16[8,24,128]{2,0,1:T(8,128)(2,1)S(1)}, u32[]{:S(2)}, u32[]{:S(2)}) collective-permute-start(bf16[8,24,128]{2,0,1:T(8,128)(2,1)S(1)} %get-tuple-element.18), channel_id=1, source_target_pairs={{0,1},{1,2},{2,3},{3,4},{4,5},{5,6},{6,7},{7,0},{8,9},{9,10},{10,1... | collective-permute-start | bytes 147464 | tf_op jit(solution)/shard_map/ppermute | solution.py:11
  175.4 3.5 %collective-permute-start.16 = (bf16[8,24,128]{2,0,1:T(8,128)(2,1)S(1)}, bf16[8,24,128]{2,0,1:T(8,128)(2,1)S(1)}, u32[]{:S(2)}, u32[]{:S(2)}) collective-permute-start(bf16[8,24,128]{2,0,1:T(8,128)(2,1)S(1)} %fusion.40), channel_id=1, source_target_pairs={{0,1},{1,2},{2,3},{3,4},{4,5},{5,6},{6,7},{7,0},{8,9},{9,10},{10,1... | collective-permute-start | bytes 147464 | tf_op jit(solution)/shard_map/ppermute | solution.py:11
  175.4 3.5 %collective-permute-start.19 = (bf16[8,24,128]{2,0,1:T(8,128)(2,1)S(1)}, bf16[8,24,128]{2,0,1:T(8,128)(2,1)S(1)}, u32[]{:S(2)}, u32[]{:S(2)}) collective-permute-start(bf16[8,24,128]{2,0,1:T(8,128)(2,1)S(1)} %get-tuple-element.19), channel_id=1, source_target_pairs={{0,7},{1,0},{2,1},{3,2},{4,3},{5,4},{6,5},{7,6},{8,15},{9,8},{10,9... | collective-permute-start | bytes 147464 | tf_op jit(solution)/shard_map/ppermute | solution.py:11
  178.9 3.5 %collective-permute-start.17 = (bf16[8,24,128]{2,0,1:T(8,128)(2,1)S(1)}, bf16[8,24,128]{2,0,1:T(8,128)(2,1)S(1)}, u32[]{:S(2)}, u32[]{:S(2)}) collective-permute-start(bf16[8,24,128]{2,0,1:T(8,128)(2,1)S(1)} %fusion.39), channel_id=1, source_target_pairs={{0,1},{1,2},{2,3},{3,4},{4,5},{5,6},{6,7},{7,0},{8,9},{9,10},{10,1... | collective-permute-start | bytes 147464 | tf_op jit(solution)/shard_map/ppermute | solution.py:11
  182.5 2.1 collective-permute-start.20
  182.9 5.8 %collective-permute-start.18 = (bf16[8,24,128]{2,0,1:T(8,128)(2,1)S(1)}, bf16[8,24,128]{2,0,1:T(8,128)(2,1)S(1)}, u32[]{:S(2)}, u32[]{:S(2)}) collective-permute-start(bf16[8,24,128]{2,0,1:T(8,128)(2,1)S(1)} %get-tuple-element.16), channel_id=1, source_target_pairs={{0,1},{1,2},{2,3},{3,4},{4,5},{5,6},{6,7},{7,0},{8,9},{9,10},{10,1... | collective-permute-start | bytes 147464 | tf_op jit(solution)/shard_map/ppermute | solution.py:11
  184.6 4.9 %collective-permute-start.21 = (bf16[8,24,128]{2,0,1:T(8,128)(2,1)S(1)}, bf16[8,24,128]{2,0,1:T(8,128)(2,1)S(1)}, u32[]{:S(2)}, u32[]{:S(2)}) collective-permute-start(bf16[8,24,128]{2,0,1:T(8,128)(2,1)S(1)} %fusion.34), channel_id=1, source_target_pairs={{0,7},{1,0},{2,1},{3,2},{4,3},{5,4},{6,5},{7,6},{8,15},{9,8},{10,9... | collective-permute-start | bytes 147464 | tf_op jit(solution)/shard_map/ppermute | solution.py:11
  (3 other events, 6.3 us)
Sparse Core Ops, SparseCore 0:
  10.6 79.8 all-gather.1
  162.4 74.0 reduce-scatter.1

commit v7 on v6

--- a/solution.py
+++ b/solution.py
@@ -115,9 +115,13 @@
     highest = lax.Precision.HIGH
 
     x_pick = jnp.einsum("qr,trk->qtk", row_pick, x_abs, preferred_element_type=F32).astype(BF16)
-    per_slot = jnp.einsum("qtk,qkn->qtn", x_pick, pair_all, preferred_element_type=F32)
-    pre = jnp.einsum(
-        "qc,qtn->ctn", col_pick.astype(F32), per_slot, precision=highest, preferred_element_type=F32
+    by_col = jnp.einsum(
+        "qcr,qkn->ckrn", onehot3.transpose(0, 2, 1), pair_all, preferred_element_type=F32
+    ).astype(BF16).reshape(tile_cols, feat, 2 * bs)
+    x_kr = x_abs.transpose(0, 2, 1).reshape(1, tok, feat)
+    x_wide = jnp.broadcast_to(x_kr, (tile_cols, tok, feat))
+    pre = lax.dot_general(
+        x_wide, by_col, (((2,), (1,)), ((0,), (0,))), preferred_element_type=F32
     ).astype(BF16)
     pre_roll = jnp.roll(pre.reshape(tile_cols, n_row, rows_per, 2 * bs), -k_row, axis=1)
     if n_row == 4:

time: 246 us -> 237 us (0.963)
  the two profiles are of different devices: /device:TPU:2 before, /device:TPU:10 now
where the time goes in v7:
time: 237 us; the launch traced here: 236 us
  waiting for transfers between devices  151 us (64%)
  starting transfers between devices  35.4 us (15%)
  matrix products  20.7 us (9%)
  between operations  14.5 us (6%)
  other arithmetic  7.62 us (3%)
  local copies, waits for them, and re-layouts  7.31 us (3%)
    all_gather x1, waiting for transfers between devices, on_device(): lax.all_gather(pair_local, 'dp', axis=0, tiled=True)  64.7 us
    reduce_scatter x1, waiting for transfers between devices, on_device(): lax.psum_scatter(slot_dw.reshape(cap * bs, 2 * bs), 'dp', scatter_dimensi...  46.5 us
    ppermute x22, waiting for transfers between devices, _shift(): return lax.ppermute(x, axis, perm=[(i, (i + step) % n) for i in range(n)])  39.6 us
    ppermute x22, starting transfers between devices, _shift(): return lax.ppermute(x, axis, perm=[(i, (i + step) % n) for i in range(n)])  35.3 us
  transfers between devices with their start and end apart: 24, of which 18 were waited for; matrix products, arithmetic and copies ran while one was open for 6% of the time, Pallas kernels for 0%

profile of v7, /device:TPU:10, one launch (start us, length us, event | category | flops | bytes accessed | tf_op | source)
XLA Modules:
  0.0 236.4 jit_solution(1855705398072119772)
XLA Ops:
  16.4 3.9 %collective-permute-done.5 = bf16[24,1024]{1,0:T(8,128)(2,1)S(1)} collective-permute-done((bf16[24,1024]{1,0:T(8,128)(2,1)S(1)}, bf16[24,1024]{1,0:T(8,128)(2,1)S(1)}, u32[]{:S(2)}, u32[]{:S(2)}) %collective-permute-start.5) | collective-permute-done | bytes 49184 | tf_op jit(solution)/shard_map/ppermute | solution.py:11
  20.4 3.7 %collective-permute-done.6 = bf16[24,1024]{1,0:T(8,128)(2,1)S(1)} collective-permute-done((bf16[24,1024]{1,0:T(8,128)(2,1)S(1)}, bf16[24,1024]{1,0:T(8,128)(2,1)S(1)}, u32[]{:S(2)}, u32[]{:S(2)}) %collective-permute-start.6) | collective-permute-done | bytes 49184 | tf_op jit(solution)/shard_map/ppermute | solution.py:11
  25.8 64.7 %all-gather.2.cloned.1.call-done = bf16[6144,256]{1,0:T(8,128)(2,1)} async-done(((bf16[384,256]{1,0:T(8,128)(2,1)}), bf16[6144,256]{1,0:T(8,128)(2,1)}) %all-gather.2.cloned.1.call-update) | async-done | bytes 3145744 | tf_op jit(solution)/shard_map/all_gather | solution.py:100
  90.4 4.5 %convolution_convert_fusion = bf16[128,256,14,8]{1,2,3,0:T(8,128)(2,1)S(1)} fusion(bf16[48,128,256,1]{2,1,0,3:T(8,128)(2,1)} %bitcast.130, s32[14,8]{0,1:T(8,128)S(1)} %bitcast.147, pred[14,8]{0,1:T(8,128)(4,1)S(1)} %bitcast.148), kind=kOutput, calls=%fused_computation.2 | convolution fusion | flops 356002304 | bytes 10486320 | tf_op jit(solution)/shard_map/qcr,qkn->ckrn/dot_general | solution.py:118
  95.0 2.9 %fusion.16 = bf16[14,192,256]{2,1,0:T(8,128)(2,1)S(1)} fusion(bf16[14,1024,256]{2,0,1:T(8,128)(2,1)S(1)} %bitcast.132, bf16[192,1024]{1,0:T(8,128)(2,1)S(1)} %copy.26), kind=kOutput, calls=%fused_computation.25 | convolution fusion | flops 1409974272 | bytes 9109504 | tf_op jit(solution)/shard_map/dot_general | solution.py:123
  99.6 3.4 %collective-permute-start.9 = (bf16[14,48,256]{2,0,1:T(8,128)(2,1)S(1)}, bf16[14,48,256]{2,0,1:T(8,128)(2,1)S(1)}, u32[]{:S(2)}, u32[]{:S(2)}) collective-permute-start(bf16[14,48,256]{2,0,1:T(8,128)(2,1)S(1)} %pad_maximum_fusion.1), channel_id=1, source_target_pairs={{0,8},{8,16},{16,24},{24,0},{1,9},{9,17},{17,25},{25,1},{2,10},{10... | collective-permute-start | bytes 1032200 | tf_op jit(solution)/shard_map/ppermute | solution.py:11
  103.2 2.4 %collective-permute-start.7 = (bf16[14,48,256]{2,0,1:T(8,128)(2,1)S(1)}, bf16[14,48,256]{2,0,1:T(8,128)(2,1)S(1)}, u32[]{:S(2)}, u32[]{:S(2)}) collective-permute-start(bf16[14,48,256]{2,0,1:T(8,128)(2,1)S(1)} %pad_maximum_fusion), channel_id=1, source_target_pairs={{0,24},{8,0},{16,8},{24,16},{1,25},{9,1},{17,9},{25,17},{2,26},{10... | collective-permute-start | bytes 1032200 | tf_op jit(solution)/shard_map/ppermute | solution.py:11
  105.6 4.4 %collective-permute-done.9 = bf16[14,48,256]{2,0,1:T(8,128)(2,1)S(1)} collective-permute-done((bf16[14,48,256]{2,0,1:T(8,128)(2,1)S(1)}, bf16[14,48,256]{2,0,1:T(8,128)(2,1)S(1)}, u32[]{:S(2)}, u32[]{:S(2)}) %collective-permute-start.9) | collective-permute-done | bytes 344096 | tf_op jit(solution)/shard_map/ppermute | solution.py:11
  110.0 3.3 %collective-permute-start.10 = (bf16[14,48,128]{2,0,1:T(8,128)(2,1)S(1)}, bf16[14,48,128]{2,0,1:T(8,128)(2,1)S(1)}, u32[]{:S(2)}, u32[]{:S(2)}) collective-permute-start(bf16[14,48,128]{2,0,1:T(8,128)(2,1)S(1)} %add_convert_fusion), channel_id=1, source_target_pairs={{0,8},{8,16},{16,24},{24,0},{1,9},{9,17},{17,25},{25,1},{2,10},{10... | collective-permute-start | bytes 516104 | tf_op jit(solution)/shard_map/ppermute | solution.py:11
  113.4 3.4 %collective-permute-start.8 = (bf16[14,48,128]{2,0,1:T(8,128)(2,1)S(1)}, bf16[14,48,128]{2,0,1:T(8,128)(2,1)S(1)}, u32[]{:S(2)}, u32[]{:S(2)}) collective-permute-start(bf16[14,48,128]{2,0,1:T(8,128)(2,1)S(1)} %add_convert_fusion.1), channel_id=1, source_target_pairs={{0,24},{8,0},{16,8},{24,16},{1,25},{9,1},{17,9},{25,17},{2,26},{10... | collective-permute-start | bytes 516104 | tf_op jit(solution)/shard_map/ppermute | solution.py:11
  117.0 3.6 %collective-permute-done.10 = bf16[14,48,128]{2,0,1:T(8,128)(2,1)S(1)} collective-permute-done((bf16[14,48,128]{2,0,1:T(8,128)(2,1)S(1)}, bf16[14,48,128]{2,0,1:T(8,128)(2,1)S(1)}, u32[]{:S(2)}, u32[]{:S(2)}) %collective-permute-start.10) | collective-permute-done | bytes 172064 | tf_op jit(solution)/shard_map/ppermute | solution.py:11
  122.9 4.4 %collective-permute-start.12 = (bf16[14,48,256]{2,0,1:T(8,128)(2,1)S(1)}, bf16[14,48,256]{2,0,1:T(8,128)(2,1)S(1)}, u32[]{:S(2)}, u32[]{:S(2)}) collective-permute-start(bf16[14,48,256]{2,0,1:T(8,128)(2,1)S(1)} %get-tuple-element.20), channel_id=1, source_target_pairs={{0,8},{8,16},{16,24},{24,0},{1,9},{9,17},{17,25},{25,1},{2,10},{10... | collective-permute-start | bytes 1032200 | tf_op jit(solution)/shard_map/ppermute | solution.py:11
  127.3 2.2 collective-permute-start.11
  129.9 3.7 %collective-permute-done.12 = bf16[14,48,256]{2,0,1:T(8,128)(2,1)S(1)} collective-permute-done((bf16[14,48,256]{2,0,1:T(8,128)(2,1)S(1)}, bf16[14,48,256]{2,0,1:T(8,128)(2,1)S(1)}, u32[]{:S(2)}, u32[]{:S(2)}) %collective-permute-start.12) | collective-permute-done | bytes 344096 | tf_op jit(solution)/shard_map/ppermute | solution.py:11
  133.6 4.3 %collective-permute-start.13 = (bf16[14,48,128]{2,0,1:T(8,128)(2,1)S(1)}, bf16[14,48,128]{2,0,1:T(8,128)(2,1)S(1)}, u32[]{:S(2)}, u32[]{:S(2)}) collective-permute-start(bf16[14,48,128]{2,0,1:T(8,128)(2,1)S(1)} %slice.128), channel_id=1, source_target_pairs={{0,8},{8,16},{16,24},{24,0},{1,9},{9,17},{17,25},{25,1},{2,10},{10... | collective-permute-start | bytes 516104 | tf_op jit(solution)/shard_map/ppermute | solution.py:11
  138.4 2.8 %collective-permute-start.14 = (bf16[14,48,128]{2,0,1:T(8,128)(2,1)S(1)}, bf16[14,48,128]{2,0,1:T(8,128)(2,1)S(1)}, u32[]{:S(2)}, u32[]{:S(2)}) collective-permute-start(bf16[14,48,128]{2,0,1:T(8,128)(2,1)S(1)} %slice.129), channel_id=1, source_target_pairs={{0,24},{8,0},{16,8},{24,16},{1,25},{9,1},{17,9},{25,17},{2,26},{10... | collective-permute-start | bytes 516104 | tf_op jit(solution)/shard_map/ppermute | solution.py:11
  142.6 3.4 %collective-permute-done.14 = bf16[14,48,128]{2,0,1:T(8,128)(2,1)S(1)} collective-permute-done((bf16[14,48,128]{2,0,1:T(8,128)(2,1)S(1)}, bf16[14,48,128]{2,0,1:T(8,128)(2,1)S(1)}, u32[]{:S(2)}, u32[]{:S(2)}) %collective-permute-start.14) | collective-permute-done | bytes 172064 | tf_op jit(solution)/shard_map/ppermute | solution.py:11
  149.7 3.6 %fusion.11 = bf16[48,128,256]{2,1,0:T(8,128)(2,1)} fusion(bf16[48,192,256]{2,0,1:T(8,128)(2,1)S(1)} %convolution_convert_fusion.1, bf16[48,192,128]{2,0,1:T(8,128)(2,1)S(1)} %convolution_convert_fusion.2), kind=kOutput, calls=%fused_computation.23 | convolution fusion | flops 605552640 | bytes 10223616 | tf_op jit(solution)/shard_map/qtk,qtn->qkn/dot_general | solution.py:145
  155.2 4.1 %fusion.6 = f32[48,192,128]{2,1,0:T(8,128)S(1)} fusion(bf16[48,128,256]{2,1,0:T(8,128)(2,1)S(1)} %bitcast.131, bf16[48,192,256]{2,0,1:T(8,128)(2,1)} %copy-done), kind=kOutput, calls=%fused_computation.7 | convolution fusion | flops 603979776 | bytes 12582912 | tf_op jit(solution)/shard_map/qtn,qkn->qtk/dot_general | solution.py:147
  159.4 3.4 %fusion.29 = bf16[8,192,128]{2,0,1:T(8,128)(2,1)S(1)} fusion(f32[48,192,128]{2,1,0:T(8,128)S(1)} %fusion.6, bf16[48,8]{0,1:T(8,128)(2,1)S(1)} %get-tuple-element.4), kind=kOutput, calls=%fused_computation.34 | convolution fusion | flops 56819712 | bytes 5112576 | tf_op jit(solution)/shard_map/qr,qtk->rtk/dot_general | solution.py:148
  163.0 3.5 %collective-permute-done.15 = bf16[8,24,128]{2,0,1:T(8,128)(2,1)S(1)} collective-permute-done((bf16[8,24,128]{2,0,1:T(8,128)(2,1)S(1)}, bf16[8,24,128]{2,0,1:T(8,128)(2,1)S(1)}, u32[]{:S(2)}, u32[]{:S(2)}) %collective-permute-start.15) | collective-permute-done | bytes 49184 | tf_op jit(solution)/shard_map/ppermute | solution.py:11
  170.1 3.5 %collective-permute-done.17 = bf16[8,24,128]{2,0,1:T(8,128)(2,1)S(1)} collective-permute-done((bf16[8,24,128]{2,0,1:T(8,128)(2,1)S(1)}, bf16[8,24,128]{2,0,1:T(8,128)(2,1)S(1)}, u32[]{:S(2)}, u32[]{:S(2)}) %collective-permute-start.17) | collective-permute-done | bytes 49184 | tf_op jit(solution)/shard_map/ppermute | solution.py:11
  175.8 3.1 %collective-permute-start.21 = (bf16[8,24,128]{2,0,1:T(8,128)(2,1)S(1)}, bf16[8,24,128]{2,0,1:T(8,128)(2,1)S(1)}, u32[]{:S(2)}, u32[]{:S(2)}) collective-permute-start(bf16[8,24,128]{2,0,1:T(8,128)(2,1)S(1)} %fusion.38), channel_id=1, source_target_pairs={{0,7},{1,0},{2,1},{3,2},{4,3},{5,4},{6,5},{7,6},{8,15},{9,8},{10,9... | collective-permute-start | bytes 147464 | tf_op jit(solution)/shard_map/ppermute | solution.py:11
  181.4 46.5 %reduce-scatter.2.cloned.1.call-done = bf16[384,256]{1,0:T(8,128)(2,1)} async-done(((bf16[6144,256]{1,0:T(8,128)(2,1)}), bf16[384,256]{1,0:T(8,128)(2,1)}) %reduce-scatter.2.cloned.1.call-update) | async-done | bytes 196624 | tf_op jit(solution)/shard_map/reduce_scatter | solution.py:155
  (95 shorter events, 33.2 us)
Async XLA Ops:
  7.2 83.3 %all-gather.2.cloned.1.call-start = ((), (), s32[]{:S(2)}) async-start(), calls=%async_computation.1 | async-start | bytes 3342336 | tf_op jit(solution)/shard_map/all_gather | solution.py:100
  8.9 219.0 %reduce-scatter.2.cloned.1.call-start = ((), (), s32[]{:S(2)}) async-start(), calls=%async_computation.2 | async-start | bytes 3342336 | tf_op jit(solution)/shard_map/reduce_scatter | solution.py:155
  8.9 2.6 %collective-permute-start = (bf16[24,1024]{1,0:T(8,128)(2,1)}, bf16[24,1024]{1,0:T(8,128)(2,1)S(1)}, u32[]{:S(2)}, u32[]{:S(2)}) collective-permute-start(bf16[24,1024]{1,0:T(8,128)(2,1)} %param.7), channel_id=1, source_target_pairs={{0,7},{1,0},{2,1},{3,2},{4,3},{5,4},{6,5},{7,6},{8,15},{9,8},{10,9... | collective-permute-start | bytes 147464 | tf_op jit(solution)/shard_map/ppermute | solution.py:11
  9.0 3.8 %collective-permute-start.3 = (bf16[24,1024]{1,0:T(8,128)(2,1)}, bf16[24,1024]{1,0:T(8,128)(2,1)S(1)}, u32[]{:S(2)}, u32[]{:S(2)}) collective-permute-start(bf16[24,1024]{1,0:T(8,128)(2,1)} %param.7), channel_id=1, source_target_pairs={{0,1},{1,2},{2,3},{3,4},{4,5},{5,6},{6,7},{7,0},{8,9},{9,10},{10,1... | collective-permute-start | bytes 147464 | tf_op jit(solution)/shard_map/ppermute | solution.py:11
  11.5 3.0 %collective-permute-start.1 = (bf16[24,1024]{1,0:T(8,128)(2,1)S(1)}, bf16[24,1024]{1,0:T(8,128)(2,1)S(1)}, u32[]{:S(2)}, u32[]{:S(2)}) collective-permute-start(bf16[24,1024]{1,0:T(8,128)(2,1)S(1)} %collective-permute-done), channel_id=1, source_target_pairs={{0,7},{1,0},{2,1},{3,2},{4,3},{5,4},{6,5},{7,6},{8,15},{9,8},{10,9... | collective-permute-start | bytes 147464 | tf_op jit(solution)/shard_map/ppermute | solution.py:11
  12.8 3.5 %collective-permute-start.4 = (bf16[24,1024]{1,0:T(8,128)(2,1)S(1)}, bf16[24,1024]{1,0:T(8,128)(2,1)S(1)}, u32[]{:S(2)}, u32[]{:S(2)}) collective-permute-start(bf16[24,1024]{1,0:T(8,128)(2,1)S(1)} %collective-permute-done.3), channel_id=1, source_target_pairs={{0,1},{1,2},{2,3},{3,4},{4,5},{5,6},{6,7},{7,0},{8,9},{9,10},{10,1... | collective-permute-start | bytes 147464 | tf_op jit(solution)/shard_map/ppermute | solution.py:11
  14.5 5.8 %collective-permute-start.2 = (bf16[24,1024]{1,0:T(8,128)(2,1)S(1)}, bf16[24,1024]{1,0:T(8,128)(2,1)S(1)}, u32[]{:S(2)}, u32[]{:S(2)}) collective-permute-start(bf16[24,1024]{1,0:T(8,128)(2,1)S(1)} %collective-permute-done.1), channel_id=1, source_target_pairs={{0,7},{1,0},{2,1},{3,2},{4,3},{5,4},{6,5},{7,6},{8,15},{9,8},{10,9... | collective-permute-start | bytes 147464 | tf_op jit(solution)/shard_map/ppermute | solution.py:11
  16.3 4.0 %collective-permute-start.5 = (bf16[24,1024]{1,0:T(8,128)(2,1)S(1)}, bf16[24,1024]{1,0:T(8,128)(2,1)S(1)}, u32[]{:S(2)}, u32[]{:S(2)}) collective-permute-start(bf16[24,1024]{1,0:T(8,128)(2,1)S(1)} %collective-permute-done.4), channel_id=1, source_target_pairs={{0,1},{1,2},{2,3},{3,4},{4,5},{5,6},{6,7},{7,0},{8,9},{9,10},{10,1... | collective-permute-start | bytes 147464 | tf_op jit(solution)/shard_map/ppermute | solution.py:11
  20.3 3.7 %collective-permute-start.6 = (bf16[24,1024]{1,0:T(8,128)(2,1)S(1)}, bf16[24,1024]{1,0:T(8,128)(2,1)S(1)}, u32[]{:S(2)}, u32[]{:S(2)}) collective-permute-start(bf16[24,1024]{1,0:T(8,128)(2,1)S(1)} %collective-permute-done.5), channel_id=1, source_target_pairs={{0,1},{1,2},{2,3},{3,4},{4,5},{5,6},{6,7},{7,0},{8,9},{9,10},{10,1... | collective-permute-start | bytes 147464 | tf_op jit(solution)/shard_map/ppermute | solution.py:11
  99.6 10.3 %collective-permute-start.9 = (bf16[14,48,256]{2,0,1:T(8,128)(2,1)S(1)}, bf16[14,48,256]{2,0,1:T(8,128)(2,1)S(1)}, u32[]{:S(2)}, u32[]{:S(2)}) collective-permute-start(bf16[14,48,256]{2,0,1:T(8,128)(2,1)S(1)} %pad_maximum_fusion.1), channel_id=1, source_target_pairs={{0,8},{8,16},{16,24},{24,0},{1,9},{9,17},{17,25},{25,1},{2,10},{10... | collective-permute-start | bytes 1032200 | tf_op jit(solution)/shard_map/ppermute | solution.py:11
  103.2 10.2 %collective-permute-start.7 = (bf16[14,48,256]{2,0,1:T(8,128)(2,1)S(1)}, bf16[14,48,256]{2,0,1:T(8,128)(2,1)S(1)}, u32[]{:S(2)}, u32[]{:S(2)}) collective-permute-start(bf16[14,48,256]{2,0,1:T(8,128)(2,1)S(1)} %pad_maximum_fusion), channel_id=1, source_target_pairs={{0,24},{8,0},{16,8},{24,16},{1,25},{9,1},{17,9},{25,17},{2,26},{10... | collective-permute-start | bytes 1032200 | tf_op jit(solution)/shard_map/ppermute | solution.py:11
  110.0 10.5 %collective-permute-start.10 = (bf16[14,48,128]{2,0,1:T(8,128)(2,1)S(1)}, bf16[14,48,128]{2,0,1:T(8,128)(2,1)S(1)}, u32[]{:S(2)}, u32[]{:S(2)}) collective-permute-start(bf16[14,48,128]{2,0,1:T(8,128)(2,1)S(1)} %add_convert_fusion), channel_id=1, source_target_pairs={{0,8},{8,16},{16,24},{24,0},{1,9},{9,17},{17,25},{25,1},{2,10},{10... | collective-permute-start | bytes 516104 | tf_op jit(solution)/shard_map/ppermute | solution.py:11
  113.4 9.1 %collective-permute-start.8 = (bf16[14,48,128]{2,0,1:T(8,128)(2,1)S(1)}, bf16[14,48,128]{2,0,1:T(8,128)(2,1)S(1)}, u32[]{:S(2)}, u32[]{:S(2)}) collective-permute-start(bf16[14,48,128]{2,0,1:T(8,128)(2,1)S(1)} %add_convert_fusion.1), channel_id=1, source_target_pairs={{0,24},{8,0},{16,8},{24,16},{1,25},{9,1},{17,9},{25,17},{2,26},{10... | collective-permute-start | bytes 516104 | tf_op jit(solution)/shard_map/ppermute | solution.py:11
  122.9 10.7 %collective-permute-start.12 = (bf16[14,48,256]{2,0,1:T(8,128)(2,1)S(1)}, bf16[14,48,256]{2,0,1:T(8,128)(2,1)S(1)}, u32[]{:S(2)}, u32[]{:S(2)}) collective-permute-start(bf16[14,48,256]{2,0,1:T(8,128)(2,1)S(1)} %get-tuple-element.20), channel_id=1, source_target_pairs={{0,8},{8,16},{16,24},{24,0},{1,9},{9,17},{17,25},{25,1},{2,10},{10... | collective-permute-start | bytes 1032200 | tf_op jit(solution)/shard_map/ppermute | solution.py:11
  127.3 11.0 %collective-permute-start.11 = (bf16[14,48,256]{2,0,1:T(8,128)(2,1)S(1)}, bf16[14,48,256]{2,0,1:T(8,128)(2,1)S(1)}, u32[]{:S(2)}, u32[]{:S(2)}) collective-permute-start(bf16[14,48,256]{2,0,1:T(8,128)(2,1)S(1)} %get-tuple-element.20), channel_id=1, source_target_pairs={{0,24},{8,0},{16,8},{24,16},{1,25},{9,1},{17,9},{25,17},{2,26},{10... | collective-permute-start | bytes 1032200 | tf_op jit(solution)/shard_map/ppermute | solution.py:11
  133.6 9.0 %collective-permute-start.13 = (bf16[14,48,128]{2,0,1:T(8,128)(2,1)S(1)}, bf16[14,48,128]{2,0,1:T(8,128)(2,1)S(1)}, u32[]{:S(2)}, u32[]{:S(2)}) collective-permute-start(bf16[14,48,128]{2,0,1:T(8,128)(2,1)S(1)} %slice.128), channel_id=1, source_target_pairs={{0,8},{8,16},{16,24},{24,0},{1,9},{9,17},{17,25},{25,1},{2,10},{10... | collective-permute-start | bytes 516104 | tf_op jit(solution)/shard_map/ppermute | solution.py:11
  138.4 7.6 %collective-permute-start.14 = (bf16[14,48,128]{2,0,1:T(8,128)(2,1)S(1)}, bf16[14,48,128]{2,0,1:T(8,128)(2,1)S(1)}, u32[]{:S(2)}, u32[]{:S(2)}) collective-permute-start(bf16[14,48,128]{2,0,1:T(8,128)(2,1)S(1)} %slice.129), channel_id=1, source_target_pairs={{0,24},{8,0},{16,8},{24,16},{1,25},{9,1},{17,9},{25,17},{2,26},{10... | collective-permute-start | bytes 516104 | tf_op jit(solution)/shard_map/ppermute | solution.py:11
  163.0 3.5 %collective-permute-start.15 = (bf16[8,24,128]{2,0,1:T(8,128)(2,1)S(1)}, bf16[8,24,128]{2,0,1:T(8,128)(2,1)S(1)}, u32[]{:S(2)}, u32[]{:S(2)}) collective-permute-start(bf16[8,24,128]{2,0,1:T(8,128)(2,1)S(1)} %get-tuple-element.18), channel_id=1, source_target_pairs={{0,1},{1,2},{2,3},{3,4},{4,5},{5,6},{6,7},{7,0},{8,9},{9,10},{10,1... | collective-permute-start | bytes 147464 | tf_op jit(solution)/shard_map/ppermute | solution.py:11
  166.5 3.5 %collective-permute-start.16 = (bf16[8,24,128]{2,0,1:T(8,128)(2,1)S(1)}, bf16[8,24,128]{2,0,1:T(8,128)(2,1)S(1)}, u32[]{:S(2)}, u32[]{:S(2)}) collective-permute-start(bf16[8,24,128]{2,0,1:T(8,128)(2,1)S(1)} %fusion.44), channel_id=1, source_target_pairs={{0,1},{1,2},{2,3},{3,4},{4,5},{5,6},{6,7},{7,0},{8,9},{9,10},{10,1... | collective-permute-start | bytes 147464 | tf_op jit(solution)/shard_map/ppermute | solution.py:11
  166.5 3.5 %collective-permute-start.19 = (bf16[8,24,128]{2,0,1:T(8,128)(2,1)S(1)}, bf16[8,24,128]{2,0,1:T(8,128)(2,1)S(1)}, u32[]{:S(2)}, u32[]{:S(2)}) collective-permute-start(bf16[8,24,128]{2,0,1:T(8,128)(2,1)S(1)} %get-tuple-element.19), channel_id=1, source_target_pairs={{0,7},{1,0},{2,1},{3,2},{4,3},{5,4},{6,5},{7,6},{8,15},{9,8},{10,9... | collective-permute-start | bytes 147464 | tf_op jit(solution)/shard_map/ppermute | solution.py:11
  170.1 3.5 %collective-permute-start.17 = (bf16[8,24,128]{2,0,1:T(8,128)(2,1)S(1)}, bf16[8,24,128]{2,0,1:T(8,128)(2,1)S(1)}, u32[]{:S(2)}, u32[]{:S(2)}) collective-permute-start(bf16[8,24,128]{2,0,1:T(8,128)(2,1)S(1)} %fusion.43), channel_id=1, source_target_pairs={{0,1},{1,2},{2,3},{3,4},{4,5},{5,6},{6,7},{7,0},{8,9},{9,10},{10,1... | collective-permute-start | bytes 147464 | tf_op jit(solution)/shard_map/ppermute | solution.py:11
  173.6 2.2 collective-permute-start.20
  174.0 5.8 %collective-permute-start.18 = (bf16[8,24,128]{2,0,1:T(8,128)(2,1)S(1)}, bf16[8,24,128]{2,0,1:T(8,128)(2,1)S(1)}, u32[]{:S(2)}, u32[]{:S(2)}) collective-permute-start(bf16[8,24,128]{2,0,1:T(8,128)(2,1)S(1)} %get-tuple-element.16), channel_id=1, source_target_pairs={{0,1},{1,2},{2,3},{3,4},{4,5},{5,6},{6,7},{7,0},{8,9},{9,10},{10,1... | collective-permute-start | bytes 147464 | tf_op jit(solution)/shard_map/ppermute | solution.py:11
  175.8 4.9 %collective-permute-start.21 = (bf16[8,24,128]{2,0,1:T(8,128)(2,1)S(1)}, bf16[8,24,128]{2,0,1:T(8,128)(2,1)S(1)}, u32[]{:S(2)}, u32[]{:S(2)}) collective-permute-start(bf16[8,24,128]{2,0,1:T(8,128)(2,1)S(1)} %fusion.38), channel_id=1, source_target_pairs={{0,7},{1,0},{2,1},{3,2},{4,3},{5,4},{6,5},{7,6},{8,15},{9,8},{10,9... | collective-permute-start | bytes 147464 | tf_op jit(solution)/shard_map/ppermute | solution.py:11
  (3 other events, 23.0 us)
Sparse Core Ops, SparseCore 0:
  10.6 79.7 all-gather.1
  153.5 74.3 reduce-scatter.1

commit v8 on v7

--- a/solution.py
+++ b/solution.py
@@ -136,13 +136,20 @@
     up_grad = (upstream * gate * sig).astype(BF16)
     grad_local = jnp.concatenate([gate_grad, up_grad], axis=2)
     if n_row == 4:
-        grad_rel = jnp.stack(ring4_gather(grad_local, "row", bs), axis=1)
+        grad_parts = ring4_gather(grad_local, "row", bs)
     else:
-        grad_rel = jnp.stack(ring_gather(grad_local, "row", n_row), axis=1)
-    grad_abs = jnp.roll(grad_rel, k_row, axis=1).reshape(tile_cols, tok, 2 * bs)
-
-    g_pick = jnp.einsum("qc,ctn->qtn", col_pick, grad_abs, preferred_element_type=F32).astype(BF16)
-    slot_dw = jnp.einsum("qtk,qtn->qkn", x_pick, g_pick, preferred_element_type=F32).astype(BF16)
+        grad_parts = ring_gather(grad_local, "row", n_row)
+    x_pick_rel = jnp.roll(x_pick.reshape(cap, n_row, rows_per, bs), -k_row, axis=1)
+    pick_parts = [
+        jnp.einsum("qc,ctn->qtn", col_pick, part, preferred_element_type=F32).astype(BF16)
+        for part in grad_parts
+    ]
+    dw_total = None
+    for m in range(n_row):
+        term = jnp.einsum("qtk,qtn->qkn", x_pick_rel[:, m], pick_parts[m], preferred_element_type=F32)
+        dw_total = term if dw_total is None else dw_total + term
+    slot_dw = dw_total.astype(BF16)
+    g_pick = jnp.roll(jnp.stack(pick_parts, axis=1), k_row, axis=1).reshape(cap, tok, 2 * bs)
 
     dx_slot = jnp.einsum("qtn,qkn->qtk", g_pick, pair_all, preferred_element_type=F32)
     dx = jnp.einsum(

time: 237 us -> 239 us (level)
  the two profiles are of different devices: /device:TPU:10 before, /device:TPU:4 now
where the time goes in v8:
time: 239 us; the launch traced here: 238 us
  waiting for transfers between devices  142 us (59%)
  starting transfers between devices  33.8 us (14%)
  matrix products  26.8 us (11%)
  local copies, waits for them, and re-layouts  15.2 us (6%)
  between operations  14.6 us (6%)
  other arithmetic  6.21 us (3%)
    all_gather x1, waiting for transfers between devices, on_device(): lax.all_gather(pair_local, 'dp', axis=0, tiled=True)  64.1 us
    reduce_scatter x1, waiting for transfers between devices, on_device(): lax.psum_scatter(slot_dw.reshape(cap * bs, 2 * bs), 'dp', scatter_dimensi...  39.9 us
    ppermute x22, waiting for transfers between devices, _shift(): return lax.ppermute(x, axis, perm=[(i, (i + step) % n) for i in range(n)])  37.7 us
    ppermute x22, starting transfers between devices, _shift(): return lax.ppermute(x, axis, perm=[(i, (i + step) % n) for i in range(n)])  33.7 us
    dot_general x4, matrix products, on_device(): jnp.einsum('qtk,qtn->qkn', x_pick_rel[:, m], pick_parts[m], preferred_ele...  7.71 us
    dot_general x4, matrix products, on_device(): jnp.einsum('qc,ctn->qtn', col_pick, part, preferred_element_type=F32)  6.06 us
    unnamed x30, local copies, waits for them, and re-layouts  5.89 us
  transfers between devices with their start and end apart: 24, of which 16 were waited for; matrix products, arithmetic and copies ran while one was open for 11% of the time, Pallas kernels for 0%

profile of v8, /device:TPU:4, one launch (start us, length us, event | category | flops | bytes accessed | tf_op | source)
XLA Modules:
  0.0 238.2 jit_solution(18030879335323904883)
XLA Ops:
  16.4 4.8 %collective-permute-done.5 = bf16[24,1024]{1,0:T(8,128)(2,1)S(1)} collective-permute-done((bf16[24,1024]{1,0:T(8,128)(2,1)S(1)}, bf16[24,1024]{1,0:T(8,128)(2,1)S(1)}, u32[]{:S(2)}, u32[]{:S(2)}) %collective-permute-start.5) | collective-permute-done | bytes 49184 | tf_op jit(solution)/shard_map/ppermute | solution.py:11
  21.2 3.5 %collective-permute-done.6 = bf16[24,1024]{1,0:T(8,128)(2,1)S(1)} collective-permute-done((bf16[24,1024]{1,0:T(8,128)(2,1)S(1)}, bf16[24,1024]{1,0:T(8,128)(2,1)S(1)}, u32[]{:S(2)}, u32[]{:S(2)}) %collective-permute-start.6) | collective-permute-done | bytes 49184 | tf_op jit(solution)/shard_map/ppermute | solution.py:11
  26.4 64.1 %all-gather.2.cloned.1.call-done = bf16[6144,256]{1,0:T(8,128)(2,1)} async-done(((bf16[384,256]{1,0:T(8,128)(2,1)}), bf16[6144,256]{1,0:T(8,128)(2,1)}) %all-gather.2.cloned.1.call-update) | async-done | bytes 3145744 | tf_op jit(solution)/shard_map/all_gather | solution.py:100
  90.5 4.5 %convolution_convert_fusion = bf16[128,256,14,8]{1,2,3,0:T(8,128)(2,1)S(1)} fusion(bf16[48,128,256,1]{2,1,0,3:T(8,128)(2,1)} %bitcast.165, s32[14,8]{0,1:T(8,128)S(1)} %bitcast.181, pred[14,8]{0,1:T(8,128)(4,1)S(1)} %bitcast.182), kind=kOutput, calls=%fused_computation.2 | convolution fusion | flops 356002304 | bytes 10486320 | tf_op jit(solution)/shard_map/qcr,qkn->ckrn/dot_general | solution.py:118
  95.0 2.9 %fusion.7 = bf16[14,192,256]{2,1,0:T(8,128)(2,1)S(1)} fusion(bf16[14,1024,256]{2,0,1:T(8,128)(2,1)S(1)} %bitcast.169, bf16[192,1024]{1,0:T(8,128)(2,1)S(1)} %copy.47), kind=kOutput, calls=%fused_computation.14 | convolution fusion | flops 1409974272 | bytes 9109504 | tf_op jit(solution)/shard_map/dot_general | solution.py:123
  99.7 4.7 %collective-permute-start.7 = (bf16[14,48,256]{2,0,1:T(8,128)(2,1)S(1)}, bf16[14,48,256]{2,0,1:T(8,128)(2,1)S(1)}, u32[]{:S(2)}, u32[]{:S(2)}) collective-permute-start(bf16[14,48,256]{2,0,1:T(8,128)(2,1)S(1)} %pad_maximum_fusion), channel_id=1, source_target_pairs={{0,24},{8,0},{16,8},{24,16},{1,25},{9,1},{17,9},{25,17},{2,26},{10... | collective-permute-start | bytes 1032200 | tf_op jit(solution)/shard_map/ppermute | solution.py:11
  104.8 1.9 collective-permute-start.9
  106.9 4.7 %collective-permute-done.7 = bf16[14,48,256]{2,0,1:T(8,128)(2,1)S(1)} collective-permute-done((bf16[14,48,256]{2,0,1:T(8,128)(2,1)S(1)}, bf16[14,48,256]{2,0,1:T(8,128)(2,1)S(1)}, u32[]{:S(2)}, u32[]{:S(2)}) %collective-permute-start.7) | collective-permute-done | bytes 344096 | tf_op jit(solution)/shard_map/ppermute | solution.py:11
  111.6 5.6 %collective-permute-start.8 = (bf16[14,48,128]{2,0,1:T(8,128)(2,1)S(1)}, bf16[14,48,128]{2,0,1:T(8,128)(2,1)S(1)}, u32[]{:S(2)}, u32[]{:S(2)}) collective-permute-start(bf16[14,48,128]{2,0,1:T(8,128)(2,1)S(1)} %add_convert_fusion.2), channel_id=1, source_target_pairs={{0,24},{8,0},{16,8},{24,16},{1,25},{9,1},{17,9},{25,17},{2,26},{10... | collective-permute-start | bytes 516104 | tf_op jit(solution)/shard_map/ppermute | solution.py:11
  117.4 2.1 collective-permute-start.10
  122.5 5.8 %collective-permute-done.10 = bf16[14,48,128]{2,0,1:T(8,128)(2,1)S(1)} collective-permute-done((bf16[14,48,128]{2,0,1:T(8,128)(2,1)S(1)}, bf16[14,48,128]{2,0,1:T(8,128)(2,1)S(1)}, u32[]{:S(2)}, u32[]{:S(2)}) %collective-permute-start.10) | collective-permute-done | bytes 172064 | tf_op jit(solution)/shard_map/ppermute | solution.py:11
  128.6 1.9 collective-permute-start.11
  130.5 3.9 %collective-permute-start.12 = (bf16[14,48,256]{2,0,1:T(8,128)(2,1)S(1)}, bf16[14,48,256]{2,0,1:T(8,128)(2,1)S(1)}, u32[]{:S(2)}, u32[]{:S(2)}) collective-permute-start(bf16[14,48,256]{2,0,1:T(8,128)(2,1)S(1)} %pad_maximum_fusion.2), channel_id=1, source_target_pairs={{0,8},{8,16},{16,24},{24,0},{1,9},{9,17},{17,25},{25,1},{2,10},{10... | collective-permute-start | bytes 1032200 | tf_op jit(solution)/shard_map/ppermute | solution.py:11
  138.3 3.1 %collective-permute-start.14 = (bf16[14,48,128]{2,0,1:T(8,128)(2,1)S(1)}, bf16[14,48,128]{2,0,1:T(8,128)(2,1)S(1)}, u32[]{:S(2)}, u32[]{:S(2)}) collective-permute-start(bf16[14,48,128]{2,0,1:T(8,128)(2,1)S(1)} %slice.145), channel_id=1, source_target_pairs={{0,24},{8,0},{16,8},{24,16},{1,25},{9,1},{17,9},{25,17},{2,26},{10... | collective-permute-start | bytes 516104 | tf_op jit(solution)/shard_map/ppermute | solution.py:11
  141.5 2.7 %collective-permute-start.13 = (bf16[14,48,128]{2,0,1:T(8,128)(2,1)S(1)}, bf16[14,48,128]{2,0,1:T(8,128)(2,1)S(1)}, u32[]{:S(2)}, u32[]{:S(2)}) collective-permute-start(bf16[14,48,128]{2,0,1:T(8,128)(2,1)S(1)} %slice.144), channel_id=1, source_target_pairs={{0,8},{8,16},{16,24},{24,0},{1,9},{9,17},{17,25},{25,1},{2,10},{10... | collective-permute-start | bytes 516104 | tf_op jit(solution)/shard_map/ppermute | solution.py:11
  146.8 3.5 %collective-permute-done.13 = bf16[14,48,128]{2,0,1:T(8,128)(2,1)S(1)} collective-permute-done((bf16[14,48,128]{2,0,1:T(8,128)(2,1)S(1)}, bf16[14,48,128]{2,0,1:T(8,128)(2,1)S(1)}, u32[]{:S(2)}, u32[]{:S(2)}) %collective-permute-start.13) | collective-permute-done | bytes 172064 | tf_op jit(solution)/shard_map/ppermute | solution.py:11
  154.4 4.6 %add_convert_fusion = bf16[48,128,256]{2,1,0:T(8,128)(2,1)} fusion(f32[48,128,256]{2,1,0:T(8,128)S(1)} %fusion.17, f32[48,128,256]{2,1,0:T(8,128)S(1)} %fusion.21, f32[48,128,256]{2,1,0:T(8,128)S(1)} %fusion.19, bf16[48,48,256]{2,0,1:T(8,128)(2,1)S(1)} %get-tuple-element.28, bf16[48,4,48,128]{3,2,0,1:T(8,128)(2,1)} %copy-done.3), kind=kOutput, calls=%fused_computation.3 | convolution fusion | flops 157286400 | bytes 23789568 | tf_op jit(solution)/shard_map/qtk,qtn->qkn/dot_general | solution.py:149
  163.7 2.6 %constant_dynamic-slice_fusion = bf16[48,4,48,256]{3,0,2,1:T(8,128)(2,1)S(1)} fusion(bf16[48,8,48,256]{3,0,2,1:T(8,128)(2,1)} %bitcast_dynamic-update-slice_fusion.1, s32[]{:T(128)S(6)} %select_n.62), kind=kLoop, calls=%fused_computation.123 | loop fusion | bytes 9437188 | tf_op jit(solution)/shard_map/jit(_roll_dynamic)/dynamic_slice | solution.py:152
  166.3 1.8 copy.52
  169.6 3.4 %fusion.13 = bf16[8,192,128]{2,0,1:T(8,128)(2,1)S(1)} fusion(f32[48,192,128]{2,1,0:T(8,128)S(1)} %fusion.57, bf16[48,8]{0,1:T(8,128)(2,1)S(1)} %get-tuple-element.3), kind=kOutput, calls=%fused_computation.20 | convolution fusion | flops 56819712 | bytes 5112576 | tf_op jit(solution)/shard_map/qr,qtk->rtk/dot_general | solution.py:155
  173.2 3.5 %collective-permute-done.15 = bf16[8,24,128]{2,0,1:T(8,128)(2,1)S(1)} collective-permute-done((bf16[8,24,128]{2,0,1:T(8,128)(2,1)S(1)}, bf16[8,24,128]{2,0,1:T(8,128)(2,1)S(1)}, u32[]{:S(2)}, u32[]{:S(2)}) %collective-permute-start.15) | collective-permute-done | bytes 49184 | tf_op jit(solution)/shard_map/ppermute | solution.py:11
  180.3 3.5 %collective-permute-done.17 = bf16[8,24,128]{2,0,1:T(8,128)(2,1)S(1)} collective-permute-done((bf16[8,24,128]{2,0,1:T(8,128)(2,1)S(1)}, bf16[8,24,128]{2,0,1:T(8,128)(2,1)S(1)}, u32[]{:S(2)}, u32[]{:S(2)}) %collective-permute-start.17) | collective-permute-done | bytes 49184 | tf_op jit(solution)/shard_map/ppermute | solution.py:11
  185.6 1.8 collective-permute-start.21
  189.8 39.9 %reduce-scatter.2.cloned.1.call-done = bf16[384,256]{1,0:T(8,128)(2,1)} async-done(((bf16[6144,256]{1,0:T(8,128)(2,1)}), bf16[384,256]{1,0:T(8,128)(2,1)}) %reduce-scatter.2.cloned.1.call-update) | async-done | bytes 196624 | tf_op jit(solution)/shard_map/reduce_scatter | solution.py:162
  (111 shorter events, 43.0 us)
Async XLA Ops:
  7.2 83.3 %all-gather.2.cloned.1.call-start = ((), (), s32[]{:S(2)}) async-start(), calls=%async_computation.1 | async-start | bytes 3342336 | tf_op jit(solution)/shard_map/all_gather | solution.py:100
  8.9 220.8 %reduce-scatter.2.cloned.1.call-start = ((), (), s32[]{:S(2)}) async-start(), calls=%async_computation.2 | async-start | bytes 3342336 | tf_op jit(solution)/shard_map/reduce_scatter | solution.py:162
  8.9 2.6 %collective-permute-start = (bf16[24,1024]{1,0:T(8,128)(2,1)}, bf16[24,1024]{1,0:T(8,128)(2,1)S(1)}, u32[]{:S(2)}, u32[]{:S(2)}) collective-permute-start(bf16[24,1024]{1,0:T(8,128)(2,1)} %param.5), channel_id=1, source_target_pairs={{0,7},{1,0},{2,1},{3,2},{4,3},{5,4},{6,5},{7,6},{8,15},{9,8},{10,9... | collective-permute-start | bytes 147464 | tf_op jit(solution)/shard_map/ppermute | solution.py:11
  9.0 3.8 %collective-permute-start.3 = (bf16[24,1024]{1,0:T(8,128)(2,1)}, bf16[24,1024]{1,0:T(8,128)(2,1)S(1)}, u32[]{:S(2)}, u32[]{:S(2)}) collective-permute-start(bf16[24,1024]{1,0:T(8,128)(2,1)} %param.5), channel_id=1, source_target_pairs={{0,1},{1,2},{2,3},{3,4},{4,5},{5,6},{6,7},{7,0},{8,9},{9,10},{10,1... | collective-permute-start | bytes 147464 | tf_op jit(solution)/shard_map/ppermute | solution.py:11
  11.5 3.0 %collective-permute-start.1 = (bf16[24,1024]{1,0:T(8,128)(2,1)S(1)}, bf16[24,1024]{1,0:T(8,128)(2,1)S(1)}, u32[]{:S(2)}, u32[]{:S(2)}) collective-permute-start(bf16[24,1024]{1,0:T(8,128)(2,1)S(1)} %collective-permute-done), channel_id=1, source_target_pairs={{0,7},{1,0},{2,1},{3,2},{4,3},{5,4},{6,5},{7,6},{8,15},{9,8},{10,9... | collective-permute-start | bytes 147464 | tf_op jit(solution)/shard_map/ppermute | solution.py:11
  12.8 3.5 %collective-permute-start.4 = (bf16[24,1024]{1,0:T(8,128)(2,1)S(1)}, bf16[24,1024]{1,0:T(8,128)(2,1)S(1)}, u32[]{:S(2)}, u32[]{:S(2)}) collective-permute-start(bf16[24,1024]{1,0:T(8,128)(2,1)S(1)} %collective-permute-done.3), channel_id=1, source_target_pairs={{0,1},{1,2},{2,3},{3,4},{4,5},{5,6},{6,7},{7,0},{8,9},{9,10},{10,1... | collective-permute-start | bytes 147464 | tf_op jit(solution)/shard_map/ppermute | solution.py:11
  14.5 6.7 %collective-permute-start.2 = (bf16[24,1024]{1,0:T(8,128)(2,1)S(1)}, bf16[24,1024]{1,0:T(8,128)(2,1)S(1)}, u32[]{:S(2)}, u32[]{:S(2)}) collective-permute-start(bf16[24,1024]{1,0:T(8,128)(2,1)S(1)} %collective-permute-done.1), channel_id=1, source_target_pairs={{0,7},{1,0},{2,1},{3,2},{4,3},{5,4},{6,5},{7,6},{8,15},{9,8},{10,9... | collective-permute-start | bytes 147464 | tf_op jit(solution)/shard_map/ppermute | solution.py:11
  16.3 4.9 %collective-permute-start.5 = (bf16[24,1024]{1,0:T(8,128)(2,1)S(1)}, bf16[24,1024]{1,0:T(8,128)(2,1)S(1)}, u32[]{:S(2)}, u32[]{:S(2)}) collective-permute-start(bf16[24,1024]{1,0:T(8,128)(2,1)S(1)} %collective-permute-done.4), channel_id=1, source_target_pairs={{0,1},{1,2},{2,3},{3,4},{4,5},{5,6},{6,7},{7,0},{8,9},{9,10},{10,1... | collective-permute-start | bytes 147464 | tf_op jit(solution)/shard_map/ppermute | solution.py:11
  21.2 3.5 %collective-permute-start.6 = (bf16[24,1024]{1,0:T(8,128)(2,1)S(1)}, bf16[24,1024]{1,0:T(8,128)(2,1)S(1)}, u32[]{:S(2)}, u32[]{:S(2)}) collective-permute-start(bf16[24,1024]{1,0:T(8,128)(2,1)S(1)} %collective-permute-done.5), channel_id=1, source_target_pairs={{0,1},{1,2},{2,3},{3,4},{4,5},{5,6},{6,7},{7,0},{8,9},{9,10},{10,1... | collective-permute-start | bytes 147464 | tf_op jit(solution)/shard_map/ppermute | solution.py:11
  99.7 11.8 %collective-permute-start.7 = (bf16[14,48,256]{2,0,1:T(8,128)(2,1)S(1)}, bf16[14,48,256]{2,0,1:T(8,128)(2,1)S(1)}, u32[]{:S(2)}, u32[]{:S(2)}) collective-permute-start(bf16[14,48,256]{2,0,1:T(8,128)(2,1)S(1)} %pad_maximum_fusion), channel_id=1, source_target_pairs={{0,24},{8,0},{16,8},{24,16},{1,25},{9,1},{17,9},{25,17},{2,26},{10... | collective-permute-start | bytes 1032200 | tf_op jit(solution)/shard_map/ppermute | solution.py:11
  104.8 12.5 %collective-permute-start.9 = (bf16[14,48,256]{2,0,1:T(8,128)(2,1)S(1)}, bf16[14,48,256]{2,0,1:T(8,128)(2,1)S(1)}, u32[]{:S(2)}, u32[]{:S(2)}) collective-permute-start(bf16[14,48,256]{2,0,1:T(8,128)(2,1)S(1)} %pad_maximum_fusion.1), channel_id=1, source_target_pairs={{0,8},{8,16},{16,24},{24,0},{1,9},{9,17},{17,25},{25,1},{2,10},{10... | collective-permute-start | bytes 1032200 | tf_op jit(solution)/shard_map/ppermute | solution.py:11
  111.6 10.9 %collective-permute-start.8 = (bf16[14,48,128]{2,0,1:T(8,128)(2,1)S(1)}, bf16[14,48,128]{2,0,1:T(8,128)(2,1)S(1)}, u32[]{:S(2)}, u32[]{:S(2)}) collective-permute-start(bf16[14,48,128]{2,0,1:T(8,128)(2,1)S(1)} %add_convert_fusion.2), channel_id=1, source_target_pairs={{0,24},{8,0},{16,8},{24,16},{1,25},{9,1},{17,9},{25,17},{2,26},{10... | collective-permute-start | bytes 516104 | tf_op jit(solution)/shard_map/ppermute | solution.py:11
  117.4 10.9 %collective-permute-start.10 = (bf16[14,48,128]{2,0,1:T(8,128)(2,1)S(1)}, bf16[14,48,128]{2,0,1:T(8,128)(2,1)S(1)}, u32[]{:S(2)}, u32[]{:S(2)}) collective-permute-start(bf16[14,48,128]{2,0,1:T(8,128)(2,1)S(1)} %add_convert_fusion.1), channel_id=1, source_target_pairs={{0,8},{8,16},{16,24},{24,0},{1,9},{9,17},{17,25},{25,1},{2,10},{10... | collective-permute-start | bytes 516104 | tf_op jit(solution)/shard_map/ppermute | solution.py:11
  128.6 9.7 %collective-permute-start.11 = (bf16[14,48,256]{2,0,1:T(8,128)(2,1)S(1)}, bf16[14,48,256]{2,0,1:T(8,128)(2,1)S(1)}, u32[]{:S(2)}, u32[]{:S(2)}) collective-permute-start(bf16[14,48,256]{2,0,1:T(8,128)(2,1)S(1)} %pad_maximum_fusion.2), channel_id=1, source_target_pairs={{0,24},{8,0},{16,8},{24,16},{1,25},{9,1},{17,9},{25,17},{2,26},{10... | collective-permute-start | bytes 1032200 | tf_op jit(solution)/shard_map/ppermute | solution.py:11
  130.5 10.9 %collective-permute-start.12 = (bf16[14,48,256]{2,0,1:T(8,128)(2,1)S(1)}, bf16[14,48,256]{2,0,1:T(8,128)(2,1)S(1)}, u32[]{:S(2)}, u32[]{:S(2)}) collective-permute-start(bf16[14,48,256]{2,0,1:T(8,128)(2,1)S(1)} %pad_maximum_fusion.2), channel_id=1, source_target_pairs={{0,8},{8,16},{16,24},{24,0},{1,9},{9,17},{17,25},{25,1},{2,10},{10... | collective-permute-start | bytes 1032200 | tf_op jit(solution)/shard_map/ppermute | solution.py:11
  138.3 8.5 %collective-permute-start.14 = (bf16[14,48,128]{2,0,1:T(8,128)(2,1)S(1)}, bf16[14,48,128]{2,0,1:T(8,128)(2,1)S(1)}, u32[]{:S(2)}, u32[]{:S(2)}) collective-permute-start(bf16[14,48,128]{2,0,1:T(8,128)(2,1)S(1)} %slice.145), channel_id=1, source_target_pairs={{0,24},{8,0},{16,8},{24,16},{1,25},{9,1},{17,9},{25,17},{2,26},{10... | collective-permute-start | bytes 516104 | tf_op jit(solution)/shard_map/ppermute | solution.py:11
  141.5 8.8 %collective-permute-start.13 = (bf16[14,48,128]{2,0,1:T(8,128)(2,1)S(1)}, bf16[14,48,128]{2,0,1:T(8,128)(2,1)S(1)}, u32[]{:S(2)}, u32[]{:S(2)}) collective-permute-start(bf16[14,48,128]{2,0,1:T(8,128)(2,1)S(1)} %slice.144), channel_id=1, source_target_pairs={{0,8},{8,16},{16,24},{24,0},{1,9},{9,17},{17,25},{25,1},{2,10},{10... | collective-permute-start | bytes 516104 | tf_op jit(solution)/shard_map/ppermute | solution.py:11
  173.2 3.5 %collective-permute-start.15 = (bf16[8,24,128]{2,0,1:T(8,128)(2,1)S(1)}, bf16[8,24,128]{2,0,1:T(8,128)(2,1)S(1)}, u32[]{:S(2)}, u32[]{:S(2)}) collective-permute-start(bf16[8,24,128]{2,0,1:T(8,128)(2,1)S(1)} %get-tuple-element.17), channel_id=1, source_target_pairs={{0,1},{1,2},{2,3},{3,4},{4,5},{5,6},{6,7},{7,0},{8,9},{9,10},{10,1... | collective-permute-start | bytes 147464 | tf_op jit(solution)/shard_map/ppermute | solution.py:11
  176.7 3.5 %collective-permute-start.16 = (bf16[8,24,128]{2,0,1:T(8,128)(2,1)S(1)}, bf16[8,24,128]{2,0,1:T(8,128)(2,1)S(1)}, u32[]{:S(2)}, u32[]{:S(2)}) collective-permute-start(bf16[8,24,128]{2,0,1:T(8,128)(2,1)S(1)} %fusion.38), channel_id=1, source_target_pairs={{0,1},{1,2},{2,3},{3,4},{4,5},{5,6},{6,7},{7,0},{8,9},{9,10},{10,1... | collective-permute-start | bytes 147464 | tf_op jit(solution)/shard_map/ppermute | solution.py:11
  176.8 3.5 %collective-permute-start.19 = (bf16[8,24,128]{2,0,1:T(8,128)(2,1)S(1)}, bf16[8,24,128]{2,0,1:T(8,128)(2,1)S(1)}, u32[]{:S(2)}, u32[]{:S(2)}) collective-permute-start(bf16[8,24,128]{2,0,1:T(8,128)(2,1)S(1)} %get-tuple-element.18), channel_id=1, source_target_pairs={{0,7},{1,0},{2,1},{3,2},{4,3},{5,4},{6,5},{7,6},{8,15},{9,8},{10,9... | collective-permute-start | bytes 147464 | tf_op jit(solution)/shard_map/ppermute | solution.py:11
  180.3 3.5 %collective-permute-start.17 = (bf16[8,24,128]{2,0,1:T(8,128)(2,1)S(1)}, bf16[8,24,128]{2,0,1:T(8,128)(2,1)S(1)}, u32[]{:S(2)}, u32[]{:S(2)}) collective-permute-start(bf16[8,24,128]{2,0,1:T(8,128)(2,1)S(1)} %fusion.37), channel_id=1, source_target_pairs={{0,1},{1,2},{2,3},{3,4},{4,5},{5,6},{6,7},{7,0},{8,9},{9,10},{10,1... | collective-permute-start | bytes 147464 | tf_op jit(solution)/shard_map/ppermute | solution.py:11
  183.8 1.8 collective-permute-start.20
  183.9 3.5 %collective-permute-start.18 = (bf16[8,24,128]{2,0,1:T(8,128)(2,1)S(1)}, bf16[8,24,128]{2,0,1:T(8,128)(2,1)S(1)}, u32[]{:S(2)}, u32[]{:S(2)}) collective-permute-start(bf16[8,24,128]{2,0,1:T(8,128)(2,1)S(1)} %get-tuple-element.15), channel_id=1, source_target_pairs={{0,1},{1,2},{2,3},{3,4},{4,5},{5,6},{6,7},{7,0},{8,9},{9,10},{10,1... | collective-permute-start | bytes 147464 | tf_op jit(solution)/shard_map/ppermute | solution.py:11
  185.6 3.5 %collective-permute-start.21 = (bf16[8,24,128]{2,0,1:T(8,128)(2,1)S(1)}, bf16[8,24,128]{2,0,1:T(8,128)(2,1)S(1)}, u32[]{:S(2)}, u32[]{:S(2)}) collective-permute-start(bf16[8,24,128]{2,0,1:T(8,128)(2,1)S(1)} %fusion.32), channel_id=1, source_target_pairs={{0,7},{1,0},{2,1},{3,2},{4,3},{5,4},{6,5},{7,6},{8,15},{9,8},{10,9... | collective-permute-start | bytes 147464 | tf_op jit(solution)/shard_map/ppermute | solution.py:11
  (5 other events, 40.4 us)
Sparse Core Ops, SparseCore 0:
  10.6 79.8 all-gather.1
  159.1 70.4 reduce-scatter.1

commit v9 on v7

--- a/solution.py
+++ b/solution.py
@@ -139,15 +139,18 @@
         grad_rel = jnp.stack(ring4_gather(grad_local, "row", bs), axis=1)
     else:
         grad_rel = jnp.stack(ring_gather(grad_local, "row", n_row), axis=1)
-    grad_abs = jnp.roll(grad_rel, k_row, axis=1).reshape(tile_cols, tok, 2 * bs)
+    grad_rel = grad_rel.reshape(tile_cols, tok, 2 * bs)
+    x_pick_rel = jnp.roll(x_pick.reshape(cap, n_row, rows_per, bs), -k_row, axis=1)
+    x_pick_rel = x_pick_rel.reshape(cap, tok, bs)
 
-    g_pick = jnp.einsum("qc,ctn->qtn", col_pick, grad_abs, preferred_element_type=F32).astype(BF16)
-    slot_dw = jnp.einsum("qtk,qtn->qkn", x_pick, g_pick, preferred_element_type=F32).astype(BF16)
+    g_pick = jnp.einsum("qc,ctn->qtn", col_pick, grad_rel, preferred_element_type=F32).astype(BF16)
+    slot_dw = jnp.einsum("qtk,qtn->qkn", x_pick_rel, g_pick, preferred_element_type=F32).astype(BF16)
 
     dx_slot = jnp.einsum("qtn,qkn->qtk", g_pick, pair_all, preferred_element_type=F32)
     dx = jnp.einsum(
         "qr,qtk->rtk", row_pick.astype(F32), dx_slot, precision=highest, preferred_element_type=F32
     ).astype(BF16)
+    dx = jnp.roll(dx.reshape(tile_rows, n_row, rows_per, bs), k_row, axis=1)
     dx_roll = jnp.roll(dx.reshape(tile_rows, n_col, cols_per, bs), -k_col, axis=1)
     dx_sum = ring_sum_scatter([dx_roll[:, m] for m in range(n_col)], "col", n_col)
     input_grad = dx_sum.transpose(1, 0, 2).reshape(cols_per, feat).astype(BF16)

time: 237 us -> 236 us (level)
  the two profiles are of different devices: /device:TPU:10 before, /device:TPU:8 now
where the time goes in v9:
time: 236 us; the launch traced here: 235 us
  waiting for transfers between devices  143 us (61%)
  starting transfers between devices  41.5 us (18%)
  matrix products  21 us (9%)
  between operations  14.6 us (6%)
  local copies, waits for them, and re-layouts  7.9 us (3%)
  other arithmetic  6.72 us (3%)
    all_gather x1, waiting for transfers between devices, on_device(): lax.all_gather(pair_local, 'dp', axis=0, tiled=True)  58.4 us
    reduce_scatter x1, waiting for transfers between devices, on_device(): lax.psum_scatter(slot_dw.reshape(cap * bs, 2 * bs), 'dp', scatter_dimensi...  42.9 us
    ppermute x22, waiting for transfers between devices, _shift(): return lax.ppermute(x, axis, perm=[(i, (i + step) % n) for i in range(n)])  41.9 us
    ppermute x22, starting transfers between devices, _shift(): return lax.ppermute(x, axis, perm=[(i, (i + step) % n) for i in range(n)])  41.5 us
  transfers between devices with their start and end apart: 24, of which 16 were waited for; matrix products, arithmetic and copies ran while one was open for 7% of the time, Pallas kernels for 0%

profile of v9, /device:TPU:8, one launch (start us, length us, event | category | flops | bytes accessed | tf_op | source)
XLA Modules:
  0.0 234.9 jit_solution(235537017957814232)
XLA Ops:
  13.2 3.0 %collective-permute-start.1 = (bf16[24,1024]{1,0:T(8,128)(2,1)S(1)}, bf16[24,1024]{1,0:T(8,128)(2,1)S(1)}, u32[]{:S(2)}, u32[]{:S(2)}) collective-permute-start(bf16[24,1024]{1,0:T(8,128)(2,1)S(1)} %collective-permute-done), channel_id=1, source_target_pairs={{0,7},{1,0},{2,1},{3,2},{4,3},{5,4},{6,5},{7,6},{8,15},{9,8},{10,9... | collective-permute-start | bytes 147464 | tf_op jit(solution)/shard_map/ppermute | solution.py:11
  17.9 3.0 %collective-permute-start.2 = (bf16[24,1024]{1,0:T(8,128)(2,1)S(1)}, bf16[24,1024]{1,0:T(8,128)(2,1)S(1)}, u32[]{:S(2)}, u32[]{:S(2)}) collective-permute-start(bf16[24,1024]{1,0:T(8,128)(2,1)S(1)} %collective-permute-done.1), channel_id=1, source_target_pairs={{0,7},{1,0},{2,1},{3,2},{4,3},{5,4},{6,5},{7,6},{8,15},{9,8},{10,9... | collective-permute-start | bytes 147464 | tf_op jit(solution)/shard_map/ppermute | solution.py:11
  20.9 4.7 %collective-permute-done.5 = bf16[24,1024]{1,0:T(8,128)(2,1)S(1)} collective-permute-done((bf16[24,1024]{1,0:T(8,128)(2,1)S(1)}, bf16[24,1024]{1,0:T(8,128)(2,1)S(1)}, u32[]{:S(2)}, u32[]{:S(2)}) %collective-permute-start.5) | collective-permute-done | bytes 49184 | tf_op jit(solution)/shard_map/ppermute | solution.py:11
  25.6 4.7 %collective-permute-done.6 = bf16[24,1024]{1,0:T(8,128)(2,1)S(1)} collective-permute-done((bf16[24,1024]{1,0:T(8,128)(2,1)S(1)}, bf16[24,1024]{1,0:T(8,128)(2,1)S(1)}, u32[]{:S(2)}, u32[]{:S(2)}) %collective-permute-start.6) | collective-permute-done | bytes 49184 | tf_op jit(solution)/shard_map/ppermute | solution.py:11
  32.1 58.4 %all-gather.2.cloned.1.call-done = bf16[6144,256]{1,0:T(8,128)(2,1)} async-done(((bf16[384,256]{1,0:T(8,128)(2,1)}), bf16[6144,256]{1,0:T(8,128)(2,1)}) %all-gather.2.cloned.1.call-update) | async-done | bytes 3145744 | tf_op jit(solution)/shard_map/all_gather | solution.py:100
  90.5 4.5 %convolution_convert_fusion = bf16[128,256,14,8]{1,2,3,0:T(8,128)(2,1)S(1)} fusion(bf16[48,128,256,1]{2,1,0,3:T(8,128)(2,1)} %bitcast.134, s32[14,8]{0,1:T(8,128)S(1)} %bitcast.154, pred[14,8]{0,1:T(8,128)(4,1)S(1)} %bitcast.155), kind=kOutput, calls=%fused_computation.2 | convolution fusion | flops 356002304 | bytes 10486320 | tf_op jit(solution)/shard_map/qcr,qkn->ckrn/dot_general | solution.py:118
  95.0 2.9 %fusion.14 = bf16[14,192,256]{2,1,0:T(8,128)(2,1)S(1)} fusion(bf16[14,1024,256]{2,0,1:T(8,128)(2,1)S(1)} %bitcast.138, bf16[192,1024]{1,0:T(8,128)(2,1)S(1)} %copy.27), kind=kOutput, calls=%fused_computation.19 | convolution fusion | flops 1409974272 | bytes 9109504 | tf_op jit(solution)/shard_map/dot_general | solution.py:123
  99.7 3.4 %collective-permute-start.9 = (bf16[14,48,256]{2,0,1:T(8,128)(2,1)S(1)}, bf16[14,48,256]{2,0,1:T(8,128)(2,1)S(1)}, u32[]{:S(2)}, u32[]{:S(2)}) collective-permute-start(bf16[14,48,256]{2,0,1:T(8,128)(2,1)S(1)} %pad_maximum_fusion.2), channel_id=1, source_target_pairs={{0,8},{8,16},{16,24},{24,0},{1,9},{9,17},{17,25},{25,1},{2,10},{10... | collective-permute-start | bytes 1032200 | tf_op jit(solution)/shard_map/ppermute | solution.py:11
  105.6 4.4 %collective-permute-done.9 = bf16[14,48,256]{2,0,1:T(8,128)(2,1)S(1)} collective-permute-done((bf16[14,48,256]{2,0,1:T(8,128)(2,1)S(1)}, bf16[14,48,256]{2,0,1:T(8,128)(2,1)S(1)}, u32[]{:S(2)}, u32[]{:S(2)}) %collective-permute-start.9) | collective-permute-done | bytes 344096 | tf_op jit(solution)/shard_map/ppermute | solution.py:11
  110.1 3.3 %collective-permute-start.10 = (bf16[14,48,128]{2,0,1:T(8,128)(2,1)S(1)}, bf16[14,48,128]{2,0,1:T(8,128)(2,1)S(1)}, u32[]{:S(2)}, u32[]{:S(2)}) collective-permute-start(bf16[14,48,128]{2,0,1:T(8,128)(2,1)S(1)} %add_convert_fusion), channel_id=1, source_target_pairs={{0,8},{8,16},{16,24},{24,0},{1,9},{9,17},{17,25},{25,1},{2,10},{10... | collective-permute-start | bytes 516104 | tf_op jit(solution)/shard_map/ppermute | solution.py:11
  113.4 3.5 %collective-permute-start.8 = (bf16[14,48,128]{2,0,1:T(8,128)(2,1)S(1)}, bf16[14,48,128]{2,0,1:T(8,128)(2,1)S(1)}, u32[]{:S(2)}, u32[]{:S(2)}) collective-permute-start(bf16[14,48,128]{2,0,1:T(8,128)(2,1)S(1)} %add_convert_fusion.1), channel_id=1, source_target_pairs={{0,24},{8,0},{16,8},{24,16},{1,25},{9,1},{17,9},{25,17},{2,26},{10... | collective-permute-start | bytes 516104 | tf_op jit(solution)/shard_map/ppermute | solution.py:11
  117.1 3.6 %collective-permute-done.10 = bf16[14,48,128]{2,0,1:T(8,128)(2,1)S(1)} collective-permute-done((bf16[14,48,128]{2,0,1:T(8,128)(2,1)S(1)}, bf16[14,48,128]{2,0,1:T(8,128)(2,1)S(1)}, u32[]{:S(2)}, u32[]{:S(2)}) %collective-permute-start.10) | collective-permute-done | bytes 172064 | tf_op jit(solution)/shard_map/ppermute | solution.py:11
  122.8 4.5 %collective-permute-start.12 = (bf16[14,48,256]{2,0,1:T(8,128)(2,1)S(1)}, bf16[14,48,256]{2,0,1:T(8,128)(2,1)S(1)}, u32[]{:S(2)}, u32[]{:S(2)}) collective-permute-start(bf16[14,48,256]{2,0,1:T(8,128)(2,1)S(1)} %get-tuple-element.20), channel_id=1, source_target_pairs={{0,8},{8,16},{16,24},{24,0},{1,9},{9,17},{17,25},{25,1},{2,10},{10... | collective-permute-start | bytes 1032200 | tf_op jit(solution)/shard_map/ppermute | solution.py:11
  130.0 3.9 %collective-permute-done.12 = bf16[14,48,256]{2,0,1:T(8,128)(2,1)S(1)} collective-permute-done((bf16[14,48,256]{2,0,1:T(8,128)(2,1)S(1)}, bf16[14,48,256]{2,0,1:T(8,128)(2,1)S(1)}, u32[]{:S(2)}, u32[]{:S(2)}) %collective-permute-start.12) | collective-permute-done | bytes 344096 | tf_op jit(solution)/shard_map/ppermute | solution.py:11
  133.9 4.2 %collective-permute-start.13 = (bf16[14,48,128]{2,0,1:T(8,128)(2,1)S(1)}, bf16[14,48,128]{2,0,1:T(8,128)(2,1)S(1)}, u32[]{:S(2)}, u32[]{:S(2)}) collective-permute-start(bf16[14,48,128]{2,0,1:T(8,128)(2,1)S(1)} %slice.128), channel_id=1, source_target_pairs={{0,8},{8,16},{16,24},{24,0},{1,9},{9,17},{17,25},{25,1},{2,10},{10... | collective-permute-start | bytes 516104 | tf_op jit(solution)/shard_map/ppermute | solution.py:11
  138.5 2.8 %collective-permute-start.14 = (bf16[14,48,128]{2,0,1:T(8,128)(2,1)S(1)}, bf16[14,48,128]{2,0,1:T(8,128)(2,1)S(1)}, u32[]{:S(2)}, u32[]{:S(2)}) collective-permute-start(bf16[14,48,128]{2,0,1:T(8,128)(2,1)S(1)} %slice.129), channel_id=1, source_target_pairs={{0,24},{8,0},{16,8},{24,16},{1,25},{9,1},{17,9},{25,17},{2,26},{10... | collective-permute-start | bytes 516104 | tf_op jit(solution)/shard_map/ppermute | solution.py:11
  147.9 3.8 %fusion.11 = bf16[48,128,256]{2,1,0:T(8,128)(2,1)} fusion(bf16[48,192,128]{2,1,0:T(8,128)(2,1)S(1)} %bitcast.136, bf16[48,192,256]{2,0,1:T(8,128)(2,1)S(1)} %convolution_convert_fusion.1), kind=kOutput, calls=%fused_computation.17 | convolution fusion | flops 605552640 | bytes 10223616 | tf_op jit(solution)/shard_map/qtk,qtn->qkn/dot_general | solution.py:147
  153.7 4.1 %fusion.6 = f32[48,192,128]{2,1,0:T(8,128)S(1)} fusion(bf16[48,128,256]{2,1,0:T(8,128)(2,1)S(1)} %bitcast.135, bf16[48,192,256]{2,0,1:T(8,128)(2,1)} %copy-done), kind=kOutput, calls=%fused_computation.9 | convolution fusion | flops 603979776 | bytes 12582912 | tf_op jit(solution)/shard_map/qtn,qkn->qtk/dot_general | solution.py:149
  157.8 3.4 %fusion.20 = bf16[8,192,128]{2,0,1:T(8,128)(2,1)S(1)} fusion(f32[48,192,128]{2,1,0:T(8,128)S(1)} %fusion.6, bf16[48,8]{0,1:T(8,128)(2,1)S(1)} %get-tuple-element.3), kind=kOutput, calls=%fused_computation.22 | convolution fusion | flops 56819712 | bytes 5112576 | tf_op jit(solution)/shard_map/qr,qtk->rtk/dot_general | solution.py:150
  161.6 4.7 %collective-permute-done.15 = bf16[8,24,128]{2,0,1:T(8,128)(2,1)S(1)} collective-permute-done((bf16[8,24,128]{2,0,1:T(8,128)(2,1)S(1)}, bf16[8,24,128]{2,0,1:T(8,128)(2,1)S(1)}, u32[]{:S(2)}, u32[]{:S(2)}) %collective-permute-start.15) | collective-permute-done | bytes 49184 | tf_op jit(solution)/shard_map/ppermute | solution.py:11
  166.3 2.9 %collective-permute-start.19 = (bf16[8,24,128]{2,0,1:T(8,128)(2,1)S(1)}, bf16[8,24,128]{2,0,1:T(8,128)(2,1)S(1)}, u32[]{:S(2)}, u32[]{:S(2)}) collective-permute-start(bf16[8,24,128]{2,0,1:T(8,128)(2,1)S(1)} %get-tuple-element.18), channel_id=1, source_target_pairs={{0,7},{1,0},{2,1},{3,2},{4,3},{5,4},{6,5},{7,6},{8,15},{9,8},{10,9... | collective-permute-start | bytes 147464 | tf_op jit(solution)/shard_map/ppermute | solution.py:11
  171.1 4.7 %collective-permute-done.17 = bf16[8,24,128]{2,0,1:T(8,128)(2,1)S(1)} collective-permute-done((bf16[8,24,128]{2,0,1:T(8,128)(2,1)S(1)}, bf16[8,24,128]{2,0,1:T(8,128)(2,1)S(1)}, u32[]{:S(2)}, u32[]{:S(2)}) %collective-permute-start.17) | collective-permute-done | bytes 49184 | tf_op jit(solution)/shard_map/ppermute | solution.py:11
  177.6 3.4 %collective-permute-start.21 = (bf16[8,24,128]{2,0,1:T(8,128)(2,1)S(1)}, bf16[8,24,128]{2,0,1:T(8,128)(2,1)S(1)}, u32[]{:S(2)}, u32[]{:S(2)}) collective-permute-start(bf16[8,24,128]{2,0,1:T(8,128)(2,1)S(1)} %fusion.30), channel_id=1, source_target_pairs={{0,7},{1,0},{2,1},{3,2},{4,3},{5,4},{6,5},{7,6},{8,15},{9,8},{10,9... | collective-permute-start | bytes 147464 | tf_op jit(solution)/shard_map/ppermute | solution.py:11
  183.4 42.9 %reduce-scatter.2.cloned.1.call-done = bf16[384,256]{1,0:T(8,128)(2,1)} async-done(((bf16[6144,256]{1,0:T(8,128)(2,1)}), bf16[384,256]{1,0:T(8,128)(2,1)}) %reduce-scatter.2.cloned.1.call-update) | async-done | bytes 196624 | tf_op jit(solution)/shard_map/reduce_scatter | solution.py:158
  (98 shorter events, 35.7 us)
Async XLA Ops:
  7.2 83.3 %all-gather.2.cloned.1.call-start = ((), (), s32[]{:S(2)}) async-start(), calls=%async_computation.1 | async-start | bytes 3342336 | tf_op jit(solution)/shard_map/all_gather | solution.py:100
  8.9 217.5 %reduce-scatter.2.cloned.1.call-start = ((), (), s32[]{:S(2)}) async-start(), calls=%async_computation.2 | async-start | bytes 3342336 | tf_op jit(solution)/shard_map/reduce_scatter | solution.py:158
  8.9 4.3 %collective-permute-start = (bf16[24,1024]{1,0:T(8,128)(2,1)}, bf16[24,1024]{1,0:T(8,128)(2,1)S(1)}, u32[]{:S(2)}, u32[]{:S(2)}) collective-permute-start(bf16[24,1024]{1,0:T(8,128)(2,1)} %param.5), channel_id=1, source_target_pairs={{0,7},{1,0},{2,1},{3,2},{4,3},{5,4},{6,5},{7,6},{8,15},{9,8},{10,9... | collective-permute-start | bytes 147464 | tf_op jit(solution)/shard_map/ppermute | solution.py:11
  11.1 5.0 %collective-permute-start.3 = (bf16[24,1024]{1,0:T(8,128)(2,1)}, bf16[24,1024]{1,0:T(8,128)(2,1)S(1)}, u32[]{:S(2)}, u32[]{:S(2)}) collective-permute-start(bf16[24,1024]{1,0:T(8,128)(2,1)} %param.5), channel_id=1, source_target_pairs={{0,1},{1,2},{2,3},{3,4},{4,5},{5,6},{6,7},{7,0},{8,9},{9,10},{10,1... | collective-permute-start | bytes 147464 | tf_op jit(solution)/shard_map/ppermute | solution.py:11
  13.2 4.7 %collective-permute-start.1 = (bf16[24,1024]{1,0:T(8,128)(2,1)S(1)}, bf16[24,1024]{1,0:T(8,128)(2,1)S(1)}, u32[]{:S(2)}, u32[]{:S(2)}) collective-permute-start(bf16[24,1024]{1,0:T(8,128)(2,1)S(1)} %collective-permute-done), channel_id=1, source_target_pairs={{0,7},{1,0},{2,1},{3,2},{4,3},{5,4},{6,5},{7,6},{8,15},{9,8},{10,9... | collective-permute-start | bytes 147464 | tf_op jit(solution)/shard_map/ppermute | solution.py:11
  16.2 4.7 %collective-permute-start.4 = (bf16[24,1024]{1,0:T(8,128)(2,1)S(1)}, bf16[24,1024]{1,0:T(8,128)(2,1)S(1)}, u32[]{:S(2)}, u32[]{:S(2)}) collective-permute-start(bf16[24,1024]{1,0:T(8,128)(2,1)S(1)} %collective-permute-done.3), channel_id=1, source_target_pairs={{0,1},{1,2},{2,3},{3,4},{4,5},{5,6},{6,7},{7,0},{8,9},{9,10},{10,1... | collective-permute-start | bytes 147464 | tf_op jit(solution)/shard_map/ppermute | solution.py:11
  17.9 7.7 %collective-permute-start.2 = (bf16[24,1024]{1,0:T(8,128)(2,1)S(1)}, bf16[24,1024]{1,0:T(8,128)(2,1)S(1)}, u32[]{:S(2)}, u32[]{:S(2)}) collective-permute-start(bf16[24,1024]{1,0:T(8,128)(2,1)S(1)} %collective-permute-done.1), channel_id=1, source_target_pairs={{0,7},{1,0},{2,1},{3,2},{4,3},{5,4},{6,5},{7,6},{8,15},{9,8},{10,9... | collective-permute-start | bytes 147464 | tf_op jit(solution)/shard_map/ppermute | solution.py:11
  20.9 4.7 %collective-permute-start.5 = (bf16[24,1024]{1,0:T(8,128)(2,1)S(1)}, bf16[24,1024]{1,0:T(8,128)(2,1)S(1)}, u32[]{:S(2)}, u32[]{:S(2)}) collective-permute-start(bf16[24,1024]{1,0:T(8,128)(2,1)S(1)} %collective-permute-done.4), channel_id=1, source_target_pairs={{0,1},{1,2},{2,3},{3,4},{4,5},{5,6},{6,7},{7,0},{8,9},{9,10},{10,1... | collective-permute-start | bytes 147464 | tf_op jit(solution)/shard_map/ppermute | solution.py:11
  25.6 4.7 %collective-permute-start.6 = (bf16[24,1024]{1,0:T(8,128)(2,1)S(1)}, bf16[24,1024]{1,0:T(8,128)(2,1)S(1)}, u32[]{:S(2)}, u32[]{:S(2)}) collective-permute-start(bf16[24,1024]{1,0:T(8,128)(2,1)S(1)} %collective-permute-done.5), channel_id=1, source_target_pairs={{0,1},{1,2},{2,3},{3,4},{4,5},{5,6},{6,7},{7,0},{8,9},{9,10},{10,1... | collective-permute-start | bytes 147464 | tf_op jit(solution)/shard_map/ppermute | solution.py:11
  99.7 10.4 %collective-permute-start.9 = (bf16[14,48,256]{2,0,1:T(8,128)(2,1)S(1)}, bf16[14,48,256]{2,0,1:T(8,128)(2,1)S(1)}, u32[]{:S(2)}, u32[]{:S(2)}) collective-permute-start(bf16[14,48,256]{2,0,1:T(8,128)(2,1)S(1)} %pad_maximum_fusion.2), channel_id=1, source_target_pairs={{0,8},{8,16},{16,24},{24,0},{1,9},{9,17},{17,25},{25,1},{2,10},{10... | collective-permute-start | bytes 1032200 | tf_op jit(solution)/shard_map/ppermute | solution.py:11
  103.2 10.2 %collective-permute-start.7 = (bf16[14,48,256]{2,0,1:T(8,128)(2,1)S(1)}, bf16[14,48,256]{2,0,1:T(8,128)(2,1)S(1)}, u32[]{:S(2)}, u32[]{:S(2)}) collective-permute-start(bf16[14,48,256]{2,0,1:T(8,128)(2,1)S(1)} %pad_maximum_fusion.1), channel_id=1, source_target_pairs={{0,24},{8,0},{16,8},{24,16},{1,25},{9,1},{17,9},{25,17},{2,26},{10... | collective-permute-start | bytes 1032200 | tf_op jit(solution)/shard_map/ppermute | solution.py:11
  110.1 10.6 %collective-permute-start.10 = (bf16[14,48,128]{2,0,1:T(8,128)(2,1)S(1)}, bf16[14,48,128]{2,0,1:T(8,128)(2,1)S(1)}, u32[]{:S(2)}, u32[]{:S(2)}) collective-permute-start(bf16[14,48,128]{2,0,1:T(8,128)(2,1)S(1)} %add_convert_fusion), channel_id=1, source_target_pairs={{0,8},{8,16},{16,24},{24,0},{1,9},{9,17},{17,25},{25,1},{2,10},{10... | collective-permute-start | bytes 516104 | tf_op jit(solution)/shard_map/ppermute | solution.py:11
  113.4 9.0 %collective-permute-start.8 = (bf16[14,48,128]{2,0,1:T(8,128)(2,1)S(1)}, bf16[14,48,128]{2,0,1:T(8,128)(2,1)S(1)}, u32[]{:S(2)}, u32[]{:S(2)}) collective-permute-start(bf16[14,48,128]{2,0,1:T(8,128)(2,1)S(1)} %add_convert_fusion.1), channel_id=1, source_target_pairs={{0,24},{8,0},{16,8},{24,16},{1,25},{9,1},{17,9},{25,17},{2,26},{10... | collective-permute-start | bytes 516104 | tf_op jit(solution)/shard_map/ppermute | solution.py:11
  122.8 11.0 %collective-permute-start.12 = (bf16[14,48,256]{2,0,1:T(8,128)(2,1)S(1)}, bf16[14,48,256]{2,0,1:T(8,128)(2,1)S(1)}, u32[]{:S(2)}, u32[]{:S(2)}) collective-permute-start(bf16[14,48,256]{2,0,1:T(8,128)(2,1)S(1)} %get-tuple-element.20), channel_id=1, source_target_pairs={{0,8},{8,16},{16,24},{24,0},{1,9},{9,17},{17,25},{25,1},{2,10},{10... | collective-permute-start | bytes 1032200 | tf_op jit(solution)/shard_map/ppermute | solution.py:11
  127.4 11.1 %collective-permute-start.11 = (bf16[14,48,256]{2,0,1:T(8,128)(2,1)S(1)}, bf16[14,48,256]{2,0,1:T(8,128)(2,1)S(1)}, u32[]{:S(2)}, u32[]{:S(2)}) collective-permute-start(bf16[14,48,256]{2,0,1:T(8,128)(2,1)S(1)} %get-tuple-element.20), channel_id=1, source_target_pairs={{0,24},{8,0},{16,8},{24,16},{1,25},{9,1},{17,9},{25,17},{2,26},{10... | collective-permute-start | bytes 1032200 | tf_op jit(solution)/shard_map/ppermute | solution.py:11
  133.9 9.7 %collective-permute-start.13 = (bf16[14,48,128]{2,0,1:T(8,128)(2,1)S(1)}, bf16[14,48,128]{2,0,1:T(8,128)(2,1)S(1)}, u32[]{:S(2)}, u32[]{:S(2)}) collective-permute-start(bf16[14,48,128]{2,0,1:T(8,128)(2,1)S(1)} %slice.128), channel_id=1, source_target_pairs={{0,8},{8,16},{16,24},{24,0},{1,9},{9,17},{17,25},{25,1},{2,10},{10... | collective-permute-start | bytes 516104 | tf_op jit(solution)/shard_map/ppermute | solution.py:11
  138.5 7.6 %collective-permute-start.14 = (bf16[14,48,128]{2,0,1:T(8,128)(2,1)S(1)}, bf16[14,48,128]{2,0,1:T(8,128)(2,1)S(1)}, u32[]{:S(2)}, u32[]{:S(2)}) collective-permute-start(bf16[14,48,128]{2,0,1:T(8,128)(2,1)S(1)} %slice.129), channel_id=1, source_target_pairs={{0,24},{8,0},{16,8},{24,16},{1,25},{9,1},{17,9},{25,17},{2,26},{10... | collective-permute-start | bytes 516104 | tf_op jit(solution)/shard_map/ppermute | solution.py:11
  161.5 4.7 %collective-permute-start.15 = (bf16[8,24,128]{2,0,1:T(8,128)(2,1)S(1)}, bf16[8,24,128]{2,0,1:T(8,128)(2,1)S(1)}, u32[]{:S(2)}, u32[]{:S(2)}) collective-permute-start(bf16[8,24,128]{2,0,1:T(8,128)(2,1)S(1)} %get-tuple-element.17), channel_id=1, source_target_pairs={{0,1},{1,2},{2,3},{3,4},{4,5},{5,6},{6,7},{7,0},{8,9},{9,10},{10,1... | collective-permute-start | bytes 147464 | tf_op jit(solution)/shard_map/ppermute | solution.py:11
  166.3 4.7 %collective-permute-start.16 = (bf16[8,24,128]{2,0,1:T(8,128)(2,1)S(1)}, bf16[8,24,128]{2,0,1:T(8,128)(2,1)S(1)}, u32[]{:S(2)}, u32[]{:S(2)}) collective-permute-start(bf16[8,24,128]{2,0,1:T(8,128)(2,1)S(1)} %fusion.36), channel_id=1, source_target_pairs={{0,1},{1,2},{2,3},{3,4},{4,5},{5,6},{6,7},{7,0},{8,9},{9,10},{10,1... | collective-permute-start | bytes 147464 | tf_op jit(solution)/shard_map/ppermute | solution.py:11
  166.3 4.8 %collective-permute-start.19 = (bf16[8,24,128]{2,0,1:T(8,128)(2,1)S(1)}, bf16[8,24,128]{2,0,1:T(8,128)(2,1)S(1)}, u32[]{:S(2)}, u32[]{:S(2)}) collective-permute-start(bf16[8,24,128]{2,0,1:T(8,128)(2,1)S(1)} %get-tuple-element.18), channel_id=1, source_target_pairs={{0,7},{1,0},{2,1},{3,2},{4,3},{5,4},{6,5},{7,6},{8,15},{9,8},{10,9... | collective-permute-start | bytes 147464 | tf_op jit(solution)/shard_map/ppermute | solution.py:11
  171.1 4.7 %collective-permute-start.17 = (bf16[8,24,128]{2,0,1:T(8,128)(2,1)S(1)}, bf16[8,24,128]{2,0,1:T(8,128)(2,1)S(1)}, u32[]{:S(2)}, u32[]{:S(2)}) collective-permute-start(bf16[8,24,128]{2,0,1:T(8,128)(2,1)S(1)} %fusion.35), channel_id=1, source_target_pairs={{0,1},{1,2},{2,3},{3,4},{4,5},{5,6},{6,7},{7,0},{8,9},{9,10},{10,1... | collective-permute-start | bytes 147464 | tf_op jit(solution)/shard_map/ppermute | solution.py:11
  175.8 1.8 collective-permute-start.20
  175.9 5.2 %collective-permute-start.18 = (bf16[8,24,128]{2,0,1:T(8,128)(2,1)S(1)}, bf16[8,24,128]{2,0,1:T(8,128)(2,1)S(1)}, u32[]{:S(2)}, u32[]{:S(2)}) collective-permute-start(bf16[8,24,128]{2,0,1:T(8,128)(2,1)S(1)} %get-tuple-element.15), channel_id=1, source_target_pairs={{0,1},{1,2},{2,3},{3,4},{4,5},{5,6},{6,7},{7,0},{8,9},{9,10},{10,1... | collective-permute-start | bytes 147464 | tf_op jit(solution)/shard_map/ppermute | solution.py:11
  177.6 5.1 %collective-permute-start.21 = (bf16[8,24,128]{2,0,1:T(8,128)(2,1)S(1)}, bf16[8,24,128]{2,0,1:T(8,128)(2,1)S(1)}, u32[]{:S(2)}, u32[]{:S(2)}) collective-permute-start(bf16[8,24,128]{2,0,1:T(8,128)(2,1)S(1)} %fusion.30), channel_id=1, source_target_pairs={{0,7},{1,0},{2,1},{3,2},{4,3},{5,4},{6,5},{7,6},{8,15},{9,8},{10,9... | collective-permute-start | bytes 147464 | tf_op jit(solution)/shard_map/ppermute | solution.py:11
  (3 other events, 23.3 us)
Sparse Core Ops, SparseCore 0:
  10.6 79.7 all-gather.1
  151.9 74.3 reduce-scatter.1
